TPU v7x, 1024 devices: a whole 4x4x32 slice. The times are simulated.
1024 devices in a mesh: row: 32 (over x, y, z_hi), col: 32 (over z_lo, core).
Axes of the slice: x: 4, y: 4, z: 32 (z_hi: 2, z_lo: 16; z = z_hi * 16 + z_lo), core: 2. Of those that a mesh axis runs over, the one named last changes fastest.
Arguments:
- density: float32 [1024, 7, 128, 128], P(('row', 'col')), as said below
- pattern: int32 [1024, 12], P(('row', 'col')), may hold values from 0 to 1023, as said below
Outputs:
- purified: float32 [1024, 7, 128, 128], P(('row', 'col'))
Inputs may be any that keep to these rules, and one draw needn't show every extreme that they name: `pattern`: row I lists the block columns (I + o) mod 1024 for o = -6..6 in rising order of o, all but one o; the omitted o is nonzero and of magnitude 3 or less, and row (I + o) mod 1024 omits -o. density[I, 0] is symmetric, and density[I, t] is zero where (I + t) mod 1024 is not listed in row I of pattern.
All inputs are finite; a program needn't handle non-finite values.
Results may differ from a plain program's by a relative error of at most 0.0001.
Values sent between devices are 32-bit elements; how exact they have to be, the bound alone decides.
No kernel may reach another device: no remote copies, remote signals or barrier semaphores. Data moves between devices by JAX's collectives and lax.ppermute only.
A program may use at most 32 MiB of HBM per device.

v0:
```python
import jax
import jax.numpy as jnp
from jax import lax
from jax.sharding import PartitionSpec as P

REACH = 6


def from_behind(block, axis, distance):
    devices = range(lax.axis_size(axis))
    route = [((i - distance) % len(devices), i) for i in devices]
    return lax.ppermute(block, axis, route)


def fetch_rows(local_band):
    rows_above = []
    rows_below = []
    for distance in range(1, REACH + 1):
        rows_above.append(from_behind(local_band[distance:], ("row", "col"), distance))
        rows_below.append(
            from_behind(local_band[: REACH + 1 - distance], ("row", "col"), -distance)
        )
    return (rows_above, rows_below)


def make_upper(local_band, rows_above, rows_below):

    def upper_block(offset, width):
        if offset == 0:
            return local_band[width]
        if offset < 0:
            return rows_above[-offset - 1][width + offset]
        return rows_below[offset - 1][width]

    return upper_block


def left_operand(upper_block, inner):
    if inner >= 0:
        return (upper_block(0, inner), 1)
    return (upper_block(inner, -inner), 0)


def right_operand(upper_block, inner, target):
    if target >= inner:
        return (upper_block(inner, target - inner), 0)
    return (upper_block(target, inner - target), 1)


def band_product(upper_left, upper_right):
    results = []
    for target in range(REACH + 1):
        total = None
        for inner in range(target - REACH, REACH + 1):
            left_block, left_dim = left_operand(upper_left, inner)
            right_block, right_dim = right_operand(upper_right, inner, target)
            term = lax.dot_general(
                left_block,
                right_block,
                (((left_dim,), (right_dim,)), ((), ())),
                precision=lax.Precision.HIGHEST,
                preferred_element_type=jnp.float32,
            )
            total = term if total is None else total + term
        results.append(total)
    return jnp.stack(results, axis=0)


def on_device(density, pattern):
    local_band = density[0]
    total_rows = lax.axis_size("row") * lax.axis_size("col")
    position = lax.axis_index("row") * lax.axis_size("col") + lax.axis_index("col")
    columns = (position + jnp.arange(REACH + 1, dtype=jnp.int32)) % total_rows
    flags = jnp.any(pattern[0][None, :] == columns[:, None], axis=1).astype(jnp.float32)[
        :, None, None
    ]
    above_p, below_p = fetch_rows(local_band)
    upper_p = make_upper(local_band, above_p, below_p)
    square = flags * band_product(upper_p, upper_p)
    above_s, below_s = fetch_rows(square)
    upper_s = make_upper(square, above_s, below_s)
    cube = flags * band_product(upper_p, upper_s)
    return (3.0 * square - 2.0 * cube)[None]


def solution(mesh):
    return jax.shard_map(
        on_device,
        mesh=mesh,
        in_specs=(P(("row", "col"), None, None, None), P(("row", "col"), None)),
        out_specs=P(("row", "col"), None, None, None),
        check_vma=False,
    )
```

profile of v0, /device:TPU:1, one launch (start us, length us, event | category | flops | bytes accessed | tf_op | source)
XLA Modules:
  0.0 261.8 jit_solution(9371953522649447362)
XLA Ops:
  1.2 4.9 %collective-permute-start.5 = (f32[6,128,128]{2,1,0:T(8,128)S(1)}, f32[6,128,128]{2,1,0:T(8,128)S(1)}, u32[]{:S(2)}, u32[]{:S(2)}) collective-permute-start(f32[6,128,128]{2,1,0:T(8,128)S(1)} %get-tuple-element.28), channel_id=1, source_target_pairs={{1023,0},{0,1},{1,2},{2,3},{3,4},{4,5},{5,6},{6,7},{7,8},{8,9},{9,... | collective-permute-start | bytes 1179656 | tf_op jit(solution)/shard_map/ppermute | solution.py:12
  6.2 3.5 %collective-permute-start.4 = (f32[5,128,128]{2,1,0:T(8,128)S(1)}, f32[5,128,128]{2,1,0:T(8,128)S(1)}, u32[]{:S(2)}, u32[]{:S(2)}) collective-permute-start(f32[5,128,128]{2,1,0:T(8,128)S(1)} %get-tuple-element.26), channel_id=1, source_target_pairs={{1022,0},{1023,1},{0,2},{1,3},{2,4},{3,5},{4,6},{5,7},{6,8},{7,9},... | collective-permute-start | bytes 983048 | tf_op jit(solution)/shard_map/ppermute | solution.py:12
  10.6 3.5 %collective-permute-start.3 = (f32[4,128,128]{2,1,0:T(8,128)}, f32[4,128,128]{2,1,0:T(8,128)S(1)}, u32[]{:S(2)}, u32[]{:S(2)}) collective-permute-start(f32[4,128,128]{2,1,0:T(8,128)} %get-tuple-element.24), channel_id=1, source_target_pairs={{1021,0},{1022,1},{1023,2},{0,3},{1,4},{2,5},{3,6},{4,7},{5,8},{6,... | collective-permute-start | bytes 786440 | tf_op jit(solution)/shard_map/ppermute | solution.py:12
  14.9 6.1 %collective-permute-start.2 = (f32[3,128,128]{2,1,0:T(8,128)}, f32[3,128,128]{2,1,0:T(8,128)S(1)}, u32[]{:S(2)}, u32[]{:S(2)}) collective-permute-start(f32[3,128,128]{2,1,0:T(8,128)} %get-tuple-element.22), channel_id=1, source_target_pairs={{1020,0},{1021,1},{1022,2},{1023,3},{0,4},{1,5},{2,6},{3,7},{4,8},... | collective-permute-start | bytes 589832 | tf_op jit(solution)/shard_map/ppermute | solution.py:12
  21.7 16.3 %collective-permute-start.11 = (f32[1,128,128]{2,1,0:T(8,128)}, f32[1,128,128]{2,1,0:T(8,128)}, u32[]{:S(2)}, u32[]{:S(2)}) collective-permute-start(f32[1,128,128]{2,1,0:T(8,128)} %get-tuple-element.17), channel_id=1, source_target_pairs={{6,0},{7,1},{8,2},{9,3},{10,4},{11,5},{12,6},{13,7},{14,8},{15,9},... | collective-permute-start | bytes 196616 | tf_op jit(solution)/shard_map/ppermute | solution.py:12
  41.8 9.6 %collective-permute-start.10 = (f32[2,128,128]{2,1,0:T(8,128)}, f32[2,128,128]{2,1,0:T(8,128)S(1)}, u32[]{:S(2)}, u32[]{:S(2)}) collective-permute-start(f32[2,128,128]{2,1,0:T(8,128)} %get-tuple-element.19), channel_id=1, source_target_pairs={{5,0},{6,1},{7,2},{8,3},{9,4},{10,5},{11,6},{12,7},{13,8},{14,9},{... | collective-permute-start | bytes 393224 | tf_op jit(solution)/shard_map/ppermute | solution.py:12
  52.5 5.2 %collective-permute-done.10 = f32[2,128,128]{2,1,0:T(8,128)S(1)} collective-permute-done((f32[2,128,128]{2,1,0:T(8,128)}, f32[2,128,128]{2,1,0:T(8,128)S(1)}, u32[]{:S(2)}, u32[]{:S(2)}) %collective-permute-start.10) | collective-permute-done | bytes 131104 | tf_op jit(solution)/shard_map/ppermute | solution.py:12
  60.3 13.4 %collective-permute-done.1 = f32[2,128,128]{2,1,0:T(8,128)S(1)} collective-permute-done((f32[2,128,128]{2,1,0:T(8,128)S(1)}, f32[2,128,128]{2,1,0:T(8,128)S(1)}, u32[]{:S(2)}, u32[]{:S(2)}) %collective-permute-start.1) | collective-permute-done | bytes 131104 | tf_op jit(solution)/shard_map/ppermute | solution.py:12
  76.6 7.8 %collective-permute-done.9 = f32[3,128,128]{2,1,0:T(8,128)S(1)} collective-permute-done((f32[3,128,128]{2,1,0:T(8,128)S(1)}, f32[3,128,128]{2,1,0:T(8,128)S(1)}, u32[]{:S(2)}, u32[]{:S(2)}) %collective-permute-start.9) | collective-permute-done | bytes 196640 | tf_op jit(solution)/shard_map/ppermute | solution.py:12
  87.3 4.2 %collective-permute-start.6 = (f32[6,128,128]{2,1,0:T(8,128)S(1)}, f32[6,128,128]{2,1,0:T(8,128)S(1)}, u32[]{:S(2)}, u32[]{:S(2)}) collective-permute-start(f32[6,128,128]{2,1,0:T(8,128)S(1)} %get-tuple-element.27), channel_id=1, source_target_pairs={{1,0},{2,1},{3,2},{4,3},{5,4},{6,5},{7,6},{8,7},{9,8},{10,9},{11,1... | collective-permute-start | bytes 1179656 | tf_op jit(solution)/shard_map/ppermute | solution.py:12
  92.3 7.9 %collective-permute-start.8 = (f32[4,128,128]{2,1,0:T(8,128)S(1)}, f32[4,128,128]{2,1,0:T(8,128)S(1)}, u32[]{:S(2)}, u32[]{:S(2)}) collective-permute-start(f32[4,128,128]{2,1,0:T(8,128)S(1)} %copy-done.1), channel_id=1, source_target_pairs={{3,0},{4,1},{5,2},{6,3},{7,4},{8,5},{9,6},{10,7},{11,8},{12,9},{13... | collective-permute-start | bytes 786440 | tf_op jit(solution)/shard_map/ppermute | solution.py:12
  100.9 7.9 %collective-permute-done.8 = f32[4,128,128]{2,1,0:T(8,128)S(1)} collective-permute-done((f32[4,128,128]{2,1,0:T(8,128)S(1)}, f32[4,128,128]{2,1,0:T(8,128)S(1)}, u32[]{:S(2)}, u32[]{:S(2)}) %collective-permute-start.8) | collective-permute-done | bytes 262176 | tf_op jit(solution)/shard_map/ppermute | solution.py:12
  108.8 8.2 %collective-permute-start.7 = (f32[5,128,128]{2,1,0:T(8,128)S(1)}, f32[5,128,128]{2,1,0:T(8,128)S(1)}, u32[]{:S(2)}, u32[]{:S(2)}) collective-permute-start(f32[5,128,128]{2,1,0:T(8,128)S(1)} %get-tuple-element.25), channel_id=1, source_target_pairs={{2,0},{3,1},{4,2},{5,3},{6,4},{7,5},{8,6},{9,7},{10,8},{11,9},{12,... | collective-permute-start | bytes 983048 | tf_op jit(solution)/shard_map/ppermute | solution.py:12
  133.9 4.9 %collective-permute-start.18 = (f32[6,128,128]{2,1,0:T(8,128)S(1)}, f32[6,128,128]{2,1,0:T(8,128)S(1)}, u32[]{:S(2)}, u32[]{:S(2)}) collective-permute-start(f32[6,128,128]{2,1,0:T(8,128)S(1)} %get-tuple-element.15), channel_id=1, source_target_pairs={{1,0},{2,1},{3,2},{4,3},{5,4},{6,5},{7,6},{8,7},{9,8},{10,9},{11,1... | collective-permute-start | bytes 1179656 | tf_op jit(solution)/shard_map/ppermute | solution.py:12
  144.5 16.1 %collective-permute-start.23 = (f32[1,128,128]{2,1,0:T(8,128)S(1)}, f32[1,128,128]{2,1,0:T(8,128)S(1)}, u32[]{:S(2)}, u32[]{:S(2)}) collective-permute-start(f32[1,128,128]{2,1,0:T(8,128)S(1)} %get-tuple-element.5), channel_id=1, source_target_pairs={{6,0},{7,1},{8,2},{9,3},{10,4},{11,5},{12,6},{13,7},{14,8},{15,9},... | collective-permute-start | bytes 196616 | tf_op jit(solution)/shard_map/ppermute | solution.py:12
  160.7 3.8 %collective-permute-done.23 = f32[1,128,128]{2,1,0:T(8,128)S(1)} collective-permute-done((f32[1,128,128]{2,1,0:T(8,128)S(1)}, f32[1,128,128]{2,1,0:T(8,128)S(1)}, u32[]{:S(2)}, u32[]{:S(2)}) %collective-permute-start.23) | collective-permute-done | bytes 65568 | tf_op jit(solution)/shard_map/ppermute | solution.py:12
  164.6 9.6 %collective-permute-start.22 = (f32[2,128,128]{2,1,0:T(8,128)S(1)}, f32[2,128,128]{2,1,0:T(8,128)S(1)}, u32[]{:S(2)}, u32[]{:S(2)}) collective-permute-start(f32[2,128,128]{2,1,0:T(8,128)S(1)} %get-tuple-element.7), channel_id=1, source_target_pairs={{5,0},{6,1},{7,2},{8,3},{9,4},{10,5},{11,6},{12,7},{13,8},{14,9},{... | collective-permute-start | bytes 393224 | tf_op jit(solution)/shard_map/ppermute | solution.py:12
  174.4 6.1 %collective-permute-done.22 = f32[2,128,128]{2,1,0:T(8,128)S(1)} collective-permute-done((f32[2,128,128]{2,1,0:T(8,128)S(1)}, f32[2,128,128]{2,1,0:T(8,128)S(1)}, u32[]{:S(2)}, u32[]{:S(2)}) %collective-permute-start.22) | collective-permute-done | bytes 131104 | tf_op jit(solution)/shard_map/ppermute | solution.py:12
  183.2 13.6 %collective-permute-done.13 = f32[2,128,128]{2,1,0:T(8,128)S(1)} collective-permute-done((f32[2,128,128]{2,1,0:T(8,128)S(1)}, f32[2,128,128]{2,1,0:T(8,128)S(1)}, u32[]{:S(2)}, u32[]{:S(2)}) %collective-permute-start.13) | collective-permute-done | bytes 131104 | tf_op jit(solution)/shard_map/ppermute | solution.py:12
  199.0 12.1 %collective-permute-done.14 = f32[3,128,128]{2,1,0:T(8,128)S(1)} collective-permute-done((f32[3,128,128]{2,1,0:T(8,128)S(1)}, f32[3,128,128]{2,1,0:T(8,128)S(1)}, u32[]{:S(2)}, u32[]{:S(2)}) %collective-permute-start.14) | collective-permute-done | bytes 196640 | tf_op jit(solution)/shard_map/ppermute | solution.py:12
  213.5 5.4 %collective-permute-done.21 = f32[3,128,128]{2,1,0:T(8,128)S(1)} collective-permute-done((f32[3,128,128]{2,1,0:T(8,128)S(1)}, f32[3,128,128]{2,1,0:T(8,128)S(1)}, u32[]{:S(2)}, u32[]{:S(2)}) %collective-permute-start.21) | collective-permute-done | bytes 196640 | tf_op jit(solution)/shard_map/ppermute | solution.py:12
  222.0 12.3 %collective-permute-start.20 = (f32[4,128,128]{2,1,0:T(8,128)S(1)}, f32[4,128,128]{2,1,0:T(8,128)S(1)}, u32[]{:S(2)}, u32[]{:S(2)}) collective-permute-start(f32[4,128,128]{2,1,0:T(8,128)S(1)} %get-tuple-element.11), channel_id=1, source_target_pairs={{3,0},{4,1},{5,2},{6,3},{7,4},{8,5},{9,6},{10,7},{11,8},{12,9},{13... | collective-permute-start | bytes 786440 | tf_op jit(solution)/shard_map/ppermute | solution.py:12
  235.2 4.2 %collective-permute-done.20 = f32[4,128,128]{2,1,0:T(8,128)S(1)} collective-permute-done((f32[4,128,128]{2,1,0:T(8,128)S(1)}, f32[4,128,128]{2,1,0:T(8,128)S(1)}, u32[]{:S(2)}, u32[]{:S(2)}) %collective-permute-start.20) | collective-permute-done | bytes 262176 | tf_op jit(solution)/shard_map/ppermute | solution.py:12
  239.4 7.6 %collective-permute-start.19 = (f32[5,128,128]{2,1,0:T(8,128)S(1)}, f32[5,128,128]{2,1,0:T(8,128)S(1)}, u32[]{:S(2)}, u32[]{:S(2)}) collective-permute-start(f32[5,128,128]{2,1,0:T(8,128)S(1)} %get-tuple-element.13), channel_id=1, source_target_pairs={{2,0},{3,1},{4,2},{5,3},{6,4},{7,5},{8,6},{9,7},{10,8},{11,9},{12,... | collective-permute-start | bytes 983048 | tf_op jit(solution)/shard_map/ppermute | solution.py:12
  (200 shorter events, 66.3 us)
Async XLA Ops:
  1.2 123.0 %collective-permute-start.5 = (f32[6,128,128]{2,1,0:T(8,128)S(1)}, f32[6,128,128]{2,1,0:T(8,128)S(1)}, u32[]{:S(2)}, u32[]{:S(2)}) collective-permute-start(f32[6,128,128]{2,1,0:T(8,128)S(1)} %get-tuple-element.28), channel_id=1, source_target_pairs={{1023,0},{0,1},{1,2},{2,3},{3,4},{4,5},{5,6},{6,7},{7,8},{8,9},{9,... | collective-permute-start | bytes 1179656 | tf_op jit(solution)/shard_map/ppermute | solution.py:12
  6.2 112.7 %collective-permute-start.4 = (f32[5,128,128]{2,1,0:T(8,128)S(1)}, f32[5,128,128]{2,1,0:T(8,128)S(1)}, u32[]{:S(2)}, u32[]{:S(2)}) collective-permute-start(f32[5,128,128]{2,1,0:T(8,128)S(1)} %get-tuple-element.26), channel_id=1, source_target_pairs={{1022,0},{1023,1},{0,2},{1,3},{2,4},{3,5},{4,6},{5,7},{6,8},{7,9},... | collective-permute-start | bytes 983048 | tf_op jit(solution)/shard_map/ppermute | solution.py:12
  10.6 81.7 %collective-permute-start.3 = (f32[4,128,128]{2,1,0:T(8,128)}, f32[4,128,128]{2,1,0:T(8,128)S(1)}, u32[]{:S(2)}, u32[]{:S(2)}) collective-permute-start(f32[4,128,128]{2,1,0:T(8,128)} %get-tuple-element.24), channel_id=1, source_target_pairs={{1021,0},{1022,1},{1023,2},{0,3},{1,4},{2,5},{3,6},{4,7},{5,8},{6,... | collective-permute-start | bytes 786440 | tf_op jit(solution)/shard_map/ppermute | solution.py:12
  14.9 72.4 %collective-permute-start.2 = (f32[3,128,128]{2,1,0:T(8,128)}, f32[3,128,128]{2,1,0:T(8,128)S(1)}, u32[]{:S(2)}, u32[]{:S(2)}) collective-permute-start(f32[3,128,128]{2,1,0:T(8,128)} %get-tuple-element.22), channel_id=1, source_target_pairs={{1020,0},{1021,1},{1022,2},{1023,3},{0,4},{1,5},{2,6},{3,7},{4,8},... | collective-permute-start | bytes 589832 | tf_op jit(solution)/shard_map/ppermute | solution.py:12
  21.7 20.1 %collective-permute-start.11 = (f32[1,128,128]{2,1,0:T(8,128)}, f32[1,128,128]{2,1,0:T(8,128)}, u32[]{:S(2)}, u32[]{:S(2)}) collective-permute-start(f32[1,128,128]{2,1,0:T(8,128)} %get-tuple-element.17), channel_id=1, source_target_pairs={{6,0},{7,1},{8,2},{9,3},{10,4},{11,5},{12,6},{13,7},{14,8},{15,9},... | collective-permute-start | bytes 196616 | tf_op jit(solution)/shard_map/ppermute | solution.py:12
  41.8 15.9 %collective-permute-start.10 = (f32[2,128,128]{2,1,0:T(8,128)}, f32[2,128,128]{2,1,0:T(8,128)S(1)}, u32[]{:S(2)}, u32[]{:S(2)}) collective-permute-start(f32[2,128,128]{2,1,0:T(8,128)} %get-tuple-element.19), channel_id=1, source_target_pairs={{5,0},{6,1},{7,2},{8,3},{9,4},{10,5},{11,6},{12,7},{13,8},{14,9},{... | collective-permute-start | bytes 393224 | tf_op jit(solution)/shard_map/ppermute | solution.py:12
  57.7 16.1 %collective-permute-start.1 = (f32[2,128,128]{2,1,0:T(8,128)S(1)}, f32[2,128,128]{2,1,0:T(8,128)S(1)}, u32[]{:S(2)}, u32[]{:S(2)}) collective-permute-start(f32[2,128,128]{2,1,0:T(8,128)S(1)} %copy-done.3), channel_id=1, source_target_pairs={{1019,0},{1020,1},{1021,2},{1022,3},{1023,4},{0,5},{1,6},{2,7},{3,... | collective-permute-start | bytes 393224 | tf_op jit(solution)/shard_map/ppermute | solution.py:12
  73.8 10.7 %collective-permute-start.9 = (f32[3,128,128]{2,1,0:T(8,128)S(1)}, f32[3,128,128]{2,1,0:T(8,128)S(1)}, u32[]{:S(2)}, u32[]{:S(2)}) collective-permute-start(f32[3,128,128]{2,1,0:T(8,128)S(1)} %copy-done.2), channel_id=1, source_target_pairs={{4,0},{5,1},{6,2},{7,3},{8,4},{9,5},{10,6},{11,7},{12,8},{13,9},{1... | collective-permute-start | bytes 589832 | tf_op jit(solution)/shard_map/ppermute | solution.py:12
  84.4 40.1 %collective-permute-start = (f32[1,128,128]{2,1,0:T(8,128)S(1)}, f32[1,128,128]{2,1,0:T(8,128)S(1)}, u32[]{:S(2)}, u32[]{:S(2)}) collective-permute-start(f32[1,128,128]{2,1,0:T(8,128)S(1)} %copy-done.4), channel_id=1, source_target_pairs={{1018,0},{1019,1},{1020,2},{1021,3},{1022,4},{1023,5},{0,6},{1,7},... | collective-permute-start | bytes 196616 | tf_op jit(solution)/shard_map/ppermute | solution.py:12
  87.3 39.4 %collective-permute-start.6 = (f32[6,128,128]{2,1,0:T(8,128)S(1)}, f32[6,128,128]{2,1,0:T(8,128)S(1)}, u32[]{:S(2)}, u32[]{:S(2)}) collective-permute-start(f32[6,128,128]{2,1,0:T(8,128)S(1)} %get-tuple-element.27), channel_id=1, source_target_pairs={{1,0},{2,1},{3,2},{4,3},{5,4},{6,5},{7,6},{8,7},{9,8},{10,9},{11,1... | collective-permute-start | bytes 1179656 | tf_op jit(solution)/shard_map/ppermute | solution.py:12
  92.3 16.4 %collective-permute-start.8 = (f32[4,128,128]{2,1,0:T(8,128)S(1)}, f32[4,128,128]{2,1,0:T(8,128)S(1)}, u32[]{:S(2)}, u32[]{:S(2)}) collective-permute-start(f32[4,128,128]{2,1,0:T(8,128)S(1)} %copy-done.1), channel_id=1, source_target_pairs={{3,0},{4,1},{5,2},{6,3},{7,4},{8,5},{9,6},{10,7},{11,8},{12,9},{13... | collective-permute-start | bytes 786440 | tf_op jit(solution)/shard_map/ppermute | solution.py:12
  108.8 12.9 %collective-permute-start.7 = (f32[5,128,128]{2,1,0:T(8,128)S(1)}, f32[5,128,128]{2,1,0:T(8,128)S(1)}, u32[]{:S(2)}, u32[]{:S(2)}) collective-permute-start(f32[5,128,128]{2,1,0:T(8,128)S(1)} %get-tuple-element.25), channel_id=1, source_target_pairs={{2,0},{3,1},{4,2},{5,3},{6,4},{7,5},{8,6},{9,7},{10,8},{11,9},{12,... | collective-permute-start | bytes 983048 | tf_op jit(solution)/shard_map/ppermute | solution.py:12
  133.9 122.6 %collective-permute-start.18 = (f32[6,128,128]{2,1,0:T(8,128)S(1)}, f32[6,128,128]{2,1,0:T(8,128)S(1)}, u32[]{:S(2)}, u32[]{:S(2)}) collective-permute-start(f32[6,128,128]{2,1,0:T(8,128)S(1)} %get-tuple-element.15), channel_id=1, source_target_pairs={{1,0},{2,1},{3,2},{4,3},{5,4},{6,5},{7,6},{8,7},{9,8},{10,9},{11,1... | collective-permute-start | bytes 1179656 | tf_op jit(solution)/shard_map/ppermute | solution.py:12
  138.7 114.4 %collective-permute-start.17 = (f32[6,128,128]{2,1,0:T(8,128)S(1)}, f32[6,128,128]{2,1,0:T(8,128)S(1)}, u32[]{:S(2)}, u32[]{:S(2)}) collective-permute-start(f32[6,128,128]{2,1,0:T(8,128)S(1)} %get-tuple-element.16), channel_id=1, source_target_pairs={{1023,0},{0,1},{1,2},{2,3},{3,4},{4,5},{5,6},{6,7},{7,8},{8,9},{9,... | collective-permute-start | bytes 1179656 | tf_op jit(solution)/shard_map/ppermute | solution.py:12
  140.7 107.9 %collective-permute-start.16 = (f32[5,128,128]{2,1,0:T(8,128)S(1)}, f32[5,128,128]{2,1,0:T(8,128)S(1)}, u32[]{:S(2)}, u32[]{:S(2)}) collective-permute-start(f32[5,128,128]{2,1,0:T(8,128)S(1)} %get-tuple-element.14), channel_id=1, source_target_pairs={{1022,0},{1023,1},{0,2},{1,3},{2,4},{3,5},{4,6},{5,7},{6,8},{7,9},... | collective-permute-start | bytes 983048 | tf_op jit(solution)/shard_map/ppermute | solution.py:12
  142.6 79.4 %collective-permute-start.15 = (f32[4,128,128]{2,1,0:T(8,128)S(1)}, f32[4,128,128]{2,1,0:T(8,128)S(1)}, u32[]{:S(2)}, u32[]{:S(2)}) collective-permute-start(f32[4,128,128]{2,1,0:T(8,128)S(1)} %get-tuple-element.12), channel_id=1, source_target_pairs={{1021,0},{1022,1},{1023,2},{0,3},{1,4},{2,5},{3,6},{4,7},{5,8},{6,... | collective-permute-start | bytes 786440 | tf_op jit(solution)/shard_map/ppermute | solution.py:12
  144.5 20.0 %collective-permute-start.23 = (f32[1,128,128]{2,1,0:T(8,128)S(1)}, f32[1,128,128]{2,1,0:T(8,128)S(1)}, u32[]{:S(2)}, u32[]{:S(2)}) collective-permute-start(f32[1,128,128]{2,1,0:T(8,128)S(1)} %get-tuple-element.5), channel_id=1, source_target_pairs={{6,0},{7,1},{8,2},{9,3},{10,4},{11,5},{12,6},{13,7},{14,8},{15,9},... | collective-permute-start | bytes 196616 | tf_op jit(solution)/shard_map/ppermute | solution.py:12
  164.6 16.0 %collective-permute-start.22 = (f32[2,128,128]{2,1,0:T(8,128)S(1)}, f32[2,128,128]{2,1,0:T(8,128)S(1)}, u32[]{:S(2)}, u32[]{:S(2)}) collective-permute-start(f32[2,128,128]{2,1,0:T(8,128)S(1)} %get-tuple-element.7), channel_id=1, source_target_pairs={{5,0},{6,1},{7,2},{8,3},{9,4},{10,5},{11,6},{12,7},{13,8},{14,9},{... | collective-permute-start | bytes 393224 | tf_op jit(solution)/shard_map/ppermute | solution.py:12
  180.6 16.2 %collective-permute-start.13 = (f32[2,128,128]{2,1,0:T(8,128)S(1)}, f32[2,128,128]{2,1,0:T(8,128)S(1)}, u32[]{:S(2)}, u32[]{:S(2)}) collective-permute-start(f32[2,128,128]{2,1,0:T(8,128)S(1)} %get-tuple-element.8), channel_id=1, source_target_pairs={{1019,0},{1020,1},{1021,2},{1022,3},{1023,4},{0,5},{1,6},{2,7},{3,... | collective-permute-start | bytes 393224 | tf_op jit(solution)/shard_map/ppermute | solution.py:12
  196.7 14.3 %collective-permute-start.14 = (f32[3,128,128]{2,1,0:T(8,128)S(1)}, f32[3,128,128]{2,1,0:T(8,128)S(1)}, u32[]{:S(2)}, u32[]{:S(2)}) collective-permute-start(f32[3,128,128]{2,1,0:T(8,128)S(1)} %get-tuple-element.10), channel_id=1, source_target_pairs={{1020,0},{1021,1},{1022,2},{1023,3},{0,4},{1,5},{2,6},{3,7},{4,8},... | collective-permute-start | bytes 589832 | tf_op jit(solution)/shard_map/ppermute | solution.py:12
  211.0 7.9 %collective-permute-start.21 = (f32[3,128,128]{2,1,0:T(8,128)S(1)}, f32[3,128,128]{2,1,0:T(8,128)S(1)}, u32[]{:S(2)}, u32[]{:S(2)}) collective-permute-start(f32[3,128,128]{2,1,0:T(8,128)S(1)} %get-tuple-element.9), channel_id=1, source_target_pairs={{4,0},{5,1},{6,2},{7,3},{8,4},{9,5},{10,6},{11,7},{12,8},{13,9},{1... | collective-permute-start | bytes 589832 | tf_op jit(solution)/shard_map/ppermute | solution.py:12
  218.9 34.5 %collective-permute-start.12 = (f32[1,128,128]{2,1,0:T(8,128)S(1)}, f32[1,128,128]{2,1,0:T(8,128)S(1)}, u32[]{:S(2)}, u32[]{:S(2)}) collective-permute-start(f32[1,128,128]{2,1,0:T(8,128)S(1)} %get-tuple-element.6), channel_id=1, source_target_pairs={{1018,0},{1019,1},{1020,2},{1021,3},{1022,4},{1023,5},{0,6},{1,7},... | collective-permute-start | bytes 196616 | tf_op jit(solution)/shard_map/ppermute | solution.py:12
  222.0 17.4 %collective-permute-start.20 = (f32[4,128,128]{2,1,0:T(8,128)S(1)}, f32[4,128,128]{2,1,0:T(8,128)S(1)}, u32[]{:S(2)}, u32[]{:S(2)}) collective-permute-start(f32[4,128,128]{2,1,0:T(8,128)S(1)} %get-tuple-element.11), channel_id=1, source_target_pairs={{3,0},{4,1},{5,2},{6,3},{7,4},{8,5},{9,6},{10,7},{11,8},{12,9},{13... | collective-permute-start | bytes 786440 | tf_op jit(solution)/shard_map/ppermute | solution.py:12
  239.4 11.8 %collective-permute-start.19 = (f32[5,128,128]{2,1,0:T(8,128)S(1)}, f32[5,128,128]{2,1,0:T(8,128)S(1)}, u32[]{:S(2)}, u32[]{:S(2)}) collective-permute-start(f32[5,128,128]{2,1,0:T(8,128)S(1)} %get-tuple-element.13), channel_id=1, source_target_pairs={{2,0},{3,1},{4,2},{5,3},{6,4},{7,5},{8,6},{9,7},{10,8},{11,9},{12,... | collective-permute-start | bytes 983048 | tf_op jit(solution)/shard_map/ppermute | solution.py:12
  (6 other events, 53.9 us)
where the time goes:
time: 263 us; the launch traced here: 262 us
  starting transfers between devices  135 us (51%)
  waiting for transfers between devices  84.1 us (32%)
  matrix products  35.7 us (14%)
  local copies, waits for them, and re-layouts  4.96 us (2%)
    ppermute x24, starting transfers between devices, from_behind(): return lax.ppermute(block, axis, route)  135 us
    ppermute x24, waiting for transfers between devices, from_behind(): return lax.ppermute(block, axis, route)  84.1 us
    dot_general x140, matrix products, band_product(): lax.dot_general(left_block, right_block, (((left_dim,), (right_dim,)), ((...  35.7 us
  transfers between devices with their start and end apart: 24, of which 13 were waited for; matrix products, arithmetic and copies ran while one was open for 11% of the time, Pallas kernels for 0%

commit v1 on v0

v1 whole, which is shorter than its diff:
```python
import jax
import jax.numpy as jnp
from jax import lax
from jax.sharding import PartitionSpec as P

REACH = 6
WIDTH = REACH + 1
AXES = ("row", "col")
CHIPS_OUT = 3
FLOW_BASE = {1: 0, 2: 11, 3: 18}


def swap_in_chip(x, n):
    return lax.ppermute(x, AXES, [(i, i ^ 1) for i in range(n)])


def exchange(x, is_odd, n):
    partner = swap_in_chip(x, n)
    r0 = jnp.where(is_odd, partner, x)
    r1 = jnp.where(is_odd, x, partner)
    received = []
    for d in range(1, CHIPS_OUT + 1):
        up = jnp.concatenate([r1[2 * d - 1:], r0[2 * d:]], axis=0)
        down = jnp.concatenate([r0[: 8 - 2 * d], r1[: 7 - 2 * d]], axis=0)
        buf = jnp.where(is_odd, up, down)
        step = 2 * d - 1
        route = [(i, (i + step) % n) if i % 2 else (i, (i - step) % n) for i in range(n)]
        received.append(lax.ppermute(buf, AXES, route))
    got = jnp.concatenate(received, axis=0)
    other = swap_in_chip(got, n)
    from_below_chips = jnp.where(is_odd, other, got)
    from_above_chips = jnp.where(is_odd, got, other)
    return r0, r1, from_below_chips, from_above_chips


def block_source(k, o, w, r0, r1, lower, upper):
    q = k + o
    if q == 0:
        return r0[w]
    if q == 1:
        return r1[w]
    if q < 0:
        d = (-q + 1) // 2
        base = FLOW_BASE[d]
        if -q % 2 == 1:
            return lower[base + w - (2 * d - 1)]
        return lower[base + (8 - 2 * d) + w - 2 * d]
    d = q // 2
    base = FLOW_BASE[d]
    if q % 2 == 0:
        return upper[base + w]
    return upper[base + (8 - 2 * d) + w]


def band_window(x, is_odd, n):
    r0, r1, lower, upper = exchange(x, is_odd, n)

    def get(o, w):
        even = block_source(0, o, w, r0, r1, lower, upper)
        odd = block_source(1, o, w, r0, r1, lower, upper)
        return jnp.where(is_odd, odd, even)

    zero = jnp.zeros(x.shape[1:], x.dtype)
    rows = []
    for o in range(-REACH, REACH + 1):
        blocks = []
        for t in range(WIDTH):
            if abs(t - o) > REACH:
                blocks.append(zero)
            elif t >= o:
                blocks.append(get(o, t - o))
            else:
                blocks.append(get(t, o - t).T)
        rows.append(jnp.stack(blocks, axis=1))
    window = jnp.stack(rows, axis=0)
    b = x.shape[-1]
    return window.reshape((2 * REACH + 1) * b, WIDTH * b)


def row_product(left_col, window):
    b = left_col.shape[1]
    out = lax.dot_general(
        left_col,
        window,
        (((0,), (0,)), ((), ())),
        precision=lax.Precision.HIGHEST,
        preferred_element_type=jnp.float32,
    )
    return out.reshape(b, WIDTH, b).transpose(1, 0, 2)


def on_device(density, pattern):
    local_band = density[0]
    n = lax.axis_size("row") * lax.axis_size("col")
    position = lax.axis_index("row") * lax.axis_size("col") + lax.axis_index("col")
    is_odd = (position % 2) == 1
    columns = (position + jnp.arange(WIDTH, dtype=jnp.int32)) % n
    flags = jnp.any(pattern[0][None, :] == columns[:, None], axis=1).astype(jnp.float32)[
        :, None, None
    ]
    b = local_band.shape[-1]
    window_p = band_window(local_band, is_odd, n)
    left_col = window_p[:, :b]
    square = flags * row_product(left_col, window_p)
    window_q = band_window(square, is_odd, n)
    cube = flags * row_product(left_col, window_q)
    return (3.0 * square - 2.0 * cube)[None]


def solution(mesh):
    return jax.shard_map(
        on_device,
        mesh=mesh,
        in_specs=(P(AXES, None, None, None), P(AXES, None)),
        out_specs=P(AXES, None, None, None),
        check_vma=False,
    )
```

time: 263 us -> 284 us (1.080)
  the two profiles are of different devices: /device:TPU:1 before, /device:TPU:65 now
where the time goes in v1:
time: 284 us; the launch traced here: 280 us
  local copies, waits for them, and re-layouts  131 us (46%)
  starting transfers between devices  57.1 us (20%)
  waiting for transfers between devices  37.2 us (13%)
  other arithmetic  34.9 us (12%)
  matrix products  18.7 us (7%)
    unnamed x113, local copies, waits for them, and re-layouts  55.5 us
    another operation x49, local copies, waits for them, and re-layouts, band_window(): rows.append(jnp.stack(blocks, axis=1))  52.7 us
    ppermute x4, starting transfers between devices, swap_in_chip(): return lax.ppermute(x, AXES, [(i, i ^ 1) for i in range(n)])  37.3 us
    ppermute x6, waiting for transfers between devices, exchange(): received.append(lax.ppermute(buf, AXES, route))  33.8 us
    unnamed x35, other arithmetic  23.1 us
    ppermute x6, starting transfers between devices, exchange(): received.append(lax.ppermute(buf, AXES, route))  19.8 us
    dot_general x2, matrix products, row_product(): lax.dot_general(left_col, window, (((0,), (0,)), ((), ())), precision=lax...  18.7 us
    dot_general x2, local copies, waits for them, and re-layouts, row_product(): lax.dot_general(left_col, window, (((0,), (0,)), ((), ())), precision=lax...  14.3 us
  transfers between devices with their start and end apart: 10, of which 6 were waited for; matrix products, arithmetic and copies ran while one was open for 5% of the time, Pallas kernels for 0%

profile of v1, /device:TPU:65, one launch (start us, length us, event | category | flops | bytes accessed | tf_op | source)
XLA Modules:
  0.0 280.3 jit_solution(2504734950862517200)
XLA Ops:
  0.0 2.6 collective-permute-start
  5.5 3.8 %collective-permute-start.1 = (f32[11,128,128]{2,1,0:T(8,128)S(1)}, f32[11,128,128]{2,1,0:T(8,128)S(1)}, u32[]{:S(2)}, u32[]{:S(2)}) collective-permute-start(f32[11,128,128]{2,1,0:T(8,128)S(1)} %maximum_select_fusion), channel_id=1, source_target_pairs={{0,1023},{1,2},{2,1},{3,4},{4,3},{5,6},{6,5},{7,8},{8,7},{9,10},{1... | collective-permute-start | bytes 2162696 | tf_op jit(solution)/shard_map/ppermute | solution.py:28
  9.6 4.5 %collective-permute-start.2 = (f32[7,128,128]{2,1,0:T(8,128)S(1)}, f32[7,128,128]{2,1,0:T(8,128)S(1)}, u32[]{:S(2)}, u32[]{:S(2)}) collective-permute-start(f32[7,128,128]{2,1,0:T(8,128)S(1)} %maximum_select_fusion.2), channel_id=1, source_target_pairs={{0,1021},{1,4},{2,1023},{3,6},{4,1},{5,8},{6,3},{7,10},{8,5},{9,12... | collective-permute-start | bytes 1376264 | tf_op jit(solution)/shard_map/ppermute | solution.py:28
  14.1 5.8 %collective-permute-start.3 = (f32[3,128,128]{2,1,0:T(8,128)S(1)}, f32[3,128,128]{2,1,0:T(8,128)S(1)}, u32[]{:S(2)}, u32[]{:S(2)}) collective-permute-start(f32[3,128,128]{2,1,0:T(8,128)S(1)} %maximum_select_fusion.4), channel_id=1, source_target_pairs={{0,1019},{1,6},{2,1021},{3,8},{4,1023},{5,10},{6,1},{7,12},{8,3},{... | collective-permute-start | bytes 589832 | tf_op jit(solution)/shard_map/ppermute | solution.py:28
  19.9 4.7 %collective-permute-done.1 = f32[11,128,128]{2,1,0:T(8,128)S(1)} collective-permute-done((f32[11,128,128]{2,1,0:T(8,128)S(1)}, f32[11,128,128]{2,1,0:T(8,128)S(1)}, u32[]{:S(2)}, u32[]{:S(2)}) %collective-permute-start.1) | collective-permute-done | bytes 720928 | tf_op jit(solution)/shard_map/ppermute | solution.py:28
  24.6 6.5 %collective-permute-done.2 = f32[7,128,128]{2,1,0:T(8,128)S(1)} collective-permute-done((f32[7,128,128]{2,1,0:T(8,128)S(1)}, f32[7,128,128]{2,1,0:T(8,128)S(1)}, u32[]{:S(2)}, u32[]{:S(2)}) %collective-permute-start.2) | collective-permute-done | bytes 458784 | tf_op jit(solution)/shard_map/ppermute | solution.py:28
  31.2 7.3 %collective-permute-done.3 = f32[3,128,128]{2,1,0:T(8,128)S(1)} collective-permute-done((f32[3,128,128]{2,1,0:T(8,128)S(1)}, f32[3,128,128]{2,1,0:T(8,128)S(1)}, u32[]{:S(2)}, u32[]{:S(2)}) %collective-permute-start.3) | collective-permute-done | bytes 196640 | tf_op jit(solution)/shard_map/ppermute | solution.py:28
  38.5 12.4 %collective-permute-start.4 = (f32[21,128,128]{2,1,0:T(8,128)S(1)}, f32[21,128,128]{2,1,0:T(8,128)}, u32[]{:S(2)}, u32[]{:S(2)}) collective-permute-start(f32[21,128,128]{2,1,0:T(8,128)S(1)} %constant_dynamic-update-slice_fusion), channel_id=1, source_target_pairs={{0,1},{1,0},{2,3},{3,2},{4,5},{5,4},{6,7},{7,6},{8,9},{9,8},{10,11... | collective-permute-start | bytes 4128776 | tf_op jit(solution)/shard_map/ppermute | solution.py:14
  54.4 1.9 broadcast_select_fusion.2
  110.1 4.1 %copy.114 = f32[13,128,7,128]{3,2,1,0:T(8,128)S(1)} copy(f32[13,128,7,128]{3,1,2,0:T(8,128)S(1)} %bitcast_dynamic-update-slice_fusion.10) | data formatting | bytes 11927552 | tf_op jit(solution)/shard_map/stack | solution.py:75
  114.3 4.0 %copy.149 = f32[208,8,7,128]{3,1,2,0:T(8,128)} copy(f32[208,8,7,128]{3,2,1,0:T(8,128)S(1)} %bitcast.575) | data formatting | bytes 11927552
  118.2 4.0 %copy.148 = f32[208,8,7,128]{3,1,2,0:T(8,128)} copy(f32[208,8,7,128]{3,2,1,0:T(8,128)S(1)} %bitcast.576) | data formatting | bytes 11927552
  122.2 7.1 %copy.116 = f32[896,1664]{1,0:T(8,128)} copy(f32[896,1664]{0,1:T(8,128)} %bitcast.579) | data formatting | bytes 11927552 | tf_op jit(solution)/shard_map/dot_general | solution.py:82
  129.4 8.9 %fusion.1 = f32[7,128,128]{2,1,0:T(8,128)S(1)} fusion(f32[7,128,1664]{2,1,0:T(8,128)} %bitcast.580, f32[1664,896]{1,0:T(8,128)} %bitcast.582, f32[7]{0:T(128)S(1)} %convert_element_type.7), kind=kOutput, calls=%fused_computation.5 | convolution fusion | flops 2290204672 | bytes 7274524 | tf_op jit(solution)/shard_map/dot_general | solution.py:82
  138.3 1.9 collective-permute-start.5
  142.3 1.9 collective-permute-start.6
  144.4 1.9 collective-permute-start.7
  149.0 15.3 %collective-permute-done.6 = f32[11,128,128]{2,1,0:T(8,128)S(1)} collective-permute-done((f32[11,128,128]{2,1,0:T(8,128)S(1)}, f32[11,128,128]{2,1,0:T(8,128)S(1)}, u32[]{:S(2)}, u32[]{:S(2)}) %collective-permute-start.6) | collective-permute-done | bytes 720928 | tf_op jit(solution)/shard_map/ppermute | solution.py:28
  164.5 20.4 %collective-permute-start.9 = (f32[21,128,128]{2,1,0:T(8,128)S(1)}, f32[21,128,128]{2,1,0:T(8,128)}, u32[]{:S(2)}, u32[]{:S(2)}) collective-permute-start(f32[21,128,128]{2,1,0:T(8,128)S(1)} %constant_dynamic-update-slice_fusion.71), channel_id=1, source_target_pairs={{0,1},{1,0},{2,3},{3,2},{4,5},{5,4},{6,7},{7,6},{8,9},{9,8},{10,11... | collective-permute-start | bytes 4128776 | tf_op jit(solution)/shard_map/ppermute | solution.py:14
  193.5 1.9 broadcast_select_fusion
  255.3 4.1 %copy.138 = f32[13,128,7,128]{3,2,1,0:T(8,128)S(1)} copy(f32[13,128,7,128]{3,1,2,0:T(8,128)S(1)} %bitcast_dynamic-update-slice_fusion) | data formatting | bytes 11927552 | tf_op jit(solution)/shard_map/stack | solution.py:75
  259.4 4.0 %copy.147 = f32[208,8,7,128]{3,1,2,0:T(8,128)} copy(f32[208,8,7,128]{3,2,1,0:T(8,128)S(1)} %bitcast.577) | data formatting | bytes 11927552
  263.4 7.2 %copy.139 = f32[896,1664]{1,0:T(8,128)} copy(f32[896,1664]{0,1:T(8,128)} %bitcast.581) | data formatting | bytes 11927552 | tf_op jit(solution)/shard_map/dot_general | solution.py:82
  270.6 9.8 %fusion.4 = f32[1,7,128,128]{3,2,1,0:T(8,128)} fusion(f32[7,128,1664]{2,1,0:T(8,128)} %bitcast.578, f32[1664,896]{1,0:T(8,128)} %bitcast.583, f32[7,128,128]{2,1,0:T(8,128)S(1)} %fusion.1, f32[7]{0:T(128)S(1)} %convert_element_type.7), kind=kOutput, calls=%fused_computation.8 | convolution fusion | flops 2290548736 | bytes 7733276 | tf_op jit(solution)/shard_map/dot_general | solution.py:82
  (249 shorter events, 133.1 us)
Async XLA Ops:
  0.0 4.2 %collective-permute-start = (f32[7,128,128]{2,1,0:T(8,128)}, f32[7,128,128]{2,1,0:T(8,128)S(1)}, u32[]{:S(2)}, u32[]{:S(2)}) collective-permute-start(f32[7,128,128]{2,1,0:T(8,128)} %bitcast.584), channel_id=1, source_target_pairs={{0,1},{1,0},{2,3},{3,2},{4,5},{5,4},{6,7},{7,6},{8,9},{9,8},{10,11... | collective-permute-start | bytes 1376264 | tf_op jit(solution)/shard_map/ppermute | solution.py:14
  5.4 45.6 %copy-start.21 = (s32[1,12]{1,0:T(1,128)S(1)}, s32[1,12]{1,0:T(1,128)}, u32[]{:S(2)}) copy-start(s32[1,12]{1,0:T(1,128)} %param.3) | copy-start | bytes 148
  5.5 19.0 %collective-permute-start.1 = (f32[11,128,128]{2,1,0:T(8,128)S(1)}, f32[11,128,128]{2,1,0:T(8,128)S(1)}, u32[]{:S(2)}, u32[]{:S(2)}) collective-permute-start(f32[11,128,128]{2,1,0:T(8,128)S(1)} %maximum_select_fusion), channel_id=1, source_target_pairs={{0,1023},{1,2},{2,1},{3,4},{4,3},{5,6},{6,5},{7,8},{8,7},{9,10},{1... | collective-permute-start | bytes 2162696 | tf_op jit(solution)/shard_map/ppermute | solution.py:28
  9.6 21.6 %collective-permute-start.2 = (f32[7,128,128]{2,1,0:T(8,128)S(1)}, f32[7,128,128]{2,1,0:T(8,128)S(1)}, u32[]{:S(2)}, u32[]{:S(2)}) collective-permute-start(f32[7,128,128]{2,1,0:T(8,128)S(1)} %maximum_select_fusion.2), channel_id=1, source_target_pairs={{0,1021},{1,4},{2,1023},{3,6},{4,1},{5,8},{6,3},{7,10},{8,5},{9,12... | collective-permute-start | bytes 1376264 | tf_op jit(solution)/shard_map/ppermute | solution.py:28
  14.1 24.4 %collective-permute-start.3 = (f32[3,128,128]{2,1,0:T(8,128)S(1)}, f32[3,128,128]{2,1,0:T(8,128)S(1)}, u32[]{:S(2)}, u32[]{:S(2)}) collective-permute-start(f32[3,128,128]{2,1,0:T(8,128)S(1)} %maximum_select_fusion.4), channel_id=1, source_target_pairs={{0,1019},{1,6},{2,1021},{3,8},{4,1023},{5,10},{6,1},{7,12},{8,3},{... | collective-permute-start | bytes 589832 | tf_op jit(solution)/shard_map/ppermute | solution.py:28
  38.5 15.8 %collective-permute-start.4 = (f32[21,128,128]{2,1,0:T(8,128)S(1)}, f32[21,128,128]{2,1,0:T(8,128)}, u32[]{:S(2)}, u32[]{:S(2)}) collective-permute-start(f32[21,128,128]{2,1,0:T(8,128)S(1)} %constant_dynamic-update-slice_fusion), channel_id=1, source_target_pairs={{0,1},{1,0},{2,3},{3,2},{4,5},{5,4},{6,7},{7,6},{8,9},{9,8},{10,11... | collective-permute-start | bytes 4128776 | tf_op jit(solution)/shard_map/ppermute | solution.py:14
  82.2 24.1 %copy-start.17 = (f32[128,1,128]{2,0,1:T(8,128)S(1)}, f32[128,1,128]{2,0,1:T(8,128)}, u32[]{:S(2)}) copy-start(f32[128,1,128]{2,0,1:T(8,128)} %copy.113) | copy-start | bytes 196612
  90.7 18.8 %copy-start.8 = (f32[128,7,128]{2,0,1:T(8,128)S(1)}, f32[128,7,128]{2,0,1:T(8,128)}, u32[]{:S(2)}) copy-start(f32[128,7,128]{2,0,1:T(8,128)} %get-tuple-element.108) | copy-start | bytes 1376260
  90.8 18.9 %copy-start.10 = (f32[128,7,128]{2,0,1:T(8,128)S(1)}, f32[128,7,128]{2,0,1:T(8,128)}, u32[]{:S(2)}) copy-start(f32[128,7,128]{2,0,1:T(8,128)} %get-tuple-element.107) | copy-start | bytes 1376260
  92.1 17.4 %copy-start.12 = (f32[128,7,128]{2,0,1:T(8,128)S(1)}, f32[128,7,128]{2,0,1:T(8,128)}, u32[]{:S(2)}) copy-start(f32[128,7,128]{2,0,1:T(8,128)} %constant_dynamic-update-slice_fusion.15) | copy-start | bytes 1376260
  138.3 3.7 %collective-permute-start.5 = (f32[7,128,128]{2,1,0:T(8,128)S(1)}, f32[7,128,128]{2,1,0:T(8,128)S(1)}, u32[]{:S(2)}, u32[]{:S(2)}) collective-permute-start(f32[7,128,128]{2,1,0:T(8,128)S(1)} %fusion.1), channel_id=1, source_target_pairs={{0,1},{1,0},{2,3},{3,2},{4,5},{5,4},{6,7},{7,6},{8,9},{9,8},{10,11... | collective-permute-start | bytes 1376264 | tf_op jit(solution)/shard_map/ppermute | solution.py:14
  142.3 22.0 %collective-permute-start.6 = (f32[11,128,128]{2,1,0:T(8,128)S(1)}, f32[11,128,128]{2,1,0:T(8,128)S(1)}, u32[]{:S(2)}, u32[]{:S(2)}) collective-permute-start(f32[11,128,128]{2,1,0:T(8,128)S(1)} %maximum_select_fusion.1), channel_id=1, source_target_pairs={{0,1023},{1,2},{2,1},{3,4},{4,3},{5,6},{6,5},{7,8},{8,7},{9,10},{1... | collective-permute-start | bytes 2162696 | tf_op jit(solution)/shard_map/ppermute | solution.py:28
  144.4 20.0 %collective-permute-start.7 = (f32[7,128,128]{2,1,0:T(8,128)S(1)}, f32[7,128,128]{2,1,0:T(8,128)S(1)}, u32[]{:S(2)}, u32[]{:S(2)}) collective-permute-start(f32[7,128,128]{2,1,0:T(8,128)S(1)} %maximum_select_fusion.3), channel_id=1, source_target_pairs={{0,1021},{1,4},{2,1023},{3,6},{4,1},{5,8},{6,3},{7,10},{8,5},{9,12... | collective-permute-start | bytes 1376264 | tf_op jit(solution)/shard_map/ppermute | solution.py:28
  147.1 17.3 %collective-permute-start.8 = (f32[3,128,128]{2,1,0:T(8,128)S(1)}, f32[3,128,128]{2,1,0:T(8,128)S(1)}, u32[]{:S(2)}, u32[]{:S(2)}) collective-permute-start(f32[3,128,128]{2,1,0:T(8,128)S(1)} %maximum_select_fusion.5), channel_id=1, source_target_pairs={{0,1019},{1,6},{2,1021},{3,8},{4,1023},{5,10},{6,1},{7,12},{8,3},{... | collective-permute-start | bytes 589832 | tf_op jit(solution)/shard_map/ppermute | solution.py:28
  164.5 29.0 %copy-start.3 = (f32[21,128,128]{2,1,0:T(8,128)}, f32[21,128,128]{2,1,0:T(8,128)S(1)}, u32[]{:S(2)}) copy-start(f32[21,128,128]{2,1,0:T(8,128)S(1)} %constant_dynamic-update-slice_fusion.71) | copy-start | bytes 4128772
  164.5 29.0 %collective-permute-start.9 = (f32[21,128,128]{2,1,0:T(8,128)S(1)}, f32[21,128,128]{2,1,0:T(8,128)}, u32[]{:S(2)}, u32[]{:S(2)}) collective-permute-start(f32[21,128,128]{2,1,0:T(8,128)S(1)} %constant_dynamic-update-slice_fusion.71), channel_id=1, source_target_pairs={{0,1},{1,0},{2,3},{3,2},{4,5},{5,4},{6,7},{7,6},{8,9},{9,8},{10,11... | collective-permute-start | bytes 4128776 | tf_op jit(solution)/shard_map/ppermute | solution.py:14
  224.4 24.4 %copy-start.20 = (f32[128,1,128]{2,0,1:T(8,128)S(1)}, f32[128,1,128]{2,0,1:T(8,128)}, u32[]{:S(2)}) copy-start(f32[128,1,128]{2,0,1:T(8,128)} %copy.134) | copy-start | bytes 196612
  224.4 24.4 %copy-start.19 = (f32[128,1,128]{2,0,1:T(8,128)S(1)}, f32[128,1,128]{2,0,1:T(8,128)}, u32[]{:S(2)}) copy-start(f32[128,1,128]{2,0,1:T(8,128)} %copy.135) | copy-start | bytes 196612
  224.4 24.4 %copy-start.18 = (f32[128,1,128]{2,0,1:T(8,128)S(1)}, f32[128,1,128]{2,0,1:T(8,128)}, u32[]{:S(2)}) copy-start(f32[128,1,128]{2,0,1:T(8,128)} %copy.136) | copy-start | bytes 196612
  224.4 24.4 %copy-start.16 = (f32[128,1,128]{2,0,1:T(8,128)S(1)}, f32[128,1,128]{2,0,1:T(8,128)}, u32[]{:S(2)}) copy-start(f32[128,1,128]{2,0,1:T(8,128)} %copy.137) | copy-start | bytes 196612
  224.4 24.4 %copy-start.14 = (f32[128,1,128]{2,0,1:T(8,128)S(1)}, f32[128,1,128]{2,0,1:T(8,128)}, u32[]{:S(2)}) copy-start(f32[128,1,128]{2,0,1:T(8,128)} %get-tuple-element.71) | copy-start | bytes 196612
  224.4 24.4 %copy-start.15 = (f32[128,1,128]{2,0,1:T(8,128)S(1)}, f32[128,1,128]{2,0,1:T(8,128)}, u32[]{:S(2)}) copy-start(f32[128,1,128]{2,0,1:T(8,128)} %get-tuple-element.72) | copy-start | bytes 196612
  224.4 24.5 %copy-start.13 = (f32[128,1,128]{2,0,1:T(8,128)S(1)}, f32[128,1,128]{2,0,1:T(8,128)}, u32[]{:S(2)}) copy-start(f32[128,1,128]{2,0,1:T(8,128)} %get-tuple-element.70) | copy-start | bytes 196612
  232.2 18.0 %copy-start.9 = (f32[128,7,128]{2,0,1:T(8,128)S(1)}, f32[128,7,128]{2,0,1:T(8,128)}, u32[]{:S(2)}) copy-start(f32[128,7,128]{2,0,1:T(8,128)} %get-tuple-element.52) | copy-start | bytes 1376260
  (8 other events, 72.1 us)

commit v2 on v0

--- a/solution.py
+++ b/solution.py
@@ -4,23 +4,73 @@
 from jax.sharding import PartitionSpec as P
 
 REACH = 6
+WIDTH = REACH + 1
+AXES = ("row", "col")
+CHIPS_OUT = 3
+FLOW_BASE = {1: 0, 2: 11, 3: 18}
 
 
-def from_behind(block, axis, distance):
-    devices = range(lax.axis_size(axis))
-    route = [((i - distance) % len(devices), i) for i in devices]
-    return lax.ppermute(block, axis, route)
+def swap_in_chip(x, n):
+    return lax.ppermute(x, AXES, [(i, i ^ 1) for i in range(n)])
 
 
-def fetch_rows(local_band):
-    rows_above = []
-    rows_below = []
-    for distance in range(1, REACH + 1):
-        rows_above.append(from_behind(local_band[distance:], ("row", "col"), distance))
-        rows_below.append(
-            from_behind(local_band[: REACH + 1 - distance], ("row", "col"), -distance)
-        )
-    return (rows_above, rows_below)
+def exchange(x, is_odd, n):
+    partner = swap_in_chip(x, n)
+    r0 = jnp.where(is_odd, partner, x)
+    r1 = jnp.where(is_odd, x, partner)
+    received = []
+    for d in range(1, CHIPS_OUT + 1):
+        up = jnp.concatenate([r1[2 * d - 1:], r0[2 * d:]], axis=0)
+        down = jnp.concatenate([r0[: 8 - 2 * d], r1[: 7 - 2 * d]], axis=0)
+        buf = jnp.where(is_odd, up, down)
+        step = 2 * d - 1
+        route = [(i, (i + step) % n) if i % 2 else (i, (i - step) % n) for i in range(n)]
+        received.append(lax.ppermute(buf, AXES, route))
+    got = jnp.concatenate(received, axis=0)
+    other = swap_in_chip(got, n)
+    from_below_chips = jnp.where(is_odd, other, got)
+    from_above_chips = jnp.where(is_odd, got, other)
+    return r0, r1, from_below_chips, from_above_chips
+
+
+def block_source(k, o, w, r0, r1, lower, upper):
+    q = k + o
+    if q == 0:
+        return r0[w]
+    if q == 1:
+        return r1[w]
+    if q < 0:
+        d = (-q + 1) // 2
+        base = FLOW_BASE[d]
+        if -q % 2 == 1:
+            return lower[base + w - (2 * d - 1)]
+        return lower[base + (8 - 2 * d) + w - 2 * d]
+    d = q // 2
+    base = FLOW_BASE[d]
+    if q % 2 == 0:
+        return upper[base + w]
+    return upper[base + (8 - 2 * d) + w]
+
+
+def fetch_rows(x, is_odd, n):
+    r0, r1, lower, upper = exchange(x, is_odd, n)
+
+    def gather(k, sign):
+        blocks = []
+        for d in range(1, REACH + 1):
+            widths = range(d, WIDTH) if sign < 0 else range(WIDTH - d)
+            blocks += [block_source(k, sign * d, w, r0, r1, lower, upper) for w in widths]
+        return jnp.stack(blocks, axis=0)
+
+    above = jnp.where(is_odd, gather(1, -1), gather(0, -1))
+    below = jnp.where(is_odd, gather(1, 1), gather(0, 1))
+    rows_above, rows_below = [], []
+    start = 0
+    for d in range(1, REACH + 1):
+        rows_above.append(above[start:start + WIDTH - d])
+        rows_below.append(below[start:start + WIDTH - d])
+        start += WIDTH - d
+    return rows_above, rows_below
 
 
 def make_upper(local_band, rows_above, rows_below):
@@ -68,16 +118,17 @@
 
 def on_device(density, pattern):
     local_band = density[0]
-    total_rows = lax.axis_size("row") * lax.axis_size("col")
+    n = lax.axis_size("row") * lax.axis_size("col")
     position = lax.axis_index("row") * lax.axis_size("col") + lax.axis_index("col")
-    columns = (position + jnp.arange(REACH + 1, dtype=jnp.int32)) % total_rows
+    is_odd = (position % 2) == 1
+    columns = (position + jnp.arange(WIDTH, dtype=jnp.int32)) % n
     flags = jnp.any(pattern[0][None, :] == columns[:, None], axis=1).astype(jnp.float32)[
         :, None, None
     ]
-    above_p, below_p = fetch_rows(local_band)
+    above_p, below_p = fetch_rows(local_band, is_odd, n)
     upper_p = make_upper(local_band, above_p, below_p)
     square = flags * band_product(upper_p, upper_p)
-    above_s, below_s = fetch_rows(square)
+    above_s, below_s = fetch_rows(square, is_odd, n)
     upper_s = make_upper(square, above_s, below_s)
     cube = flags * band_product(upper_p, upper_s)
     return (3.0 * square - 2.0 * cube)[None]
@@ -87,7 +138,7 @@
     return jax.shard_map(
         on_device,
         mesh=mesh,
-        in_specs=(P(("row", "col"), None, None, None), P(("row", "col"), None)),
-        out_specs=P(("row", "col"), None, None, None),
+        in_specs=(P(AXES, None, None, None), P(AXES, None)),
+        out_specs=P(AXES, None, None, None),
         check_vma=False,
     )

time: 263 us -> 141 us (0.54)
  the two profiles are of different devices: /device:TPU:1 before, /device:TPU:65 now
where the time goes in v2:
time: 141 us
  starting transfers between devices  57.8 us (41%)
  waiting for transfers between devices  41.5 us (29%)
  matrix products  34.7 us (25%)
  other arithmetic  4.21 us (3%)
  between operations  1.48 us (1%)
    ppermute x4, starting transfers between devices, swap_in_chip(): return lax.ppermute(x, AXES, [(i, i ^ 1) for i in range(n)])  37.9 us
    dot_general x140, matrix products, band_product(): lax.dot_general(left_block, right_block, (((left_dim,), (right_dim,)), ((...  34.7 us
    ppermute x6, waiting for transfers between devices, exchange(): received.append(lax.ppermute(buf, AXES, route))  34.4 us
    ppermute x6, starting transfers between devices, exchange(): received.append(lax.ppermute(buf, AXES, route))  19.9 us
    ppermute x4, waiting for transfers between devices, swap_in_chip(): return lax.ppermute(x, AXES, [(i, i ^ 1) for i in range(n)])  7.18 us
  transfers between devices with their start and end apart: 10, of which 8 were waited for; matrix products, arithmetic and copies ran while one was open for 1% of the time, Pallas kernels for 0%

profile of v2, /device:TPU:65, one launch (start us, length us, event | category | flops | bytes accessed | tf_op | source)
XLA Modules:
  0.0 140.9 jit_solution(14343232377136158353)
XLA Ops:
  0.0 2.6 %collective-permute-start = (f32[7,128,128]{2,1,0:T(8,128)}, f32[7,128,128]{2,1,0:T(8,128)S(1)}, u32[]{:S(2)}, u32[]{:S(2)}) collective-permute-start(f32[7,128,128]{2,1,0:T(8,128)} %bitcast.982), channel_id=1, source_target_pairs={{0,1},{1,0},{2,3},{3,2},{4,5},{5,4},{6,7},{7,6},{8,9},{9,8},{10,11... | collective-permute-start | bytes 1376264 | tf_op jit(solution)/shard_map/ppermute | solution.py:14
  2.6 1.6 %collective-permute-done = f32[7,128,128]{2,1,0:T(8,128)S(1)} collective-permute-done((f32[7,128,128]{2,1,0:T(8,128)}, f32[7,128,128]{2,1,0:T(8,128)S(1)}, u32[]{:S(2)}, u32[]{:S(2)}) %collective-permute-start) | collective-permute-done | bytes 458784 | tf_op jit(solution)/shard_map/ppermute | solution.py:14
  4.2 1.1 broadcast_select_fusion.10
  5.6 3.8 %collective-permute-start.1 = (f32[11,128,128]{2,1,0:T(8,128)S(1)}, f32[11,128,128]{2,1,0:T(8,128)S(1)}, u32[]{:S(2)}, u32[]{:S(2)}) collective-permute-start(f32[11,128,128]{2,1,0:T(8,128)S(1)} %maximum_select_fusion), channel_id=1, source_target_pairs={{0,1023},{1,2},{2,1},{3,4},{4,3},{5,6},{6,5},{7,8},{8,7},{9,10},{1... | collective-permute-start | bytes 2162696 | tf_op jit(solution)/shard_map/ppermute | solution.py:28
  9.6 4.5 %collective-permute-start.2 = (f32[7,128,128]{2,1,0:T(8,128)S(1)}, f32[7,128,128]{2,1,0:T(8,128)S(1)}, u32[]{:S(2)}, u32[]{:S(2)}) collective-permute-start(f32[7,128,128]{2,1,0:T(8,128)S(1)} %maximum_select_fusion.2), channel_id=1, source_target_pairs={{0,1021},{1,4},{2,1023},{3,6},{4,1},{5,8},{6,3},{7,10},{8,5},{9,12... | collective-permute-start | bytes 1376264 | tf_op jit(solution)/shard_map/ppermute | solution.py:28
  14.2 5.9 %collective-permute-start.3 = (f32[3,128,128]{2,1,0:T(8,128)S(1)}, f32[3,128,128]{2,1,0:T(8,128)S(1)}, u32[]{:S(2)}, u32[]{:S(2)}) collective-permute-start(f32[3,128,128]{2,1,0:T(8,128)S(1)} %maximum_select_fusion.4), channel_id=1, source_target_pairs={{0,1019},{1,6},{2,1021},{3,8},{4,1023},{5,10},{6,1},{7,12},{8,3},{... | collective-permute-start | bytes 589832 | tf_op jit(solution)/shard_map/ppermute | solution.py:28
  20.1 4.6 %collective-permute-done.1 = f32[11,128,128]{2,1,0:T(8,128)S(1)} collective-permute-done((f32[11,128,128]{2,1,0:T(8,128)S(1)}, f32[11,128,128]{2,1,0:T(8,128)S(1)}, u32[]{:S(2)}, u32[]{:S(2)}) %collective-permute-start.1) | collective-permute-done | bytes 720928 | tf_op jit(solution)/shard_map/ppermute | solution.py:28
  24.7 6.5 %collective-permute-done.2 = f32[7,128,128]{2,1,0:T(8,128)S(1)} collective-permute-done((f32[7,128,128]{2,1,0:T(8,128)S(1)}, f32[7,128,128]{2,1,0:T(8,128)S(1)}, u32[]{:S(2)}, u32[]{:S(2)}) %collective-permute-start.2) | collective-permute-done | bytes 458784 | tf_op jit(solution)/shard_map/ppermute | solution.py:28
  31.3 7.3 %collective-permute-done.3 = f32[3,128,128]{2,1,0:T(8,128)S(1)} collective-permute-done((f32[3,128,128]{2,1,0:T(8,128)S(1)}, f32[3,128,128]{2,1,0:T(8,128)S(1)}, u32[]{:S(2)}, u32[]{:S(2)}) %collective-permute-start.3) | collective-permute-done | bytes 196640 | tf_op jit(solution)/shard_map/ppermute | solution.py:28
  38.6 12.4 %collective-permute-start.4 = (f32[21,128,128]{2,1,0:T(8,128)S(1)}, f32[21,128,128]{2,1,0:T(8,128)S(1)}, u32[]{:S(2)}, u32[]{:S(2)}) collective-permute-start(f32[21,128,128]{2,1,0:T(8,128)S(1)} %constant_dynamic-update-slice_fusion), channel_id=1, source_target_pairs={{0,1},{1,0},{2,3},{3,2},{4,5},{5,4},{6,7},{7,6},{8,9},{9,8},{10,11... | collective-permute-start | bytes 4128776 | tf_op jit(solution)/shard_map/ppermute | solution.py:14
  51.7 2.1 %collective-permute-done.4 = f32[21,128,128]{2,1,0:T(8,128)S(1)} collective-permute-done((f32[21,128,128]{2,1,0:T(8,128)S(1)}, f32[21,128,128]{2,1,0:T(8,128)S(1)}, u32[]{:S(2)}, u32[]{:S(2)}) %collective-permute-start.4) | collective-permute-done | bytes 1376288 | tf_op jit(solution)/shard_map/ppermute | solution.py:14
  58.7 0.3 convolution_add_fusion.48
  62.0 0.3 convolution_add_fusion.31
  72.0 2.3 %collective-permute-start.5 = (f32[7,128,128]{2,1,0:T(8,128)S(1)}, f32[7,128,128]{2,1,0:T(8,128)S(1)}, u32[]{:S(2)}, u32[]{:S(2)}) collective-permute-start(f32[7,128,128]{2,1,0:T(8,128)S(1)} %broadcast_multiply_fusion), channel_id=1, source_target_pairs={{0,1},{1,0},{2,3},{3,2},{4,5},{5,4},{6,7},{7,6},{8,9},{9,8},{10,11... | collective-permute-start | bytes 1376264 | tf_op jit(solution)/shard_map/ppermute | solution.py:14
  74.3 1.4 %collective-permute-done.5 = f32[7,128,128]{2,1,0:T(8,128)S(1)} collective-permute-done((f32[7,128,128]{2,1,0:T(8,128)S(1)}, f32[7,128,128]{2,1,0:T(8,128)S(1)}, u32[]{:S(2)}, u32[]{:S(2)}) %collective-permute-start.5) | collective-permute-done | bytes 458784 | tf_op jit(solution)/shard_map/ppermute | solution.py:14
  76.2 1.9 %collective-permute-start.6 = (f32[11,128,128]{2,1,0:T(8,128)S(1)}, f32[11,128,128]{2,1,0:T(8,128)S(1)}, u32[]{:S(2)}, u32[]{:S(2)}) collective-permute-start(f32[11,128,128]{2,1,0:T(8,128)S(1)} %maximum_select_fusion.1), channel_id=1, source_target_pairs={{0,1023},{1,2},{2,1},{3,4},{4,3},{5,6},{6,5},{7,8},{8,7},{9,10},{1... | collective-permute-start | bytes 2162696 | tf_op jit(solution)/shard_map/ppermute | solution.py:28
  78.3 1.9 %collective-permute-start.7 = (f32[7,128,128]{2,1,0:T(8,128)S(1)}, f32[7,128,128]{2,1,0:T(8,128)S(1)}, u32[]{:S(2)}, u32[]{:S(2)}) collective-permute-start(f32[7,128,128]{2,1,0:T(8,128)S(1)} %maximum_select_fusion.3), channel_id=1, source_target_pairs={{0,1021},{1,4},{2,1023},{3,6},{4,1},{5,8},{6,3},{7,10},{8,5},{9,12... | collective-permute-start | bytes 1376264 | tf_op jit(solution)/shard_map/ppermute | solution.py:28
  80.3 1.9 %collective-permute-start.8 = (f32[3,128,128]{2,1,0:T(8,128)S(1)}, f32[3,128,128]{2,1,0:T(8,128)S(1)}, u32[]{:S(2)}, u32[]{:S(2)}) collective-permute-start(f32[3,128,128]{2,1,0:T(8,128)S(1)} %maximum_select_fusion.5), channel_id=1, source_target_pairs={{0,1019},{1,6},{2,1021},{3,8},{4,1023},{5,10},{6,1},{7,12},{8,3},{... | collective-permute-start | bytes 589832 | tf_op jit(solution)/shard_map/ppermute | solution.py:28
  82.3 16.0 %collective-permute-done.6 = f32[11,128,128]{2,1,0:T(8,128)S(1)} collective-permute-done((f32[11,128,128]{2,1,0:T(8,128)S(1)}, f32[11,128,128]{2,1,0:T(8,128)S(1)}, u32[]{:S(2)}, u32[]{:S(2)}) %collective-permute-start.6) | collective-permute-done | bytes 720928 | tf_op jit(solution)/shard_map/ppermute | solution.py:28
  98.4 20.6 %collective-permute-start.9 = (f32[21,128,128]{2,1,0:T(8,128)S(1)}, f32[21,128,128]{2,1,0:T(8,128)S(1)}, u32[]{:S(2)}, u32[]{:S(2)}) collective-permute-start(f32[21,128,128]{2,1,0:T(8,128)S(1)} %constant_dynamic-update-slice_fusion.19), channel_id=1, source_target_pairs={{0,1},{1,0},{2,3},{3,2},{4,5},{5,4},{6,7},{7,6},{8,9},{9,8},{10,11... | collective-permute-start | bytes 4128776 | tf_op jit(solution)/shard_map/ppermute | solution.py:14
  119.5 2.1 %collective-permute-done.9 = f32[21,128,128]{2,1,0:T(8,128)S(1)} collective-permute-done((f32[21,128,128]{2,1,0:T(8,128)S(1)}, f32[21,128,128]{2,1,0:T(8,128)S(1)}, u32[]{:S(2)}, u32[]{:S(2)}) %collective-permute-start.9) | collective-permute-done | bytes 1376288 | tf_op jit(solution)/shard_map/ppermute | solution.py:14
  121.5 0.3 broadcast_select_fusion.1
  122.1 0.5 broadcast_select_fusion
  140.0 0.9 multiply_subtract_fusion
  (215 shorter events, 36.6 us)
Async XLA Ops:
  0.0 4.2 %collective-permute-start = (f32[7,128,128]{2,1,0:T(8,128)}, f32[7,128,128]{2,1,0:T(8,128)S(1)}, u32[]{:S(2)}, u32[]{:S(2)}) collective-permute-start(f32[7,128,128]{2,1,0:T(8,128)} %bitcast.982), channel_id=1, source_target_pairs={{0,1},{1,0},{2,3},{3,2},{4,5},{5,4},{6,7},{7,6},{8,9},{9,8},{10,11... | collective-permute-start | bytes 1376264 | tf_op jit(solution)/shard_map/ppermute | solution.py:14
  5.6 19.0 %collective-permute-start.1 = (f32[11,128,128]{2,1,0:T(8,128)S(1)}, f32[11,128,128]{2,1,0:T(8,128)S(1)}, u32[]{:S(2)}, u32[]{:S(2)}) collective-permute-start(f32[11,128,128]{2,1,0:T(8,128)S(1)} %maximum_select_fusion), channel_id=1, source_target_pairs={{0,1023},{1,2},{2,1},{3,4},{4,3},{5,6},{6,5},{7,8},{8,7},{9,10},{1... | collective-permute-start | bytes 2162696 | tf_op jit(solution)/shard_map/ppermute | solution.py:28
  9.6 21.7 %collective-permute-start.2 = (f32[7,128,128]{2,1,0:T(8,128)S(1)}, f32[7,128,128]{2,1,0:T(8,128)S(1)}, u32[]{:S(2)}, u32[]{:S(2)}) collective-permute-start(f32[7,128,128]{2,1,0:T(8,128)S(1)} %maximum_select_fusion.2), channel_id=1, source_target_pairs={{0,1021},{1,4},{2,1023},{3,6},{4,1},{5,8},{6,3},{7,10},{8,5},{9,12... | collective-permute-start | bytes 1376264 | tf_op jit(solution)/shard_map/ppermute | solution.py:28
  14.2 36.9 %copy-start.1 = (s32[1,12]{1,0:T(1,128)S(1)}, s32[1,12]{1,0:T(1,128)}, u32[]{:S(2)}) copy-start(s32[1,12]{1,0:T(1,128)} %param.3) | copy-start | bytes 148
  14.2 37.1 %copy-start = (f32[1,7,128,128]{3,2,1,0:T(8,128)S(1)}, f32[1,7,128,128]{3,2,1,0:T(8,128)}, u32[]{:S(2)}) copy-start(f32[1,7,128,128]{3,2,1,0:T(8,128)} %param.2) | copy-start | bytes 1376260
  14.2 24.4 %collective-permute-start.3 = (f32[3,128,128]{2,1,0:T(8,128)S(1)}, f32[3,128,128]{2,1,0:T(8,128)S(1)}, u32[]{:S(2)}, u32[]{:S(2)}) collective-permute-start(f32[3,128,128]{2,1,0:T(8,128)S(1)} %maximum_select_fusion.4), channel_id=1, source_target_pairs={{0,1019},{1,6},{2,1021},{3,8},{4,1023},{5,10},{6,1},{7,12},{8,3},{... | collective-permute-start | bytes 589832 | tf_op jit(solution)/shard_map/ppermute | solution.py:28
  38.6 15.2 %collective-permute-start.4 = (f32[21,128,128]{2,1,0:T(8,128)S(1)}, f32[21,128,128]{2,1,0:T(8,128)S(1)}, u32[]{:S(2)}, u32[]{:S(2)}) collective-permute-start(f32[21,128,128]{2,1,0:T(8,128)S(1)} %constant_dynamic-update-slice_fusion), channel_id=1, source_target_pairs={{0,1},{1,0},{2,3},{3,2},{4,5},{5,4},{6,7},{7,6},{8,9},{9,8},{10,11... | collective-permute-start | bytes 4128776 | tf_op jit(solution)/shard_map/ppermute | solution.py:14
  72.0 3.7 %collective-permute-start.5 = (f32[7,128,128]{2,1,0:T(8,128)S(1)}, f32[7,128,128]{2,1,0:T(8,128)S(1)}, u32[]{:S(2)}, u32[]{:S(2)}) collective-permute-start(f32[7,128,128]{2,1,0:T(8,128)S(1)} %broadcast_multiply_fusion), channel_id=1, source_target_pairs={{0,1},{1,0},{2,3},{3,2},{4,5},{5,4},{6,7},{7,6},{8,9},{9,8},{10,11... | collective-permute-start | bytes 1376264 | tf_op jit(solution)/shard_map/ppermute | solution.py:14
  76.2 22.0 %collective-permute-start.6 = (f32[11,128,128]{2,1,0:T(8,128)S(1)}, f32[11,128,128]{2,1,0:T(8,128)S(1)}, u32[]{:S(2)}, u32[]{:S(2)}) collective-permute-start(f32[11,128,128]{2,1,0:T(8,128)S(1)} %maximum_select_fusion.1), channel_id=1, source_target_pairs={{0,1023},{1,2},{2,1},{3,4},{4,3},{5,6},{6,5},{7,8},{8,7},{9,10},{1... | collective-permute-start | bytes 2162696 | tf_op jit(solution)/shard_map/ppermute | solution.py:28
  78.3 20.0 %collective-permute-start.7 = (f32[7,128,128]{2,1,0:T(8,128)S(1)}, f32[7,128,128]{2,1,0:T(8,128)S(1)}, u32[]{:S(2)}, u32[]{:S(2)}) collective-permute-start(f32[7,128,128]{2,1,0:T(8,128)S(1)} %maximum_select_fusion.3), channel_id=1, source_target_pairs={{0,1021},{1,4},{2,1023},{3,6},{4,1},{5,8},{6,3},{7,10},{8,5},{9,12... | collective-permute-start | bytes 1376264 | tf_op jit(solution)/shard_map/ppermute | solution.py:28
  80.3 18.0 %collective-permute-start.8 = (f32[3,128,128]{2,1,0:T(8,128)S(1)}, f32[3,128,128]{2,1,0:T(8,128)S(1)}, u32[]{:S(2)}, u32[]{:S(2)}) collective-permute-start(f32[3,128,128]{2,1,0:T(8,128)S(1)} %maximum_select_fusion.5), channel_id=1, source_target_pairs={{0,1019},{1,6},{2,1021},{3,8},{4,1023},{5,10},{6,1},{7,12},{8,3},{... | collective-permute-start | bytes 589832 | tf_op jit(solution)/shard_map/ppermute | solution.py:28
  98.4 23.2 %collective-permute-start.9 = (f32[21,128,128]{2,1,0:T(8,128)S(1)}, f32[21,128,128]{2,1,0:T(8,128)S(1)}, u32[]{:S(2)}, u32[]{:S(2)}) collective-permute-start(f32[21,128,128]{2,1,0:T(8,128)S(1)} %constant_dynamic-update-slice_fusion.19), channel_id=1, source_target_pairs={{0,1},{1,0},{2,3},{3,2},{4,5},{5,4},{6,7},{7,6},{8,9},{9,8},{10,11... | collective-permute-start | bytes 4128776 | tf_op jit(solution)/shard_map/ppermute | solution.py:14

commit v3 on v2

--- a/solution.py
+++ b/solution.py
@@ -18,18 +18,23 @@
     partner = swap_in_chip(x, n)
     r0 = jnp.where(is_odd, partner, x)
     r1 = jnp.where(is_odd, x, partner)
-    received = []
-    for d in range(1, CHIPS_OUT + 1):
-        up = jnp.concatenate([r1[2 * d - 1:], r0[2 * d:]], axis=0)
-        down = jnp.concatenate([r0[: 8 - 2 * d], r1[: 7 - 2 * d]], axis=0)
-        buf = jnp.where(is_odd, up, down)
-        step = 2 * d - 1
-        route = [(i, (i + step) % n) if i % 2 else (i, (i - step) % n) for i in range(n)]
-        received.append(lax.ppermute(buf, AXES, route))
-    got = jnp.concatenate(received, axis=0)
-    other = swap_in_chip(got, n)
-    from_below_chips = jnp.where(is_odd, other, got)
-    from_above_chips = jnp.where(is_odd, got, other)
+    up = jnp.concatenate([r1[1:], r0[2:]], axis=0)
+    down = jnp.concatenate([r0[:6], r1[:5]], axis=0)
+    near = [(i, (i + 1) % n) if i % 2 else (i, (i - 1) % n) for i in range(n)]
+    far = [(i, (i - 3) % n) if i % 2 else (i, (i + 3) % n) for i in range(n)]
+    got1 = lax.ppermute(jnp.where(is_odd, up, down), AXES, near)
+    fwd_up = jnp.concatenate([got1[2:6], got1[8:11]], axis=0)
+    fwd_down = jnp.concatenate([got1[0:4], got1[6:9]], axis=0)
+    got2 = lax.ppermute(jnp.where(is_odd, fwd_down, fwd_up), AXES, far)
+    fwd_up = jnp.concatenate([got2[2:4], got2[6:7]], axis=0)
+    fwd_down = jnp.concatenate([got2[0:2], got2[4:5]], axis=0)
+    got3 = lax.ppermute(jnp.where(is_odd, fwd_up, fwd_down), AXES, near)
+    mine = jnp.concatenate([got1, got2, got3], axis=0)
+    other = swap_in_chip(mine, n)
+    a = jnp.concatenate([mine[0:11], other[11:18], mine[18:21]], axis=0)
+    b = jnp.concatenate([other[0:11], mine[11:18], other[18:21]], axis=0)
+    from_below_chips = jnp.where(is_odd, b, a)
+    from_above_chips = jnp.where(is_odd, a, b)
     return r0, r1, from_below_chips, from_above_chips
 
 

time: 141 us -> 155 us (1.099)
  the two profiles are of different devices: /device:TPU:65 before, /device:TPU:1 now
where the time goes in v3:
time: 155 us; the launch traced here: 154 us
  starting transfers between devices  60.3 us (39%)
  waiting for transfers between devices  52.2 us (34%)
  matrix products  34.7 us (22%)
  other arithmetic  4.47 us (3%)
    dot_general x140, matrix products, band_product(): lax.dot_general(left_block, right_block, (((left_dim,), (right_dim,)), ((...  34.7 us
    ppermute x4, starting transfers between devices, swap_in_chip(): return lax.ppermute(x, AXES, [(i, i ^ 1) for i in range(n)])  33.4 us
    ppermute x2, waiting for transfers between devices, exchange(): got1 = lax.ppermute(jnp.where(is_odd, up, down), AXES, near)  21.9 us
    ppermute x2, starting transfers between devices, exchange(): got2 = lax.ppermute(jnp.where(is_odd, fwd_down, fwd_up), AXES, far)  19.2 us
    ppermute x2, waiting for transfers between devices, exchange(): got2 = lax.ppermute(jnp.where(is_odd, fwd_down, fwd_up), AXES, far)  12.6 us
    ppermute x2, waiting for transfers between devices, exchange(): got3 = lax.ppermute(jnp.where(is_odd, fwd_up, fwd_down), AXES, near)  10.1 us
    ppermute x4, waiting for transfers between devices, swap_in_chip(): return lax.ppermute(x, AXES, [(i, i ^ 1) for i in range(n)])  7.58 us
    ppermute x2, starting transfers between devices, exchange(): got3 = lax.ppermute(jnp.where(is_odd, fwd_up, fwd_down), AXES, near)  3.97 us
  transfers between devices with their start and end apart: 10, of which 10 were waited for; matrix products, arithmetic and copies ran while one was open for 0% of the time, Pallas kernels for 0%

profile of v3, /device:TPU:1, one launch (start us, length us, event | category | flops | bytes accessed | tf_op | source)
XLA Modules:
  0.0 154.3 jit_solution(15491733243450903792)
XLA Ops:
  0.0 16.0 %collective-permute-start = (f32[7,128,128]{2,1,0:T(8,128)}, f32[7,128,128]{2,1,0:T(8,128)S(1)}, u32[]{:S(2)}, u32[]{:S(2)}) collective-permute-start(f32[7,128,128]{2,1,0:T(8,128)} %bitcast.984), channel_id=1, source_target_pairs={{0,1},{1,0},{2,3},{3,2},{4,5},{5,4},{6,7},{7,6},{8,9},{9,8},{10,11... | collective-permute-start | bytes 1376264 | tf_op jit(solution)/shard_map/ppermute | solution.py:14
  16.0 1.6 %collective-permute-done = f32[7,128,128]{2,1,0:T(8,128)S(1)} collective-permute-done((f32[7,128,128]{2,1,0:T(8,128)}, f32[7,128,128]{2,1,0:T(8,128)S(1)}, u32[]{:S(2)}, u32[]{:S(2)}) %collective-permute-start) | collective-permute-done | bytes 458784 | tf_op jit(solution)/shard_map/ppermute | solution.py:14
  17.7 1.1 broadcast_select_fusion.6
  19.0 1.9 %collective-permute-start.1 = (f32[11,128,128]{2,1,0:T(8,128)S(1)}, f32[11,128,128]{2,1,0:T(8,128)S(1)}, u32[]{:S(2)}, u32[]{:S(2)}) collective-permute-start(f32[11,128,128]{2,1,0:T(8,128)S(1)} %maximum_select_fusion), channel_id=1, source_target_pairs={{0,1023},{1,2},{2,1},{3,4},{4,3},{5,6},{6,5},{7,8},{8,7},{9,10},{1... | collective-permute-start | bytes 2162696 | tf_op jit(solution)/shard_map/ppermute | solution.py:25
  21.0 11.0 %collective-permute-done.1 = f32[11,128,128]{2,1,0:T(8,128)S(1)} collective-permute-done((f32[11,128,128]{2,1,0:T(8,128)S(1)}, f32[11,128,128]{2,1,0:T(8,128)S(1)}, u32[]{:S(2)}, u32[]{:S(2)}) %collective-permute-start.1) | collective-permute-done | bytes 720928 | tf_op jit(solution)/shard_map/ppermute | solution.py:25
  32.1 10.4 %collective-permute-start.2 = (f32[7,128,128]{2,1,0:T(8,128)S(1)}, f32[7,128,128]{2,1,0:T(8,128)S(1)}, u32[]{:S(2)}, u32[]{:S(2)}) collective-permute-start(f32[7,128,128]{2,1,0:T(8,128)S(1)} %maximum_select_fusion.2), channel_id=1, source_target_pairs={{0,3},{1,1022},{2,5},{3,0},{4,7},{5,2},{6,9},{7,4},{8,11},{9,6},{1... | collective-permute-start | bytes 1376264 | tf_op jit(solution)/shard_map/ppermute | solution.py:28
  42.5 6.1 %collective-permute-done.2 = f32[7,128,128]{2,1,0:T(8,128)S(1)} collective-permute-done((f32[7,128,128]{2,1,0:T(8,128)S(1)}, f32[7,128,128]{2,1,0:T(8,128)S(1)}, u32[]{:S(2)}, u32[]{:S(2)}) %collective-permute-start.2) | collective-permute-done | bytes 458784 | tf_op jit(solution)/shard_map/ppermute | solution.py:28
  48.7 2.1 %collective-permute-start.3 = (f32[3,128,128]{2,1,0:T(8,128)S(1)}, f32[3,128,128]{2,1,0:T(8,128)S(1)}, u32[]{:S(2)}, u32[]{:S(2)}) collective-permute-start(f32[3,128,128]{2,1,0:T(8,128)S(1)} %maximum_select_fusion.4), channel_id=1, source_target_pairs={{0,1023},{1,2},{2,1},{3,4},{4,3},{5,6},{6,5},{7,8},{8,7},{9,10},{1... | collective-permute-start | bytes 589832 | tf_op jit(solution)/shard_map/ppermute | solution.py:31
  50.8 5.1 %collective-permute-done.3 = f32[3,128,128]{2,1,0:T(8,128)S(1)} collective-permute-done((f32[3,128,128]{2,1,0:T(8,128)S(1)}, f32[3,128,128]{2,1,0:T(8,128)S(1)}, u32[]{:S(2)}, u32[]{:S(2)}) %collective-permute-start.3) | collective-permute-done | bytes 196640 | tf_op jit(solution)/shard_map/ppermute | solution.py:31
  56.0 7.5 %collective-permute-start.4 = (f32[21,128,128]{2,1,0:T(8,128)S(1)}, f32[21,128,128]{2,1,0:T(8,128)S(1)}, u32[]{:S(2)}, u32[]{:S(2)}) collective-permute-start(f32[21,128,128]{2,1,0:T(8,128)S(1)} %pad_maximum_fusion.1), channel_id=1, source_target_pairs={{0,1},{1,0},{2,3},{3,2},{4,5},{5,4},{6,7},{7,6},{8,9},{9,8},{10,11... | collective-permute-start | bytes 4128776 | tf_op jit(solution)/shard_map/ppermute | solution.py:14
  63.9 2.3 %collective-permute-done.4 = f32[21,128,128]{2,1,0:T(8,128)S(1)} collective-permute-done((f32[21,128,128]{2,1,0:T(8,128)S(1)}, f32[21,128,128]{2,1,0:T(8,128)S(1)}, u32[]{:S(2)}, u32[]{:S(2)}) %collective-permute-start.4) | collective-permute-done | bytes 1376288 | tf_op jit(solution)/shard_map/ppermute | solution.py:14
  66.3 0.3 fusion.94
  84.9 2.3 %collective-permute-start.5 = (f32[7,128,128]{2,1,0:T(8,128)S(1)}, f32[7,128,128]{2,1,0:T(8,128)S(1)}, u32[]{:S(2)}, u32[]{:S(2)}) collective-permute-start(f32[7,128,128]{2,1,0:T(8,128)S(1)} %broadcast_multiply_fusion), channel_id=1, source_target_pairs={{0,1},{1,0},{2,3},{3,2},{4,5},{5,4},{6,7},{7,6},{8,9},{9,8},{10,11... | collective-permute-start | bytes 1376264 | tf_op jit(solution)/shard_map/ppermute | solution.py:14
  87.2 1.4 collective-permute-done.5
  89.0 1.9 %collective-permute-start.6 = (f32[11,128,128]{2,1,0:T(8,128)S(1)}, f32[11,128,128]{2,1,0:T(8,128)S(1)}, u32[]{:S(2)}, u32[]{:S(2)}) collective-permute-start(f32[11,128,128]{2,1,0:T(8,128)S(1)} %maximum_select_fusion.1), channel_id=1, source_target_pairs={{0,1023},{1,2},{2,1},{3,4},{4,3},{5,6},{6,5},{7,8},{8,7},{9,10},{1... | collective-permute-start | bytes 2162696 | tf_op jit(solution)/shard_map/ppermute | solution.py:25
  91.0 11.0 %collective-permute-done.6 = f32[11,128,128]{2,1,0:T(8,128)S(1)} collective-permute-done((f32[11,128,128]{2,1,0:T(8,128)S(1)}, f32[11,128,128]{2,1,0:T(8,128)S(1)}, u32[]{:S(2)}, u32[]{:S(2)}) %collective-permute-start.6) | collective-permute-done | bytes 720928 | tf_op jit(solution)/shard_map/ppermute | solution.py:25
  102.1 8.8 %collective-permute-start.7 = (f32[7,128,128]{2,1,0:T(8,128)S(1)}, f32[7,128,128]{2,1,0:T(8,128)S(1)}, u32[]{:S(2)}, u32[]{:S(2)}) collective-permute-start(f32[7,128,128]{2,1,0:T(8,128)S(1)} %maximum_select_fusion.3), channel_id=1, source_target_pairs={{0,3},{1,1022},{2,5},{3,0},{4,7},{5,2},{6,9},{7,4},{8,11},{9,6},{1... | collective-permute-start | bytes 1376264 | tf_op jit(solution)/shard_map/ppermute | solution.py:28
  110.9 6.4 %collective-permute-done.7 = f32[7,128,128]{2,1,0:T(8,128)S(1)} collective-permute-done((f32[7,128,128]{2,1,0:T(8,128)S(1)}, f32[7,128,128]{2,1,0:T(8,128)S(1)}, u32[]{:S(2)}, u32[]{:S(2)}) %collective-permute-start.7) | collective-permute-done | bytes 458784 | tf_op jit(solution)/shard_map/ppermute | solution.py:28
  117.4 1.9 %collective-permute-start.8 = (f32[3,128,128]{2,1,0:T(8,128)S(1)}, f32[3,128,128]{2,1,0:T(8,128)S(1)}, u32[]{:S(2)}, u32[]{:S(2)}) collective-permute-start(f32[3,128,128]{2,1,0:T(8,128)S(1)} %maximum_select_fusion.5), channel_id=1, source_target_pairs={{0,1023},{1,2},{2,1},{3,4},{4,3},{5,6},{6,5},{7,8},{8,7},{9,10},{1... | collective-permute-start | bytes 589832 | tf_op jit(solution)/shard_map/ppermute | solution.py:31
  119.3 5.0 %collective-permute-done.8 = f32[3,128,128]{2,1,0:T(8,128)S(1)} collective-permute-done((f32[3,128,128]{2,1,0:T(8,128)S(1)}, f32[3,128,128]{2,1,0:T(8,128)S(1)}, u32[]{:S(2)}, u32[]{:S(2)}) %collective-permute-start.8) | collective-permute-done | bytes 196640 | tf_op jit(solution)/shard_map/ppermute | solution.py:31
  124.5 7.6 %collective-permute-start.9 = (f32[21,128,128]{2,1,0:T(8,128)S(1)}, f32[21,128,128]{2,1,0:T(8,128)S(1)}, u32[]{:S(2)}, u32[]{:S(2)}) collective-permute-start(f32[21,128,128]{2,1,0:T(8,128)S(1)} %pad_maximum_fusion.3), channel_id=1, source_target_pairs={{0,1},{1,0},{2,3},{3,2},{4,5},{5,4},{6,7},{7,6},{8,9},{9,8},{10,11... | collective-permute-start | bytes 4128776 | tf_op jit(solution)/shard_map/ppermute | solution.py:14
  132.4 2.2 %collective-permute-done.9 = f32[21,128,128]{2,1,0:T(8,128)S(1)} collective-permute-done((f32[21,128,128]{2,1,0:T(8,128)S(1)}, f32[21,128,128]{2,1,0:T(8,128)S(1)}, u32[]{:S(2)}, u32[]{:S(2)}) %collective-permute-start.9) | collective-permute-done | bytes 1376288 | tf_op jit(solution)/shard_map/ppermute | solution.py:14
  135.4 0.5 broadcast_select_fusion
  153.4 0.9 multiply_subtract_fusion
  (209 shorter events, 37.5 us)
Async XLA Ops:
  0.0 17.7 %collective-permute-start = (f32[7,128,128]{2,1,0:T(8,128)}, f32[7,128,128]{2,1,0:T(8,128)S(1)}, u32[]{:S(2)}, u32[]{:S(2)}) collective-permute-start(f32[7,128,128]{2,1,0:T(8,128)} %bitcast.984), channel_id=1, source_target_pairs={{0,1},{1,0},{2,3},{3,2},{4,5},{5,4},{6,7},{7,6},{8,9},{9,8},{10,11... | collective-permute-start | bytes 1376264 | tf_op jit(solution)/shard_map/ppermute | solution.py:14
  19.0 12.9 %collective-permute-start.1 = (f32[11,128,128]{2,1,0:T(8,128)S(1)}, f32[11,128,128]{2,1,0:T(8,128)S(1)}, u32[]{:S(2)}, u32[]{:S(2)}) collective-permute-start(f32[11,128,128]{2,1,0:T(8,128)S(1)} %maximum_select_fusion), channel_id=1, source_target_pairs={{0,1023},{1,2},{2,1},{3,4},{4,3},{5,6},{6,5},{7,8},{8,7},{9,10},{1... | collective-permute-start | bytes 2162696 | tf_op jit(solution)/shard_map/ppermute | solution.py:25
  32.1 16.5 %collective-permute-start.2 = (f32[7,128,128]{2,1,0:T(8,128)S(1)}, f32[7,128,128]{2,1,0:T(8,128)S(1)}, u32[]{:S(2)}, u32[]{:S(2)}) collective-permute-start(f32[7,128,128]{2,1,0:T(8,128)S(1)} %maximum_select_fusion.2), channel_id=1, source_target_pairs={{0,3},{1,1022},{2,5},{3,0},{4,7},{5,2},{6,9},{7,4},{8,11},{9,6},{1... | collective-permute-start | bytes 1376264 | tf_op jit(solution)/shard_map/ppermute | solution.py:28
  48.7 14.8 %copy-start.1 = (s32[1,12]{1,0:T(1,128)S(1)}, s32[1,12]{1,0:T(1,128)}, u32[]{:S(2)}) copy-start(s32[1,12]{1,0:T(1,128)} %param.3) | copy-start | bytes 148
  48.7 15.0 %copy-start = (f32[1,7,128,128]{3,2,1,0:T(8,128)S(1)}, f32[1,7,128,128]{3,2,1,0:T(8,128)}, u32[]{:S(2)}) copy-start(f32[1,7,128,128]{3,2,1,0:T(8,128)} %param.2) | copy-start | bytes 1376260
  48.7 7.1 %collective-permute-start.3 = (f32[3,128,128]{2,1,0:T(8,128)S(1)}, f32[3,128,128]{2,1,0:T(8,128)S(1)}, u32[]{:S(2)}, u32[]{:S(2)}) collective-permute-start(f32[3,128,128]{2,1,0:T(8,128)S(1)} %maximum_select_fusion.4), channel_id=1, source_target_pairs={{0,1023},{1,2},{2,1},{3,4},{4,3},{5,6},{6,5},{7,8},{8,7},{9,10},{1... | collective-permute-start | bytes 589832 | tf_op jit(solution)/shard_map/ppermute | solution.py:31
  56.0 10.2 %collective-permute-start.4 = (f32[21,128,128]{2,1,0:T(8,128)S(1)}, f32[21,128,128]{2,1,0:T(8,128)S(1)}, u32[]{:S(2)}, u32[]{:S(2)}) collective-permute-start(f32[21,128,128]{2,1,0:T(8,128)S(1)} %pad_maximum_fusion.1), channel_id=1, source_target_pairs={{0,1},{1,0},{2,3},{3,2},{4,5},{5,4},{6,7},{7,6},{8,9},{9,8},{10,11... | collective-permute-start | bytes 4128776 | tf_op jit(solution)/shard_map/ppermute | solution.py:14
  84.9 3.7 %collective-permute-start.5 = (f32[7,128,128]{2,1,0:T(8,128)S(1)}, f32[7,128,128]{2,1,0:T(8,128)S(1)}, u32[]{:S(2)}, u32[]{:S(2)}) collective-permute-start(f32[7,128,128]{2,1,0:T(8,128)S(1)} %broadcast_multiply_fusion), channel_id=1, source_target_pairs={{0,1},{1,0},{2,3},{3,2},{4,5},{5,4},{6,7},{7,6},{8,9},{9,8},{10,11... | collective-permute-start | bytes 1376264 | tf_op jit(solution)/shard_map/ppermute | solution.py:14
  89.0 12.9 %collective-permute-start.6 = (f32[11,128,128]{2,1,0:T(8,128)S(1)}, f32[11,128,128]{2,1,0:T(8,128)S(1)}, u32[]{:S(2)}, u32[]{:S(2)}) collective-permute-start(f32[11,128,128]{2,1,0:T(8,128)S(1)} %maximum_select_fusion.1), channel_id=1, source_target_pairs={{0,1023},{1,2},{2,1},{3,4},{4,3},{5,6},{6,5},{7,8},{8,7},{9,10},{1... | collective-permute-start | bytes 2162696 | tf_op jit(solution)/shard_map/ppermute | solution.py:25
  102.1 15.2 %collective-permute-start.7 = (f32[7,128,128]{2,1,0:T(8,128)S(1)}, f32[7,128,128]{2,1,0:T(8,128)S(1)}, u32[]{:S(2)}, u32[]{:S(2)}) collective-permute-start(f32[7,128,128]{2,1,0:T(8,128)S(1)} %maximum_select_fusion.3), channel_id=1, source_target_pairs={{0,3},{1,1022},{2,5},{3,0},{4,7},{5,2},{6,9},{7,4},{8,11},{9,6},{1... | collective-permute-start | bytes 1376264 | tf_op jit(solution)/shard_map/ppermute | solution.py:28
  117.4 7.0 %collective-permute-start.8 = (f32[3,128,128]{2,1,0:T(8,128)S(1)}, f32[3,128,128]{2,1,0:T(8,128)S(1)}, u32[]{:S(2)}, u32[]{:S(2)}) collective-permute-start(f32[3,128,128]{2,1,0:T(8,128)S(1)} %maximum_select_fusion.5), channel_id=1, source_target_pairs={{0,1023},{1,2},{2,1},{3,4},{4,3},{5,6},{6,5},{7,8},{8,7},{9,10},{1... | collective-permute-start | bytes 589832 | tf_op jit(solution)/shard_map/ppermute | solution.py:31
  124.5 10.2 %collective-permute-start.9 = (f32[21,128,128]{2,1,0:T(8,128)S(1)}, f32[21,128,128]{2,1,0:T(8,128)S(1)}, u32[]{:S(2)}, u32[]{:S(2)}) collective-permute-start(f32[21,128,128]{2,1,0:T(8,128)S(1)} %pad_maximum_fusion.3), channel_id=1, source_target_pairs={{0,1},{1,0},{2,3},{3,2},{4,5},{5,4},{6,7},{7,6},{8,9},{9,8},{10,11... | collective-permute-start | bytes 4128776 | tf_op jit(solution)/shard_map/ppermute | solution.py:14

commit v4 on v2

--- a/solution.py
+++ b/solution.py
@@ -1,12 +1,15 @@
 import jax
 import jax.numpy as jnp
 from jax import lax
+from jax.experimental import pallas as pl
+from jax.experimental.pallas import tpu as pltpu
 from jax.sharding import PartitionSpec as P
 
 REACH = 6
 WIDTH = REACH + 1
 AXES = ("row", "col")
 CHIPS_OUT = 3
+INTERPRET = False
 FLOW_BASE = {1: 0, 2: 11, 3: 18}
 
 
@@ -64,56 +67,59 @@
 
     above = jnp.where(is_odd, gather(1, -1), gather(0, -1))
     below = jnp.where(is_odd, gather(1, 1), gather(0, 1))
-    rows_above, rows_below = [], []
-    start = 0
-    for d in range(1, REACH + 1):
-        rows_above.append(above[start:start + WIDTH - d])
-        rows_below.append(below[start:start + WIDTH - d])
-        start += WIDTH - d
-    return rows_above, rows_below
+    return above, below
 
 
-def make_upper(local_band, rows_above, rows_below):
-
-    def upper_block(offset, width):
-        if offset == 0:
-            return local_band[width]
-        if offset < 0:
-            return rows_above[-offset - 1][width + offset]
-        return rows_below[offset - 1][width]
-
-    return upper_block
+def row_starts():
+    starts, start = [], 0
+    for d in range(1, REACH + 1):
+        starts.append(start)
+        start += WIDTH - d
+    return starts
 
 
-def left_operand(upper_block, inner):
-    if inner >= 0:
-        return (upper_block(0, inner), 1)
-    return (upper_block(inner, -inner), 0)
+def band_kernel(lp, la, lb, rp, ra, rb, out):
+    starts = row_starts()
 
+    def upper(local, above, below, offset, width):
+        if offset == 0:
+            return local[width]
+        if offset < 0:
+            return above[starts[-offset - 1] + width + offset]
+        return below[starts[offset - 1] + width]
 
-def right_operand(upper_block, inner, target):
-    if target >= inner:
-        return (upper_block(inner, target - inner), 0)
-    return (upper_block(target, inner - target), 1)
-
-
-def band_product(upper_left, upper_right):
-    results = []
-    for target in range(REACH + 1):
+    for target in range(WIDTH):
         total = None
         for inner in range(target - REACH, REACH + 1):
-            left_block, left_dim = left_operand(upper_left, inner)
-            right_block, right_dim = right_operand(upper_right, inner, target)
+            if inner >= 0:
+                left = upper(lp, la, lb, 0, inner)
+            else:
+                left = upper(lp, la, lb, inner, -inner).T
+            if target >= inner:
+                right, right_dim = upper(rp, ra, rb, inner, target - inner), 0
+            else:
+                right, right_dim = upper(rp, ra, rb, target, inner - target), 1
             term = lax.dot_general(
-                left_block,
-                right_block,
-                (((left_dim,), (right_dim,)), ((), ())),
+                left,
+                right,
+                (((1,), (right_dim,)), ((), ())),
                 precision=lax.Precision.HIGHEST,
                 preferred_element_type=jnp.float32,
             )
             total = term if total is None else total + term
-        results.append(total)
-    return jnp.stack(results, axis=0)
+        out[target] = total
+
+
+def band_product(left, right):
+    local = left[0]
+    vmem = pl.BlockSpec(memory_space=pltpu.VMEM)
+    return pl.pallas_call(
+        band_kernel,
+        out_shape=jax.ShapeDtypeStruct(local.shape, jnp.float32),
+        in_specs=[vmem] * 6,
+        out_specs=vmem,
+        interpret=INTERPRET,
+    )(*left, *right)
 
 
 def on_device(density, pattern):
@@ -126,11 +132,10 @@
         :, None, None
     ]
     above_p, below_p = fetch_rows(local_band, is_odd, n)
-    upper_p = make_upper(local_band, above_p, below_p)
-    square = flags * band_product(upper_p, upper_p)
+    band_p = (local_band, above_p, below_p)
+    square = flags * band_product(band_p, band_p)
     above_s, below_s = fetch_rows(square, is_odd, n)
-    upper_s = make_upper(square, above_s, below_s)
-    cube = flags * band_product(upper_p, upper_s)
+    cube = flags * band_product(band_p, (square, above_s, below_s))
     return (3.0 * square - 2.0 * cube)[None]
 
 

time: 141 us -> 131 us (0.929)
  matrix products: 34.7 us -> 0 us
  Pallas kernels: 0 us -> 17.5 us
  other arithmetic: 4.21 us -> 10.8 us
    dot_general x140 -> x0, matrix products: 34.7 us -> none  [band_product(): lax.dot_general(left_block, right_block, (((left_dim,), (right_dim,)), ((...]
    pallas_call x0 -> x2, Pallas kernels: none -> 17.5 us  [band_product(): pl.pallas_call(band_kernel, out_shape=jax.ShapeDtypeStruct(local.shape, j...]
    select_n x2, other arithmetic: 0.68 us -> 3.23 us  [fetch_rows(): below = jnp.where(is_odd, gather(1, 1), gather(0, 1))]
    broadcast_in_dim x0 -> x1, other arithmetic: none -> 1.93 us  [on_device(): return (3.0 * square - 2.0 * cube)[None]]
where the time goes in v4:
time: 131 us; the launch traced here: 130 us
  starting transfers between devices  57.7 us (44%)
  waiting for transfers between devices  42.6 us (33%)
  Pallas kernels  17.5 us (13%)
  other arithmetic  10.8 us (8%)
    ppermute x4, starting transfers between devices, swap_in_chip(): return lax.ppermute(x, AXES, [(i, i ^ 1) for i in range(n)])  37.9 us
    ppermute x6, waiting for transfers between devices, exchange(): received.append(lax.ppermute(buf, AXES, route))  34.5 us
    ppermute x6, starting transfers between devices, exchange(): received.append(lax.ppermute(buf, AXES, route))  19.8 us
    pallas_call x2, Pallas kernels, band_product(): pl.pallas_call(band_kernel, out_shape=jax.ShapeDtypeStruct(local.shape, j...  17.5 us
    ppermute x4, waiting for transfers between devices, swap_in_chip(): return lax.ppermute(x, AXES, [(i, i ^ 1) for i in range(n)])  8.11 us
    select_n x2, other arithmetic, fetch_rows(): below = jnp.where(is_odd, gather(1, 1), gather(0, 1))  3.23 us
  transfers between devices with their start and end apart: 10, of which 8 were waited for; matrix products, arithmetic and copies ran while one was open for 1% of the time, Pallas kernels for 0%

profile of v4, /device:TPU:65, one launch (start us, length us, event | category | flops | bytes accessed | tf_op | source)
XLA Modules:
  0.0 130.3 jit_solution(3278486376853238786)
XLA Ops:
  0.0 2.6 %collective-permute-start = (f32[7,128,128]{2,1,0:T(8,128)}, f32[7,128,128]{2,1,0:T(8,128)S(1)}, u32[]{:S(2)}, u32[]{:S(2)}) collective-permute-start(f32[7,128,128]{2,1,0:T(8,128)} %bitcast.6), channel_id=1, source_target_pairs={{0,1},{1,0},{2,3},{3,2},{4,5},{5,4},{6,7},{7,6},{8,9},{9,8},{10,11... | collective-permute-start | bytes 1376264 | tf_op jit(solution)/shard_map/ppermute | solution.py:17
  2.6 1.6 %collective-permute-done = f32[7,128,128]{2,1,0:T(8,128)S(1)} collective-permute-done((f32[7,128,128]{2,1,0:T(8,128)}, f32[7,128,128]{2,1,0:T(8,128)S(1)}, u32[]{:S(2)}, u32[]{:S(2)}) %collective-permute-start) | collective-permute-done | bytes 458784 | tf_op jit(solution)/shard_map/ppermute | solution.py:17
  5.6 3.8 %collective-permute-start.1 = (f32[11,128,128]{2,1,0:T(8,128)S(1)}, f32[11,128,128]{2,1,0:T(8,128)S(1)}, u32[]{:S(2)}, u32[]{:S(2)}) collective-permute-start(f32[11,128,128]{2,1,0:T(8,128)S(1)} %maximum_select_fusion), channel_id=1, source_target_pairs={{0,1023},{1,2},{2,1},{3,4},{4,3},{5,6},{6,5},{7,8},{8,7},{9,10},{1... | collective-permute-start | bytes 2162696 | tf_op jit(solution)/shard_map/ppermute | solution.py:31
  9.6 4.5 %collective-permute-start.2 = (f32[7,128,128]{2,1,0:T(8,128)S(1)}, f32[7,128,128]{2,1,0:T(8,128)S(1)}, u32[]{:S(2)}, u32[]{:S(2)}) collective-permute-start(f32[7,128,128]{2,1,0:T(8,128)S(1)} %maximum_select_fusion.2), channel_id=1, source_target_pairs={{0,1021},{1,4},{2,1023},{3,6},{4,1},{5,8},{6,3},{7,10},{8,5},{9,12... | collective-permute-start | bytes 1376264 | tf_op jit(solution)/shard_map/ppermute | solution.py:31
  14.2 5.8 %collective-permute-start.3 = (f32[3,128,128]{2,1,0:T(8,128)S(1)}, f32[3,128,128]{2,1,0:T(8,128)S(1)}, u32[]{:S(2)}, u32[]{:S(2)}) collective-permute-start(f32[3,128,128]{2,1,0:T(8,128)S(1)} %maximum_select_fusion.4), channel_id=1, source_target_pairs={{0,1019},{1,6},{2,1021},{3,8},{4,1023},{5,10},{6,1},{7,12},{8,3},{... | collective-permute-start | bytes 589832 | tf_op jit(solution)/shard_map/ppermute | solution.py:31
  19.9 4.7 %collective-permute-done.1 = f32[11,128,128]{2,1,0:T(8,128)S(1)} collective-permute-done((f32[11,128,128]{2,1,0:T(8,128)S(1)}, f32[11,128,128]{2,1,0:T(8,128)S(1)}, u32[]{:S(2)}, u32[]{:S(2)}) %collective-permute-start.1) | collective-permute-done | bytes 720928 | tf_op jit(solution)/shard_map/ppermute | solution.py:31
  24.7 6.5 %collective-permute-done.2 = f32[7,128,128]{2,1,0:T(8,128)S(1)} collective-permute-done((f32[7,128,128]{2,1,0:T(8,128)S(1)}, f32[7,128,128]{2,1,0:T(8,128)S(1)}, u32[]{:S(2)}, u32[]{:S(2)}) %collective-permute-start.2) | collective-permute-done | bytes 458784 | tf_op jit(solution)/shard_map/ppermute | solution.py:31
  31.3 7.3 %collective-permute-done.3 = f32[3,128,128]{2,1,0:T(8,128)S(1)} collective-permute-done((f32[3,128,128]{2,1,0:T(8,128)S(1)}, f32[3,128,128]{2,1,0:T(8,128)S(1)}, u32[]{:S(2)}, u32[]{:S(2)}) %collective-permute-start.3) | collective-permute-done | bytes 196640 | tf_op jit(solution)/shard_map/ppermute | solution.py:31
  38.6 12.4 %collective-permute-start.4 = (f32[21,128,128]{2,1,0:T(8,128)S(1)}, f32[21,128,128]{2,1,0:T(8,128)S(1)}, u32[]{:S(2)}, u32[]{:S(2)}) collective-permute-start(f32[21,128,128]{2,1,0:T(8,128)S(1)} %constant_dynamic-update-slice_fusion), channel_id=1, source_target_pairs={{0,1},{1,0},{2,3},{3,2},{4,5},{5,4},{6,7},{7,6},{8,9},{9,8},{10,11... | collective-permute-start | bytes 4128776 | tf_op jit(solution)/shard_map/ppermute | solution.py:17
  51.2 2.5 %collective-permute-done.4 = f32[21,128,128]{2,1,0:T(8,128)S(1)} collective-permute-done((f32[21,128,128]{2,1,0:T(8,128)S(1)}, f32[21,128,128]{2,1,0:T(8,128)S(1)}, u32[]{:S(2)}, u32[]{:S(2)}) %collective-permute-start.4) | collective-permute-done | bytes 1376288 | tf_op jit(solution)/shard_map/ppermute | solution.py:17
  54.2 1.2 broadcast_select_fusion.4.lb.rb
  55.5 1.2 broadcast_select_fusion.6.la.ra
  56.8 8.7 %shard_map.28 = f32[7,128,128]{2,1,0:T(8,128)} custom-call(f32[7,128,128]{2,1,0:T(8,128)} %bitcast.7, f32[21,128,128]{2,1,0:T(8,128)} %broadcast_select_fusion.6.la.ra, f32[21,128,128]{2,1,0:T(8,128)} %broadcast_select_fusion.4.lb.rb, f32[7,128,128]{2,1,0:T(8,128)} %bitcast.8, f32[21,128,128]{2,1,0:T(8,128)} %broadcast_select_fusion.6.la.ra, ...), custom_call_target="tpu_custom_call" | custom-call | tf_op jit(solution)/shard_map/pallas_call | solution.py:116
  66.6 2.3 %collective-permute-start.5 = (f32[7,128,128]{2,1,0:T(8,128)S(1)}, f32[7,128,128]{2,1,0:T(8,128)S(1)}, u32[]{:S(2)}, u32[]{:S(2)}) collective-permute-start(f32[7,128,128]{2,1,0:T(8,128)S(1)} %broadcast_multiply_fusion.rp), channel_id=1, source_target_pairs={{0,1},{1,0},{2,3},{3,2},{4,5},{5,4},{6,7},{7,6},{8,9},{9,8},{10,11... | collective-permute-start | bytes 1376264 | tf_op jit(solution)/shard_map/ppermute | solution.py:17
  68.9 1.4 %collective-permute-done.5 = f32[7,128,128]{2,1,0:T(8,128)S(1)} collective-permute-done((f32[7,128,128]{2,1,0:T(8,128)S(1)}, f32[7,128,128]{2,1,0:T(8,128)S(1)}, u32[]{:S(2)}, u32[]{:S(2)}) %collective-permute-start.5) | collective-permute-done | bytes 458784 | tf_op jit(solution)/shard_map/ppermute | solution.py:17
  71.8 1.9 %collective-permute-start.6 = (f32[11,128,128]{2,1,0:T(8,128)S(1)}, f32[11,128,128]{2,1,0:T(8,128)S(1)}, u32[]{:S(2)}, u32[]{:S(2)}) collective-permute-start(f32[11,128,128]{2,1,0:T(8,128)S(1)} %maximum_select_fusion.1), channel_id=1, source_target_pairs={{0,1023},{1,2},{2,1},{3,4},{4,3},{5,6},{6,5},{7,8},{8,7},{9,10},{1... | collective-permute-start | bytes 2162696 | tf_op jit(solution)/shard_map/ppermute | solution.py:31
  73.9 1.9 %collective-permute-start.7 = (f32[7,128,128]{2,1,0:T(8,128)S(1)}, f32[7,128,128]{2,1,0:T(8,128)S(1)}, u32[]{:S(2)}, u32[]{:S(2)}) collective-permute-start(f32[7,128,128]{2,1,0:T(8,128)S(1)} %maximum_select_fusion.3), channel_id=1, source_target_pairs={{0,1021},{1,4},{2,1023},{3,6},{4,1},{5,8},{6,3},{7,10},{8,5},{9,12... | collective-permute-start | bytes 1376264 | tf_op jit(solution)/shard_map/ppermute | solution.py:31
  75.9 1.9 %collective-permute-start.8 = (f32[3,128,128]{2,1,0:T(8,128)S(1)}, f32[3,128,128]{2,1,0:T(8,128)S(1)}, u32[]{:S(2)}, u32[]{:S(2)}) collective-permute-start(f32[3,128,128]{2,1,0:T(8,128)S(1)} %maximum_select_fusion.5), channel_id=1, source_target_pairs={{0,1019},{1,6},{2,1021},{3,8},{4,1023},{5,10},{6,1},{7,12},{8,3},{... | collective-permute-start | bytes 589832 | tf_op jit(solution)/shard_map/ppermute | solution.py:31
  77.9 16.0 %collective-permute-done.6 = f32[11,128,128]{2,1,0:T(8,128)S(1)} collective-permute-done((f32[11,128,128]{2,1,0:T(8,128)S(1)}, f32[11,128,128]{2,1,0:T(8,128)S(1)}, u32[]{:S(2)}, u32[]{:S(2)}) %collective-permute-start.6) | collective-permute-done | bytes 720928 | tf_op jit(solution)/shard_map/ppermute | solution.py:31
  94.0 20.6 %collective-permute-start.9 = (f32[21,128,128]{2,1,0:T(8,128)S(1)}, f32[21,128,128]{2,1,0:T(8,128)S(1)}, u32[]{:S(2)}, u32[]{:S(2)}) collective-permute-start(f32[21,128,128]{2,1,0:T(8,128)S(1)} %constant_dynamic-update-slice_fusion.3), channel_id=1, source_target_pairs={{0,1},{1,0},{2,3},{3,2},{4,5},{5,4},{6,7},{7,6},{8,9},{9,8},{10,11... | collective-permute-start | bytes 4128776 | tf_op jit(solution)/shard_map/ppermute | solution.py:17
  114.6 2.6 %collective-permute-done.9 = f32[21,128,128]{2,1,0:T(8,128)S(1)} collective-permute-done((f32[21,128,128]{2,1,0:T(8,128)S(1)}, f32[21,128,128]{2,1,0:T(8,128)S(1)}, u32[]{:S(2)}, u32[]{:S(2)}) %collective-permute-start.9) | collective-permute-done | bytes 1376288 | tf_op jit(solution)/shard_map/ppermute | solution.py:17
  117.6 2.0 %broadcast_select_fusion = (f32[21,128,128]{2,1,0:T(8,128)}, f32[21,128,128]{2,1,0:T(8,128)}) fusion(f32[21,128,128]{2,1,0:T(8,128)S(1)} %get-tuple-element.5, f32[21,128,128]{2,1,0:T(8,128)S(1)} %slice_dynamic-update-slice_fusion.20, pred[]{:T(512)S(6)} %eq.26, f32[21,128,128]{2,1,0:T(8,128)S(1)} %slice_dynamic-update-slice_fusion.21, ...), kind=kLoop, calls=%fused_computation.2 | loop fusion | flops 688128 | bytes 8257537 | tf_op jit(solution)/shard_map/jit(_where)/select_n | solution.py:69
  119.6 8.8 %shard_map.29 = f32[7,128,128]{2,1,0:T(8,128)} custom-call(f32[7,128,128]{2,1,0:T(8,128)} %bitcast.9, f32[21,128,128]{2,1,0:T(8,128)} %broadcast_select_fusion.6.la.ra, f32[21,128,128]{2,1,0:T(8,128)} %broadcast_select_fusion.4.lb.rb, f32[7,128,128]{2,1,0:T(8,128)} %copy-done.1, f32[21,128,128]{2,1,0:T(8,128)} %get-tuple-element.22.ra, ...), custom_call_target="tpu_custom_call" | custom-call | tf_op jit(solution)/shard_map/pallas_call | solution.py:116
  128.4 1.9 %subtract_bitcast_fusion = f32[1,7,128,128]{3,2,1,0:T(8,128)} fusion(f32[7,128,128]{2,1,0:T(8,128)} %shard_map.29, f32[7]{0:T(128)S(1)} %convert_element_type.7, f32[7,128,128]{2,1,0:T(8,128)S(1)} %copy-done), kind=kLoop, calls=%fused_computation.12 | loop fusion | flops 573440 | bytes 1376284 | tf_op jit(solution)/shard_map/broadcast_in_dim | solution.py:139
  (72 shorter events, 5.5 us)
Async XLA Ops:
  0.0 4.2 %collective-permute-start = (f32[7,128,128]{2,1,0:T(8,128)}, f32[7,128,128]{2,1,0:T(8,128)S(1)}, u32[]{:S(2)}, u32[]{:S(2)}) collective-permute-start(f32[7,128,128]{2,1,0:T(8,128)} %bitcast.6), channel_id=1, source_target_pairs={{0,1},{1,0},{2,3},{3,2},{4,5},{5,4},{6,7},{7,6},{8,9},{9,8},{10,11... | collective-permute-start | bytes 1376264 | tf_op jit(solution)/shard_map/ppermute | solution.py:17
  5.6 19.0 %collective-permute-start.1 = (f32[11,128,128]{2,1,0:T(8,128)S(1)}, f32[11,128,128]{2,1,0:T(8,128)S(1)}, u32[]{:S(2)}, u32[]{:S(2)}) collective-permute-start(f32[11,128,128]{2,1,0:T(8,128)S(1)} %maximum_select_fusion), channel_id=1, source_target_pairs={{0,1023},{1,2},{2,1},{3,4},{4,3},{5,6},{6,5},{7,8},{8,7},{9,10},{1... | collective-permute-start | bytes 2162696 | tf_op jit(solution)/shard_map/ppermute | solution.py:31
  9.6 21.7 %collective-permute-start.2 = (f32[7,128,128]{2,1,0:T(8,128)S(1)}, f32[7,128,128]{2,1,0:T(8,128)S(1)}, u32[]{:S(2)}, u32[]{:S(2)}) collective-permute-start(f32[7,128,128]{2,1,0:T(8,128)S(1)} %maximum_select_fusion.2), channel_id=1, source_target_pairs={{0,1021},{1,4},{2,1023},{3,6},{4,1},{5,8},{6,3},{7,10},{8,5},{9,12... | collective-permute-start | bytes 1376264 | tf_op jit(solution)/shard_map/ppermute | solution.py:31
  14.2 36.9 %copy-start.2 = (s32[1,12]{1,0:T(1,128)S(1)}, s32[1,12]{1,0:T(1,128)}, u32[]{:S(2)}) copy-start(s32[1,12]{1,0:T(1,128)} %param.3) | copy-start | bytes 148
  14.2 24.4 %collective-permute-start.3 = (f32[3,128,128]{2,1,0:T(8,128)S(1)}, f32[3,128,128]{2,1,0:T(8,128)S(1)}, u32[]{:S(2)}, u32[]{:S(2)}) collective-permute-start(f32[3,128,128]{2,1,0:T(8,128)S(1)} %maximum_select_fusion.4), channel_id=1, source_target_pairs={{0,1019},{1,6},{2,1021},{3,8},{4,1023},{5,10},{6,1},{7,12},{8,3},{... | collective-permute-start | bytes 589832 | tf_op jit(solution)/shard_map/ppermute | solution.py:31
  38.6 15.2 %collective-permute-start.4 = (f32[21,128,128]{2,1,0:T(8,128)S(1)}, f32[21,128,128]{2,1,0:T(8,128)S(1)}, u32[]{:S(2)}, u32[]{:S(2)}) collective-permute-start(f32[21,128,128]{2,1,0:T(8,128)S(1)} %constant_dynamic-update-slice_fusion), channel_id=1, source_target_pairs={{0,1},{1,0},{2,3},{3,2},{4,5},{5,4},{6,7},{7,6},{8,9},{9,8},{10,11... | collective-permute-start | bytes 4128776 | tf_op jit(solution)/shard_map/ppermute | solution.py:17
  66.6 5.0 %copy-start.1 = (f32[7,128,128]{2,1,0:T(8,128)}, f32[7,128,128]{2,1,0:T(8,128)S(1)}, u32[]{:S(2)}) copy-start(f32[7,128,128]{2,1,0:T(8,128)S(1)} %broadcast_multiply_fusion.rp) | copy-start | bytes 1376260
  66.6 3.7 %collective-permute-start.5 = (f32[7,128,128]{2,1,0:T(8,128)S(1)}, f32[7,128,128]{2,1,0:T(8,128)S(1)}, u32[]{:S(2)}, u32[]{:S(2)}) collective-permute-start(f32[7,128,128]{2,1,0:T(8,128)S(1)} %broadcast_multiply_fusion.rp), channel_id=1, source_target_pairs={{0,1},{1,0},{2,3},{3,2},{4,5},{5,4},{6,7},{7,6},{8,9},{9,8},{10,11... | collective-permute-start | bytes 1376264 | tf_op jit(solution)/shard_map/ppermute | solution.py:17
  71.8 22.0 %collective-permute-start.6 = (f32[11,128,128]{2,1,0:T(8,128)S(1)}, f32[11,128,128]{2,1,0:T(8,128)S(1)}, u32[]{:S(2)}, u32[]{:S(2)}) collective-permute-start(f32[11,128,128]{2,1,0:T(8,128)S(1)} %maximum_select_fusion.1), channel_id=1, source_target_pairs={{0,1023},{1,2},{2,1},{3,4},{4,3},{5,6},{6,5},{7,8},{8,7},{9,10},{1... | collective-permute-start | bytes 2162696 | tf_op jit(solution)/shard_map/ppermute | solution.py:31
  73.9 20.0 %collective-permute-start.7 = (f32[7,128,128]{2,1,0:T(8,128)S(1)}, f32[7,128,128]{2,1,0:T(8,128)S(1)}, u32[]{:S(2)}, u32[]{:S(2)}) collective-permute-start(f32[7,128,128]{2,1,0:T(8,128)S(1)} %maximum_select_fusion.3), channel_id=1, source_target_pairs={{0,1021},{1,4},{2,1023},{3,6},{4,1},{5,8},{6,3},{7,10},{8,5},{9,12... | collective-permute-start | bytes 1376264 | tf_op jit(solution)/shard_map/ppermute | solution.py:31
  75.9 18.0 %collective-permute-start.8 = (f32[3,128,128]{2,1,0:T(8,128)S(1)}, f32[3,128,128]{2,1,0:T(8,128)S(1)}, u32[]{:S(2)}, u32[]{:S(2)}) collective-permute-start(f32[3,128,128]{2,1,0:T(8,128)S(1)} %maximum_select_fusion.5), channel_id=1, source_target_pairs={{0,1019},{1,6},{2,1021},{3,8},{4,1023},{5,10},{6,1},{7,12},{8,3},{... | collective-permute-start | bytes 589832 | tf_op jit(solution)/shard_map/ppermute | solution.py:31
  94.0 23.2 %collective-permute-start.9 = (f32[21,128,128]{2,1,0:T(8,128)S(1)}, f32[21,128,128]{2,1,0:T(8,128)S(1)}, u32[]{:S(2)}, u32[]{:S(2)}) collective-permute-start(f32[21,128,128]{2,1,0:T(8,128)S(1)} %constant_dynamic-update-slice_fusion.3), channel_id=1, source_target_pairs={{0,1},{1,0},{2,3},{3,2},{4,5},{5,4},{6,7},{7,6},{8,9},{9,8},{10,11... | collective-permute-start | bytes 4128776 | tf_op jit(solution)/shard_map/ppermute | solution.py:17
  119.6 8.8 %copy-start = (f32[7,128,128]{2,1,0:T(8,128)S(1)}, f32[7,128,128]{2,1,0:T(8,128)}, u32[]{:S(2)}) copy-start(f32[7,128,128]{2,1,0:T(8,128)} %shard_map.28) | copy-start | bytes 1376260

commit v5 on v1

v5 whole, which is shorter than its diff:
```python
import functools

import jax
import jax.numpy as jnp
from jax import lax
from jax.experimental import pallas as pl
from jax.experimental.pallas import tpu as pltpu
from jax.sharding import PartitionSpec as P

REACH = 6
WIDTH = REACH + 1
AXES = ("row", "col")
CHIPS_OUT = 3
INTERPRET = False
FLOW_BASE = {1: 0, 2: 11, 3: 18}


def swap_in_chip(x, n):
    return lax.ppermute(x, AXES, [(i, i ^ 1) for i in range(n)])


def block_source(k, o, w, r0, r1, lower, upper):
    q = k + o
    if q == 0:
        return r0[w]
    if q == 1:
        return r1[w]
    if q < 0:
        d = (-q + 1) // 2
        base = FLOW_BASE[d]
        if -q % 2 == 1:
            return lower[base + w - (2 * d - 1)]
        return lower[base + (8 - 2 * d) + w - 2 * d]
    d = q // 2
    base = FLOW_BASE[d]
    if q % 2 == 0:
        return upper[base + w]
    return upper[base + (8 - 2 * d) + w]


def chip_refs(k, own, partner, got, other):
    if k == 0:
        return own, partner, got, other
    return partner, own, other, got


def band_kernel(parity, flags, lx, lp, lg, lo, rx, rp, rg, ro, out, *, final):
    def compute(k):
        left = chip_refs(k, lx, lp, lg, lo)
        right = chip_refs(k, rx, rp, rg, ro)
        for target in range(WIDTH):
            total = None
            for inner in range(target - REACH, REACH + 1):
                if inner >= 0:
                    a = block_source(k, 0, inner, *left)
                else:
                    a = block_source(k, inner, -inner, *left).T
                if target >= inner:
                    b, b_dim = block_source(k, inner, target - inner, *right), 0
                else:
                    b, b_dim = block_source(k, target, inner - target, *right), 1
                term = lax.dot_general(
                    a,
                    b,
                    (((1,), (b_dim,)), ((), ())),
                    precision=lax.Precision.HIGHEST,
                    preferred_element_type=jnp.float32,
                )
                total = term if total is None else total + term
            total = flags[target] * total
            if final:
                total = 3.0 * rx[target] - 2.0 * total
            out[target] = total

    for k in (0, 1):
        pl.when(parity[0] == k)(lambda k=k: compute(k))


def band_product(parity, flags, left, right, final):
    vmem = pl.BlockSpec(memory_space=pltpu.VMEM)
    smem = pl.BlockSpec(memory_space=pltpu.SMEM)
    local = left[0]
    return pl.pallas_call(
        functools.partial(band_kernel, final=final),
        out_shape=jax.ShapeDtypeStruct(local.shape, jnp.float32),
        in_specs=[smem, smem] + [vmem] * 8,
        out_specs=vmem,
        interpret=INTERPRET,
    )(parity, flags, *left, *right)


def exchange_rows(x, is_odd, n):
    partner = swap_in_chip(x, n)
    r0 = jnp.where(is_odd, partner, x)
    r1 = jnp.where(is_odd, x, partner)
    received = []
    for d in range(1, CHIPS_OUT + 1):
        up = jnp.concatenate([r1[2 * d - 1:], r0[2 * d:]], axis=0)
        down = jnp.concatenate([r0[: 8 - 2 * d], r1[: 7 - 2 * d]], axis=0)
        buf = jnp.where(is_odd, up, down)
        step = 2 * d - 1
        route = [(i, (i + step) % n) if i % 2 else (i, (i - step) % n) for i in range(n)]
        received.append(lax.ppermute(buf, AXES, route))
    got = jnp.concatenate(received, axis=0)
    other = swap_in_chip(got, n)
    return (x, partner, got, other)


def on_device(density, pattern):
    local_band = density[0]
    n = lax.axis_size("row") * lax.axis_size("col")
    position = lax.axis_index("row") * lax.axis_size("col") + lax.axis_index("col")
    is_odd = (position % 2) == 1
    parity = (position % 2).astype(jnp.int32).reshape(1)
    columns = (position + jnp.arange(WIDTH, dtype=jnp.int32)) % n
    flags = jnp.any(pattern[0][None, :] == columns[:, None], axis=1).astype(jnp.float32)
    chip_p = exchange_rows(local_band, is_odd, n)
    square = band_product(parity, flags, chip_p, chip_p, final=False)
    chip_s = exchange_rows(square, is_odd, n)
    purified = band_product(parity, flags, chip_p, chip_s, final=True)
    return purified[None]


def solution(mesh):
    return jax.shard_map(
        on_device,
        mesh=mesh,
        in_specs=(P(AXES, None, None, None), P(AXES, None)),
        out_specs=P(AXES, None, None, None),
        check_vma=False,
    )
```

time: 284 us -> 125 us (0.44); the launches traced: 280 us -> 125 us
  local copies, waits for them, and re-layouts: 131 us -> 2.81 us
  other arithmetic: 34.9 us -> 3.58 us
  matrix products: 18.7 us -> 0 us
  Pallas kernels: 0 us -> 18.2 us
  waiting for transfers between devices: 37.2 us -> 42.3 us
    another operation x56 -> x0, local copies, waits for them, and re-layouts: 61.1 us -> none  [the longest x49 52.7 us: band_window(): rows.append(jnp.stack(blocks, axis=1))]
    unnamed x113 -> x18, local copies, waits for them, and re-layouts: 55.5 us -> 2.37 us
    unnamed x35 -> x0, other arithmetic: 23.1 us -> none
    dot_general x2 -> x0, matrix products: 18.7 us -> none  [row_product(): lax.dot_general(left_col, window, (((0,), (0,)), ((), ())), precision=lax...]
    pallas_call x0 -> x2, Pallas kernels: none -> 18.2 us  [band_product(): pl.pallas_call(functools.partial(band_kernel, final=final), out_shape=jax...]
    dot_general x2 -> x0, local copies, waits for them, and re-layouts: 14.3 us -> none  [row_product(): lax.dot_general(left_col, window, (((0,), (0,)), ((), ())), precision=lax...]
    another operation x8 -> x0, other arithmetic: 4.71 us -> none  [band_window(): rows.append(jnp.stack(blocks, axis=1))]
    ppermute x4, waiting for transfers between devices: 3.4 us -> 7.96 us  [swap_in_chip(): return lax.ppermute(x, AXES, [(i, i ^ 1) for i in range(n)])]
  transfers between devices with their start and end apart: 10 -> 10, of which waited for: 6 -> 8; matrix products, arithmetic and copies ran while one was open for 5% -> 1% of each run, Pallas kernels for 0% -> 0%
where the time goes in v5:
time: 125 us
  starting transfers between devices  57.6 us (46%)
  waiting for transfers between devices  42.3 us (34%)
  Pallas kernels  18.2 us (15%)
  other arithmetic  3.58 us (3%)
  local copies, waits for them, and re-layouts  2.81 us (2%)
    ppermute x4, starting transfers between devices, swap_in_chip(): return lax.ppermute(x, AXES, [(i, i ^ 1) for i in range(n)])  37.7 us
    ppermute x6, waiting for transfers between devices, exchange_rows(): received.append(lax.ppermute(buf, AXES, route))  34.4 us
    ppermute x6, starting transfers between devices, exchange_rows(): received.append(lax.ppermute(buf, AXES, route))  20 us
    pallas_call x2, Pallas kernels, band_product(): pl.pallas_call(functools.partial(band_kernel, final=final), out_shape=jax...  18.2 us
    ppermute x4, waiting for transfers between devices, swap_in_chip(): return lax.ppermute(x, AXES, [(i, i ^ 1) for i in range(n)])  7.96 us
    select_n x2, other arithmetic, exchange_rows(): r1 = jnp.where(is_odd, x, partner)  2.52 us
  transfers between devices with their start and end apart: 10, of which 8 were waited for; matrix products, arithmetic and copies ran while one was open for 1% of the time, Pallas kernels for 0%

profile of v5, /device:TPU:65, one launch (start us, length us, event | category | flops | bytes accessed | tf_op | source)
XLA Modules:
  0.0 125.0 jit_solution(16791546730332472103)
XLA Ops:
  0.0 2.6 %collective-permute-start = (f32[7,128,128]{2,1,0:T(8,128)}, f32[7,128,128]{2,1,0:T(8,128)S(1)}, u32[]{:S(2)}, u32[]{:S(2)}) collective-permute-start(f32[7,128,128]{2,1,0:T(8,128)} %bitcast.6), channel_id=1, source_target_pairs={{0,1},{1,0},{2,3},{3,2},{4,5},{5,4},{6,7},{7,6},{8,9},{9,8},{10,11... | collective-permute-start | bytes 1376264 | tf_op jit(solution)/shard_map/ppermute | solution.py:19
  2.6 1.6 %collective-permute-done.lp.rp = f32[7,128,128]{2,1,0:T(8,128)S(1)} collective-permute-done((f32[7,128,128]{2,1,0:T(8,128)}, f32[7,128,128]{2,1,0:T(8,128)S(1)}, u32[]{:S(2)}, u32[]{:S(2)}) %collective-permute-start) | collective-permute-done | bytes 458784 | tf_op jit(solution)/shard_map/ppermute | solution.py:19
  4.2 1.3 %broadcast_select_fusion.3 = (f32[7,128,128]{2,1,0:T(8,128)S(1)}, f32[7,128,128]{2,1,0:T(8,128)S(1)}) fusion(f32[7,128,128]{2,1,0:T(8,128)S(1)} %collective-permute-done.lp.rp, pred[]{:T(512)S(6)} %eq.27, f32[1,7,128,128]{3,2,1,0:T(8,128)} %param.2), kind=kLoop, calls=%fused_computation.7 | loop fusion | flops 229376 | bytes 1835009 | tf_op jit(solution)/shard_map/jit(_where)/select_n | solution.py:95
  5.7 3.8 %collective-permute-start.1 = (f32[11,128,128]{2,1,0:T(8,128)S(1)}, f32[11,128,128]{2,1,0:T(8,128)S(1)}, u32[]{:S(2)}, u32[]{:S(2)}) collective-permute-start(f32[11,128,128]{2,1,0:T(8,128)S(1)} %maximum_select_fusion), channel_id=1, source_target_pairs={{0,1023},{1,2},{2,1},{3,4},{4,3},{5,6},{6,5},{7,8},{8,7},{9,10},{1... | collective-permute-start | bytes 2162696 | tf_op jit(solution)/shard_map/ppermute | solution.py:103
  9.7 4.5 %collective-permute-start.2 = (f32[7,128,128]{2,1,0:T(8,128)S(1)}, f32[7,128,128]{2,1,0:T(8,128)S(1)}, u32[]{:S(2)}, u32[]{:S(2)}) collective-permute-start(f32[7,128,128]{2,1,0:T(8,128)S(1)} %maximum_select_fusion.2), channel_id=1, source_target_pairs={{0,1021},{1,4},{2,1023},{3,6},{4,1},{5,8},{6,3},{7,10},{8,5},{9,12... | collective-permute-start | bytes 1376264 | tf_op jit(solution)/shard_map/ppermute | solution.py:103
  14.3 5.8 %collective-permute-start.3 = (f32[3,128,128]{2,1,0:T(8,128)S(1)}, f32[3,128,128]{2,1,0:T(8,128)S(1)}, u32[]{:S(2)}, u32[]{:S(2)}) collective-permute-start(f32[3,128,128]{2,1,0:T(8,128)S(1)} %maximum_select_fusion.4), channel_id=1, source_target_pairs={{0,1019},{1,6},{2,1021},{3,8},{4,1023},{5,10},{6,1},{7,12},{8,3},{... | collective-permute-start | bytes 589832 | tf_op jit(solution)/shard_map/ppermute | solution.py:103
  20.0 4.7 %collective-permute-done.1 = f32[11,128,128]{2,1,0:T(8,128)S(1)} collective-permute-done((f32[11,128,128]{2,1,0:T(8,128)S(1)}, f32[11,128,128]{2,1,0:T(8,128)S(1)}, u32[]{:S(2)}, u32[]{:S(2)}) %collective-permute-start.1) | collective-permute-done | bytes 720928 | tf_op jit(solution)/shard_map/ppermute | solution.py:103
  24.8 6.5 %collective-permute-done.2 = f32[7,128,128]{2,1,0:T(8,128)S(1)} collective-permute-done((f32[7,128,128]{2,1,0:T(8,128)S(1)}, f32[7,128,128]{2,1,0:T(8,128)S(1)}, u32[]{:S(2)}, u32[]{:S(2)}) %collective-permute-start.2) | collective-permute-done | bytes 458784 | tf_op jit(solution)/shard_map/ppermute | solution.py:103
  31.4 7.3 %collective-permute-done.3 = f32[3,128,128]{2,1,0:T(8,128)S(1)} collective-permute-done((f32[3,128,128]{2,1,0:T(8,128)S(1)}, f32[3,128,128]{2,1,0:T(8,128)S(1)}, u32[]{:S(2)}, u32[]{:S(2)}) %collective-permute-start.3) | collective-permute-done | bytes 196640 | tf_op jit(solution)/shard_map/ppermute | solution.py:103
  38.7 12.4 %collective-permute-start.4 = (f32[21,128,128]{2,1,0:T(8,128)S(1)}, f32[21,128,128]{2,1,0:T(8,128)S(1)}, u32[]{:S(2)}, u32[]{:S(2)}) collective-permute-start(f32[21,128,128]{2,1,0:T(8,128)S(1)} %constant_dynamic-update-slice_fusion.lg.rg), channel_id=1, source_target_pairs={{0,1},{1,0},{2,3},{3,2},{4,5},{5,4},{6,7},{7,6},{8,9},{9,8},{10,11... | collective-permute-start | bytes 4128776 | tf_op jit(solution)/shard_map/ppermute | solution.py:19
  51.9 2.0 %collective-permute-done.4.lo.ro = f32[21,128,128]{2,1,0:T(8,128)S(1)} collective-permute-done((f32[21,128,128]{2,1,0:T(8,128)S(1)}, f32[21,128,128]{2,1,0:T(8,128)S(1)}, u32[]{:S(2)}, u32[]{:S(2)}) %collective-permute-start.4) | collective-permute-done | bytes 1376288 | tf_op jit(solution)/shard_map/ppermute | solution.py:19
  53.9 1.1 copy-done.1
  55.0 9.1 %shard_map.28.rx = f32[7,128,128]{2,1,0:T(8,128)} custom-call(s32[1]{0:T(128)} %bitcast.parity, f32[7]{0:T(128)} %convert_element_type.3.flags, f32[7,128,128]{2,1,0:T(8,128)} %bitcast.7, f32[7,128,128]{2,1,0:T(8,128)} %copy-done.2, f32[21,128,128]{2,1,0:T(8,128)} %copy-done, f32[21,128,128]{2,1,0:T(8,128)} %copy-done.1, f32[7,128,128]{2,1,0:T(8,128)} %bitcast.8, ...), custom_call_target="tpu_custom_call" | custom-call | tf_op jit(solution)/shard_map/pallas_call | solution.py:83
  64.0 2.3 %collective-permute-start.5 = (f32[7,128,128]{2,1,0:T(8,128)}, f32[7,128,128]{2,1,0:T(8,128)S(1)}, u32[]{:S(2)}, u32[]{:S(2)}) collective-permute-start(f32[7,128,128]{2,1,0:T(8,128)} %shard_map.28.rx), channel_id=1, source_target_pairs={{0,1},{1,0},{2,3},{3,2},{4,5},{5,4},{6,7},{7,6},{8,9},{9,8},{10,11... | collective-permute-start | bytes 1376264 | tf_op jit(solution)/shard_map/ppermute | solution.py:19
  66.3 1.6 %collective-permute-done.5.rp = f32[7,128,128]{2,1,0:T(8,128)S(1)} collective-permute-done((f32[7,128,128]{2,1,0:T(8,128)}, f32[7,128,128]{2,1,0:T(8,128)S(1)}, u32[]{:S(2)}, u32[]{:S(2)}) %collective-permute-start.5) | collective-permute-done | bytes 458784 | tf_op jit(solution)/shard_map/ppermute | solution.py:19
  68.0 1.3 %broadcast_select_fusion.1 = (f32[7,128,128]{2,1,0:T(8,128)S(1)}, f32[7,128,128]{2,1,0:T(8,128)S(1)}) fusion(f32[7,128,128]{2,1,0:T(8,128)} %shard_map.28.rx, f32[7,128,128]{2,1,0:T(8,128)S(1)} %collective-permute-done.5.rp, pred[]{:T(512)S(6)} %eq.27), kind=kLoop, calls=%fused_computation.5 | loop fusion | flops 229376 | bytes 1835009 | tf_op jit(solution)/shard_map/jit(_where)/select_n | solution.py:95
  69.5 2.1 %collective-permute-start.6 = (f32[11,128,128]{2,1,0:T(8,128)S(1)}, f32[11,128,128]{2,1,0:T(8,128)S(1)}, u32[]{:S(2)}, u32[]{:S(2)}) collective-permute-start(f32[11,128,128]{2,1,0:T(8,128)S(1)} %maximum_select_fusion.1), channel_id=1, source_target_pairs={{0,1023},{1,2},{2,1},{3,4},{4,3},{5,6},{6,5},{7,8},{8,7},{9,10},{1... | collective-permute-start | bytes 2162696 | tf_op jit(solution)/shard_map/ppermute | solution.py:103
  71.7 1.9 %collective-permute-start.7 = (f32[7,128,128]{2,1,0:T(8,128)S(1)}, f32[7,128,128]{2,1,0:T(8,128)S(1)}, u32[]{:S(2)}, u32[]{:S(2)}) collective-permute-start(f32[7,128,128]{2,1,0:T(8,128)S(1)} %maximum_select_fusion.3), channel_id=1, source_target_pairs={{0,1021},{1,4},{2,1023},{3,6},{4,1},{5,8},{6,3},{7,10},{8,5},{9,12... | collective-permute-start | bytes 1376264 | tf_op jit(solution)/shard_map/ppermute | solution.py:103
  73.7 1.9 %collective-permute-start.8 = (f32[3,128,128]{2,1,0:T(8,128)S(1)}, f32[3,128,128]{2,1,0:T(8,128)S(1)}, u32[]{:S(2)}, u32[]{:S(2)}) collective-permute-start(f32[3,128,128]{2,1,0:T(8,128)S(1)} %maximum_select_fusion.5), channel_id=1, source_target_pairs={{0,1019},{1,6},{2,1021},{3,8},{4,1023},{5,10},{6,1},{7,12},{8,3},{... | collective-permute-start | bytes 589832 | tf_op jit(solution)/shard_map/ppermute | solution.py:103
  75.7 15.8 %collective-permute-done.6 = f32[11,128,128]{2,1,0:T(8,128)S(1)} collective-permute-done((f32[11,128,128]{2,1,0:T(8,128)S(1)}, f32[11,128,128]{2,1,0:T(8,128)S(1)}, u32[]{:S(2)}, u32[]{:S(2)}) %collective-permute-start.6) | collective-permute-done | bytes 720928 | tf_op jit(solution)/shard_map/ppermute | solution.py:103
  91.6 20.4 %collective-permute-start.9 = (f32[21,128,128]{2,1,0:T(8,128)S(1)}, f32[21,128,128]{2,1,0:T(8,128)S(1)}, u32[]{:S(2)}, u32[]{:S(2)}) collective-permute-start(f32[21,128,128]{2,1,0:T(8,128)S(1)} %constant_dynamic-update-slice_fusion.3.rg), channel_id=1, source_target_pairs={{0,1},{1,0},{2,3},{3,2},{4,5},{5,4},{6,7},{7,6},{8,9},{9,8},{10,11... | collective-permute-start | bytes 4128776 | tf_op jit(solution)/shard_map/ppermute | solution.py:19
  112.1 2.7 %collective-permute-done.9.ro = f32[21,128,128]{2,1,0:T(8,128)S(1)} collective-permute-done((f32[21,128,128]{2,1,0:T(8,128)S(1)}, f32[21,128,128]{2,1,0:T(8,128)S(1)}, u32[]{:S(2)}, u32[]{:S(2)}) %collective-permute-start.9) | collective-permute-done | bytes 1376288 | tf_op jit(solution)/shard_map/ppermute | solution.py:19
  114.8 1.1 copy-done.5
  115.9 9.1 %shard_map.29 = f32[7,128,128]{2,1,0:T(8,128)} custom-call(s32[1]{0:T(128)} %bitcast.parity, f32[7]{0:T(128)} %convert_element_type.3.flags, f32[7,128,128]{2,1,0:T(8,128)} %bitcast.9, f32[7,128,128]{2,1,0:T(8,128)} %copy-done.2, f32[21,128,128]{2,1,0:T(8,128)} %copy-done, f32[21,128,128]{2,1,0:T(8,128)} %copy-done.1, f32[7,128,128]{2,1,0:T(8,128)} %shard_map.28.rx, ...), custom_call_target="tpu_custom_call" | custom-call | tf_op jit(solution)/shard_map/pallas_call | solution.py:83
  (53 shorter events, 1.7 us)
Async XLA Ops:
  0.0 4.2 %collective-permute-start = (f32[7,128,128]{2,1,0:T(8,128)}, f32[7,128,128]{2,1,0:T(8,128)S(1)}, u32[]{:S(2)}, u32[]{:S(2)}) collective-permute-start(f32[7,128,128]{2,1,0:T(8,128)} %bitcast.6), channel_id=1, source_target_pairs={{0,1},{1,0},{2,3},{3,2},{4,5},{5,4},{6,7},{7,6},{8,9},{9,8},{10,11... | collective-permute-start | bytes 1376264 | tf_op jit(solution)/shard_map/ppermute | solution.py:19
  4.2 1.3 %copy-start.2 = (f32[7,128,128]{2,1,0:T(8,128)}, f32[7,128,128]{2,1,0:T(8,128)S(1)}, u32[]{:S(2)}) copy-start(f32[7,128,128]{2,1,0:T(8,128)S(1)} %collective-permute-done.lp.rp) | copy-start | bytes 1376260
  5.7 19.0 %collective-permute-start.1 = (f32[11,128,128]{2,1,0:T(8,128)S(1)}, f32[11,128,128]{2,1,0:T(8,128)S(1)}, u32[]{:S(2)}, u32[]{:S(2)}) collective-permute-start(f32[11,128,128]{2,1,0:T(8,128)S(1)} %maximum_select_fusion), channel_id=1, source_target_pairs={{0,1023},{1,2},{2,1},{3,4},{4,3},{5,6},{6,5},{7,8},{8,7},{9,10},{1... | collective-permute-start | bytes 2162696 | tf_op jit(solution)/shard_map/ppermute | solution.py:103
  9.7 21.7 %collective-permute-start.2 = (f32[7,128,128]{2,1,0:T(8,128)S(1)}, f32[7,128,128]{2,1,0:T(8,128)S(1)}, u32[]{:S(2)}, u32[]{:S(2)}) collective-permute-start(f32[7,128,128]{2,1,0:T(8,128)S(1)} %maximum_select_fusion.2), channel_id=1, source_target_pairs={{0,1021},{1,4},{2,1023},{3,6},{4,1},{5,8},{6,3},{7,10},{8,5},{9,12... | collective-permute-start | bytes 1376264 | tf_op jit(solution)/shard_map/ppermute | solution.py:103
  14.3 36.9 %copy-start.6 = (s32[1,12]{1,0:T(1,128)S(1)}, s32[1,12]{1,0:T(1,128)}, u32[]{:S(2)}) copy-start(s32[1,12]{1,0:T(1,128)} %param.3) | copy-start | bytes 148
  14.3 24.4 %collective-permute-start.3 = (f32[3,128,128]{2,1,0:T(8,128)S(1)}, f32[3,128,128]{2,1,0:T(8,128)S(1)}, u32[]{:S(2)}, u32[]{:S(2)}) collective-permute-start(f32[3,128,128]{2,1,0:T(8,128)S(1)} %maximum_select_fusion.4), channel_id=1, source_target_pairs={{0,1019},{1,6},{2,1021},{3,8},{4,1023},{5,10},{6,1},{7,12},{8,3},{... | collective-permute-start | bytes 589832 | tf_op jit(solution)/shard_map/ppermute | solution.py:103
  38.7 15.2 %copy-start = (f32[21,128,128]{2,1,0:T(8,128)}, f32[21,128,128]{2,1,0:T(8,128)S(1)}, u32[]{:S(2)}) copy-start(f32[21,128,128]{2,1,0:T(8,128)S(1)} %constant_dynamic-update-slice_fusion.lg.rg) | copy-start | bytes 4128772
  38.7 15.2 %collective-permute-start.4 = (f32[21,128,128]{2,1,0:T(8,128)S(1)}, f32[21,128,128]{2,1,0:T(8,128)S(1)}, u32[]{:S(2)}, u32[]{:S(2)}) collective-permute-start(f32[21,128,128]{2,1,0:T(8,128)S(1)} %constant_dynamic-update-slice_fusion.lg.rg), channel_id=1, source_target_pairs={{0,1},{1,0},{2,3},{3,2},{4,5},{5,4},{6,7},{7,6},{8,9},{9,8},{10,11... | collective-permute-start | bytes 4128776 | tf_op jit(solution)/shard_map/ppermute | solution.py:19
  53.9 1.1 copy-start.1
  64.0 3.9 %collective-permute-start.5 = (f32[7,128,128]{2,1,0:T(8,128)}, f32[7,128,128]{2,1,0:T(8,128)S(1)}, u32[]{:S(2)}, u32[]{:S(2)}) collective-permute-start(f32[7,128,128]{2,1,0:T(8,128)} %shard_map.28.rx), channel_id=1, source_target_pairs={{0,1},{1,0},{2,3},{3,2},{4,5},{5,4},{6,7},{7,6},{8,9},{9,8},{10,11... | collective-permute-start | bytes 1376264 | tf_op jit(solution)/shard_map/ppermute | solution.py:19
  68.0 1.3 %copy-start.4 = (f32[7,128,128]{2,1,0:T(8,128)}, f32[7,128,128]{2,1,0:T(8,128)S(1)}, u32[]{:S(2)}) copy-start(f32[7,128,128]{2,1,0:T(8,128)S(1)} %collective-permute-done.5.rp) | copy-start | bytes 1376260
  69.5 22.0 %collective-permute-start.6 = (f32[11,128,128]{2,1,0:T(8,128)S(1)}, f32[11,128,128]{2,1,0:T(8,128)S(1)}, u32[]{:S(2)}, u32[]{:S(2)}) collective-permute-start(f32[11,128,128]{2,1,0:T(8,128)S(1)} %maximum_select_fusion.1), channel_id=1, source_target_pairs={{0,1023},{1,2},{2,1},{3,4},{4,3},{5,6},{6,5},{7,8},{8,7},{9,10},{1... | collective-permute-start | bytes 2162696 | tf_op jit(solution)/shard_map/ppermute | solution.py:103
  71.7 19.8 %collective-permute-start.7 = (f32[7,128,128]{2,1,0:T(8,128)S(1)}, f32[7,128,128]{2,1,0:T(8,128)S(1)}, u32[]{:S(2)}, u32[]{:S(2)}) collective-permute-start(f32[7,128,128]{2,1,0:T(8,128)S(1)} %maximum_select_fusion.3), channel_id=1, source_target_pairs={{0,1021},{1,4},{2,1023},{3,6},{4,1},{5,8},{6,3},{7,10},{8,5},{9,12... | collective-permute-start | bytes 1376264 | tf_op jit(solution)/shard_map/ppermute | solution.py:103
  73.7 17.8 %collective-permute-start.8 = (f32[3,128,128]{2,1,0:T(8,128)S(1)}, f32[3,128,128]{2,1,0:T(8,128)S(1)}, u32[]{:S(2)}, u32[]{:S(2)}) collective-permute-start(f32[3,128,128]{2,1,0:T(8,128)S(1)} %maximum_select_fusion.5), channel_id=1, source_target_pairs={{0,1019},{1,6},{2,1021},{3,8},{4,1023},{5,10},{6,1},{7,12},{8,3},{... | collective-permute-start | bytes 589832 | tf_op jit(solution)/shard_map/ppermute | solution.py:103
  91.6 23.2 %copy-start.3 = (f32[21,128,128]{2,1,0:T(8,128)}, f32[21,128,128]{2,1,0:T(8,128)S(1)}, u32[]{:S(2)}) copy-start(f32[21,128,128]{2,1,0:T(8,128)S(1)} %constant_dynamic-update-slice_fusion.3.rg) | copy-start | bytes 4128772
  91.6 23.2 %collective-permute-start.9 = (f32[21,128,128]{2,1,0:T(8,128)S(1)}, f32[21,128,128]{2,1,0:T(8,128)S(1)}, u32[]{:S(2)}, u32[]{:S(2)}) collective-permute-start(f32[21,128,128]{2,1,0:T(8,128)S(1)} %constant_dynamic-update-slice_fusion.3.rg), channel_id=1, source_target_pairs={{0,1},{1,0},{2,3},{3,2},{4,5},{5,4},{6,7},{7,6},{8,9},{9,8},{10,11... | collective-permute-start | bytes 4128776 | tf_op jit(solution)/shard_map/ppermute | solution.py:19
  114.8 1.1 copy-start.5

commit v6 on v5

--- a/solution.py
+++ b/solution.py
@@ -44,28 +44,42 @@
     return partner, own, other, got
 
 
-def band_kernel(parity, flags, lx, lp, lg, lo, rx, rp, rg, ro, out, *, final):
+def split(x):
+    hi = x.astype(jnp.bfloat16)
+    lo = (x - hi.astype(jnp.float32)).astype(jnp.bfloat16)
+    return hi, lo
+
+
+def product(a_hi, a_lo, b, b_dim):
+    b_hi, b_lo = split(b)
+    dims = (((1,), (b_dim,)), ((), ()))
+
+    def dot(x, y):
+        return lax.dot_general(x, y, dims, preferred_element_type=jnp.float32)
+
+    return dot(a_hi, b_hi) + (dot(a_hi, b_lo) + dot(a_lo, b_hi))
+
+
+def band_kernel(parity, flags, lx, lp, lg, lo, rx, rp, rg, ro, out, left_hi, left_lo, *, final):
     def compute(k):
         left = chip_refs(k, lx, lp, lg, lo)
         right = chip_refs(k, rx, rp, rg, ro)
+        for inner in range(-REACH, REACH + 1):
+            if inner >= 0:
+                a = block_source(k, 0, inner, *left)
+            else:
+                a = block_source(k, inner, -inner, *left).T
+            a_hi, a_lo = split(a)
+            left_hi[inner + REACH] = a_hi
+            left_lo[inner + REACH] = a_lo
         for target in range(WIDTH):
             total = None
             for inner in range(target - REACH, REACH + 1):
-                if inner >= 0:
-                    a = block_source(k, 0, inner, *left)
-                else:
-                    a = block_source(k, inner, -inner, *left).T
                 if target >= inner:
                     b, b_dim = block_source(k, inner, target - inner, *right), 0
                 else:
                     b, b_dim = block_source(k, target, inner - target, *right), 1
-                term = lax.dot_general(
-                    a,
-                    b,
-                    (((1,), (b_dim,)), ((), ())),
-                    precision=lax.Precision.HIGHEST,
-                    preferred_element_type=jnp.float32,
-                )
+                term = product(left_hi[inner + REACH], left_lo[inner + REACH], b, b_dim)
                 total = term if total is None else total + term
             total = flags[target] * total
             if final:
@@ -80,11 +94,13 @@
     vmem = pl.BlockSpec(memory_space=pltpu.VMEM)
     smem = pl.BlockSpec(memory_space=pltpu.SMEM)
     local = left[0]
+    b = local.shape[-1]
     return pl.pallas_call(
         functools.partial(band_kernel, final=final),
         out_shape=jax.ShapeDtypeStruct(local.shape, jnp.float32),
         in_specs=[smem, smem] + [vmem] * 8,
         out_specs=vmem,
+        scratch_shapes=[pltpu.VMEM((2 * REACH + 1, b, b), jnp.bfloat16)] * 2,
         interpret=INTERPRET,
     )(parity, flags, *left, *right)
 

time: 125 us -> 121 us (0.968)
  Pallas kernels: 18.2 us -> 13.4 us
    pallas_call x2, Pallas kernels: 18.2 us -> 13.4 us  [band_product(): pl.pallas_call(functools.partial(band_kernel, final=final), out_shape=jax...]
where the time goes in v6:
time: 121 us; the launch traced here: 120 us
  starting transfers between devices  57.4 us (47%)
  waiting for transfers between devices  42.5 us (35%)
  Pallas kernels  13.4 us (11%)
  other arithmetic  3.58 us (3%)
  local copies, waits for them, and re-layouts  2.81 us (2%)
    ppermute x4, starting transfers between devices, swap_in_chip(): return lax.ppermute(x, AXES, [(i, i ^ 1) for i in range(n)])  37.6 us
    ppermute x6, waiting for transfers between devices, exchange_rows(): received.append(lax.ppermute(buf, AXES, route))  34.5 us
    ppermute x6, starting transfers between devices, exchange_rows(): received.append(lax.ppermute(buf, AXES, route))  19.8 us
    pallas_call x2, Pallas kernels, band_product(): pl.pallas_call(functools.partial(band_kernel, final=final), out_shape=jax...  13.4 us
    ppermute x4, waiting for transfers between devices, swap_in_chip(): return lax.ppermute(x, AXES, [(i, i ^ 1) for i in range(n)])  7.98 us
    select_n x2, other arithmetic, exchange_rows(): r1 = jnp.where(is_odd, x, partner)  2.52 us
  transfers between devices with their start and end apart: 10, of which 8 were waited for; matrix products, arithmetic and copies ran while one was open for 1% of the time, Pallas kernels for 0%

profile of v6, /device:TPU:65, one launch (start us, length us, event | category | flops | bytes accessed | tf_op | source)
XLA Modules:
  0.0 120.3 jit_solution(723752215784220241)
XLA Ops:
  0.0 2.6 %collective-permute-start = (f32[7,128,128]{2,1,0:T(8,128)}, f32[7,128,128]{2,1,0:T(8,128)S(1)}, u32[]{:S(2)}, u32[]{:S(2)}) collective-permute-start(f32[7,128,128]{2,1,0:T(8,128)} %bitcast.6), channel_id=1, source_target_pairs={{0,1},{1,0},{2,3},{3,2},{4,5},{5,4},{6,7},{7,6},{8,9},{9,8},{10,11... | collective-permute-start | bytes 1376264 | tf_op jit(solution)/shard_map/ppermute | solution.py:19
  2.6 1.6 %collective-permute-done.lp.rp = f32[7,128,128]{2,1,0:T(8,128)S(1)} collective-permute-done((f32[7,128,128]{2,1,0:T(8,128)}, f32[7,128,128]{2,1,0:T(8,128)S(1)}, u32[]{:S(2)}, u32[]{:S(2)}) %collective-permute-start) | collective-permute-done | bytes 458784 | tf_op jit(solution)/shard_map/ppermute | solution.py:19
  4.2 1.3 %broadcast_select_fusion.3 = (f32[7,128,128]{2,1,0:T(8,128)S(1)}, f32[7,128,128]{2,1,0:T(8,128)S(1)}) fusion(f32[7,128,128]{2,1,0:T(8,128)S(1)} %collective-permute-done.lp.rp, pred[]{:T(512)S(6)} %eq.27, f32[1,7,128,128]{3,2,1,0:T(8,128)} %param.2), kind=kLoop, calls=%fused_computation.7 | loop fusion | flops 229376 | bytes 1835009 | tf_op jit(solution)/shard_map/jit(_where)/select_n | solution.py:111
  5.7 3.8 %collective-permute-start.1 = (f32[11,128,128]{2,1,0:T(8,128)S(1)}, f32[11,128,128]{2,1,0:T(8,128)S(1)}, u32[]{:S(2)}, u32[]{:S(2)}) collective-permute-start(f32[11,128,128]{2,1,0:T(8,128)S(1)} %maximum_select_fusion), channel_id=1, source_target_pairs={{0,1023},{1,2},{2,1},{3,4},{4,3},{5,6},{6,5},{7,8},{8,7},{9,10},{1... | collective-permute-start | bytes 2162696 | tf_op jit(solution)/shard_map/ppermute | solution.py:119
  9.7 4.5 %collective-permute-start.2 = (f32[7,128,128]{2,1,0:T(8,128)S(1)}, f32[7,128,128]{2,1,0:T(8,128)S(1)}, u32[]{:S(2)}, u32[]{:S(2)}) collective-permute-start(f32[7,128,128]{2,1,0:T(8,128)S(1)} %maximum_select_fusion.2), channel_id=1, source_target_pairs={{0,1021},{1,4},{2,1023},{3,6},{4,1},{5,8},{6,3},{7,10},{8,5},{9,12... | collective-permute-start | bytes 1376264 | tf_op jit(solution)/shard_map/ppermute | solution.py:119
  14.3 5.8 %collective-permute-start.3 = (f32[3,128,128]{2,1,0:T(8,128)S(1)}, f32[3,128,128]{2,1,0:T(8,128)S(1)}, u32[]{:S(2)}, u32[]{:S(2)}) collective-permute-start(f32[3,128,128]{2,1,0:T(8,128)S(1)} %maximum_select_fusion.4), channel_id=1, source_target_pairs={{0,1019},{1,6},{2,1021},{3,8},{4,1023},{5,10},{6,1},{7,12},{8,3},{... | collective-permute-start | bytes 589832 | tf_op jit(solution)/shard_map/ppermute | solution.py:119
  20.0 4.7 %collective-permute-done.1 = f32[11,128,128]{2,1,0:T(8,128)S(1)} collective-permute-done((f32[11,128,128]{2,1,0:T(8,128)S(1)}, f32[11,128,128]{2,1,0:T(8,128)S(1)}, u32[]{:S(2)}, u32[]{:S(2)}) %collective-permute-start.1) | collective-permute-done | bytes 720928 | tf_op jit(solution)/shard_map/ppermute | solution.py:119
  24.8 6.5 %collective-permute-done.2 = f32[7,128,128]{2,1,0:T(8,128)S(1)} collective-permute-done((f32[7,128,128]{2,1,0:T(8,128)S(1)}, f32[7,128,128]{2,1,0:T(8,128)S(1)}, u32[]{:S(2)}, u32[]{:S(2)}) %collective-permute-start.2) | collective-permute-done | bytes 458784 | tf_op jit(solution)/shard_map/ppermute | solution.py:119
  31.4 7.3 %collective-permute-done.3 = f32[3,128,128]{2,1,0:T(8,128)S(1)} collective-permute-done((f32[3,128,128]{2,1,0:T(8,128)S(1)}, f32[3,128,128]{2,1,0:T(8,128)S(1)}, u32[]{:S(2)}, u32[]{:S(2)}) %collective-permute-start.3) | collective-permute-done | bytes 196640 | tf_op jit(solution)/shard_map/ppermute | solution.py:119
  38.7 12.4 %collective-permute-start.4 = (f32[21,128,128]{2,1,0:T(8,128)S(1)}, f32[21,128,128]{2,1,0:T(8,128)S(1)}, u32[]{:S(2)}, u32[]{:S(2)}) collective-permute-start(f32[21,128,128]{2,1,0:T(8,128)S(1)} %constant_dynamic-update-slice_fusion.lg.rg), channel_id=1, source_target_pairs={{0,1},{1,0},{2,3},{3,2},{4,5},{5,4},{6,7},{7,6},{8,9},{9,8},{10,11... | collective-permute-start | bytes 4128776 | tf_op jit(solution)/shard_map/ppermute | solution.py:19
  51.9 2.0 %collective-permute-done.4.lo.ro = f32[21,128,128]{2,1,0:T(8,128)S(1)} collective-permute-done((f32[21,128,128]{2,1,0:T(8,128)S(1)}, f32[21,128,128]{2,1,0:T(8,128)S(1)}, u32[]{:S(2)}, u32[]{:S(2)}) %collective-permute-start.4) | collective-permute-done | bytes 1376288 | tf_op jit(solution)/shard_map/ppermute | solution.py:19
  53.9 1.1 copy-done.1
  55.0 6.8 %shard_map.28.rx = f32[7,128,128]{2,1,0:T(8,128)} custom-call(s32[1]{0:T(128)} %bitcast.parity, f32[7]{0:T(128)} %convert_element_type.3.flags, f32[7,128,128]{2,1,0:T(8,128)} %bitcast.7, f32[7,128,128]{2,1,0:T(8,128)} %copy-done.2, f32[21,128,128]{2,1,0:T(8,128)} %copy-done, f32[21,128,128]{2,1,0:T(8,128)} %copy-done.1, f32[7,128,128]{2,1,0:T(8,128)} %bitcast.8, ...), custom_call_target="tpu_custom_call" | custom-call | tf_op jit(solution)/shard_map/pallas_call | solution.py:98
  61.7 2.2 %collective-permute-start.5 = (f32[7,128,128]{2,1,0:T(8,128)}, f32[7,128,128]{2,1,0:T(8,128)S(1)}, u32[]{:S(2)}, u32[]{:S(2)}) collective-permute-start(f32[7,128,128]{2,1,0:T(8,128)} %shard_map.28.rx), channel_id=1, source_target_pairs={{0,1},{1,0},{2,3},{3,2},{4,5},{5,4},{6,7},{7,6},{8,9},{9,8},{10,11... | collective-permute-start | bytes 1376264 | tf_op jit(solution)/shard_map/ppermute | solution.py:19
  64.0 1.7 %collective-permute-done.5.rp = f32[7,128,128]{2,1,0:T(8,128)S(1)} collective-permute-done((f32[7,128,128]{2,1,0:T(8,128)}, f32[7,128,128]{2,1,0:T(8,128)S(1)}, u32[]{:S(2)}, u32[]{:S(2)}) %collective-permute-start.5) | collective-permute-done | bytes 458784 | tf_op jit(solution)/shard_map/ppermute | solution.py:19
  65.6 1.3 %broadcast_select_fusion.1 = (f32[7,128,128]{2,1,0:T(8,128)S(1)}, f32[7,128,128]{2,1,0:T(8,128)S(1)}) fusion(f32[7,128,128]{2,1,0:T(8,128)} %shard_map.28.rx, f32[7,128,128]{2,1,0:T(8,128)S(1)} %collective-permute-done.5.rp, pred[]{:T(512)S(6)} %eq.27), kind=kLoop, calls=%fused_computation.5 | loop fusion | flops 229376 | bytes 1835009 | tf_op jit(solution)/shard_map/jit(_where)/select_n | solution.py:111
  67.1 1.9 %collective-permute-start.6 = (f32[11,128,128]{2,1,0:T(8,128)S(1)}, f32[11,128,128]{2,1,0:T(8,128)S(1)}, u32[]{:S(2)}, u32[]{:S(2)}) collective-permute-start(f32[11,128,128]{2,1,0:T(8,128)S(1)} %maximum_select_fusion.1), channel_id=1, source_target_pairs={{0,1023},{1,2},{2,1},{3,4},{4,3},{5,6},{6,5},{7,8},{8,7},{9,10},{1... | collective-permute-start | bytes 2162696 | tf_op jit(solution)/shard_map/ppermute | solution.py:119
  69.2 1.9 %collective-permute-start.7 = (f32[7,128,128]{2,1,0:T(8,128)S(1)}, f32[7,128,128]{2,1,0:T(8,128)S(1)}, u32[]{:S(2)}, u32[]{:S(2)}) collective-permute-start(f32[7,128,128]{2,1,0:T(8,128)S(1)} %maximum_select_fusion.3), channel_id=1, source_target_pairs={{0,1021},{1,4},{2,1023},{3,6},{4,1},{5,8},{6,3},{7,10},{8,5},{9,12... | collective-permute-start | bytes 1376264 | tf_op jit(solution)/shard_map/ppermute | solution.py:119
  71.2 1.9 %collective-permute-start.8 = (f32[3,128,128]{2,1,0:T(8,128)S(1)}, f32[3,128,128]{2,1,0:T(8,128)S(1)}, u32[]{:S(2)}, u32[]{:S(2)}) collective-permute-start(f32[3,128,128]{2,1,0:T(8,128)S(1)} %maximum_select_fusion.5), channel_id=1, source_target_pairs={{0,1019},{1,6},{2,1021},{3,8},{4,1023},{5,10},{6,1},{7,12},{8,3},{... | collective-permute-start | bytes 589832 | tf_op jit(solution)/shard_map/ppermute | solution.py:119
  73.2 16.0 %collective-permute-done.6 = f32[11,128,128]{2,1,0:T(8,128)S(1)} collective-permute-done((f32[11,128,128]{2,1,0:T(8,128)S(1)}, f32[11,128,128]{2,1,0:T(8,128)S(1)}, u32[]{:S(2)}, u32[]{:S(2)}) %collective-permute-start.6) | collective-permute-done | bytes 720928 | tf_op jit(solution)/shard_map/ppermute | solution.py:119
  89.3 20.4 %collective-permute-start.9 = (f32[21,128,128]{2,1,0:T(8,128)S(1)}, f32[21,128,128]{2,1,0:T(8,128)S(1)}, u32[]{:S(2)}, u32[]{:S(2)}) collective-permute-start(f32[21,128,128]{2,1,0:T(8,128)S(1)} %constant_dynamic-update-slice_fusion.3.rg), channel_id=1, source_target_pairs={{0,1},{1,0},{2,3},{3,2},{4,5},{5,4},{6,7},{7,6},{8,9},{9,8},{10,11... | collective-permute-start | bytes 4128776 | tf_op jit(solution)/shard_map/ppermute | solution.py:19
  109.7 2.7 %collective-permute-done.9.ro = f32[21,128,128]{2,1,0:T(8,128)S(1)} collective-permute-done((f32[21,128,128]{2,1,0:T(8,128)S(1)}, f32[21,128,128]{2,1,0:T(8,128)S(1)}, u32[]{:S(2)}, u32[]{:S(2)}) %collective-permute-start.9) | collective-permute-done | bytes 1376288 | tf_op jit(solution)/shard_map/ppermute | solution.py:19
  112.5 1.1 copy-done.5
  113.6 6.7 %shard_map.29 = f32[7,128,128]{2,1,0:T(8,128)} custom-call(s32[1]{0:T(128)} %bitcast.parity, f32[7]{0:T(128)} %convert_element_type.3.flags, f32[7,128,128]{2,1,0:T(8,128)} %bitcast.9, f32[7,128,128]{2,1,0:T(8,128)} %copy-done.2, f32[21,128,128]{2,1,0:T(8,128)} %copy-done, f32[21,128,128]{2,1,0:T(8,128)} %copy-done.1, f32[7,128,128]{2,1,0:T(8,128)} %shard_map.28.rx, ...), custom_call_target="tpu_custom_call" | custom-call | tf_op jit(solution)/shard_map/pallas_call | solution.py:98
  (53 shorter events, 1.7 us)
Async XLA Ops:
  0.0 4.2 %collective-permute-start = (f32[7,128,128]{2,1,0:T(8,128)}, f32[7,128,128]{2,1,0:T(8,128)S(1)}, u32[]{:S(2)}, u32[]{:S(2)}) collective-permute-start(f32[7,128,128]{2,1,0:T(8,128)} %bitcast.6), channel_id=1, source_target_pairs={{0,1},{1,0},{2,3},{3,2},{4,5},{5,4},{6,7},{7,6},{8,9},{9,8},{10,11... | collective-permute-start | bytes 1376264 | tf_op jit(solution)/shard_map/ppermute | solution.py:19
  4.2 1.3 %copy-start.2 = (f32[7,128,128]{2,1,0:T(8,128)}, f32[7,128,128]{2,1,0:T(8,128)S(1)}, u32[]{:S(2)}) copy-start(f32[7,128,128]{2,1,0:T(8,128)S(1)} %collective-permute-done.lp.rp) | copy-start | bytes 1376260
  5.7 19.0 %collective-permute-start.1 = (f32[11,128,128]{2,1,0:T(8,128)S(1)}, f32[11,128,128]{2,1,0:T(8,128)S(1)}, u32[]{:S(2)}, u32[]{:S(2)}) collective-permute-start(f32[11,128,128]{2,1,0:T(8,128)S(1)} %maximum_select_fusion), channel_id=1, source_target_pairs={{0,1023},{1,2},{2,1},{3,4},{4,3},{5,6},{6,5},{7,8},{8,7},{9,10},{1... | collective-permute-start | bytes 2162696 | tf_op jit(solution)/shard_map/ppermute | solution.py:119
  9.7 21.7 %collective-permute-start.2 = (f32[7,128,128]{2,1,0:T(8,128)S(1)}, f32[7,128,128]{2,1,0:T(8,128)S(1)}, u32[]{:S(2)}, u32[]{:S(2)}) collective-permute-start(f32[7,128,128]{2,1,0:T(8,128)S(1)} %maximum_select_fusion.2), channel_id=1, source_target_pairs={{0,1021},{1,4},{2,1023},{3,6},{4,1},{5,8},{6,3},{7,10},{8,5},{9,12... | collective-permute-start | bytes 1376264 | tf_op jit(solution)/shard_map/ppermute | solution.py:119
  14.3 36.9 %copy-start.6 = (s32[1,12]{1,0:T(1,128)S(1)}, s32[1,12]{1,0:T(1,128)}, u32[]{:S(2)}) copy-start(s32[1,12]{1,0:T(1,128)} %param.3) | copy-start | bytes 148
  14.3 24.4 %collective-permute-start.3 = (f32[3,128,128]{2,1,0:T(8,128)S(1)}, f32[3,128,128]{2,1,0:T(8,128)S(1)}, u32[]{:S(2)}, u32[]{:S(2)}) collective-permute-start(f32[3,128,128]{2,1,0:T(8,128)S(1)} %maximum_select_fusion.4), channel_id=1, source_target_pairs={{0,1019},{1,6},{2,1021},{3,8},{4,1023},{5,10},{6,1},{7,12},{8,3},{... | collective-permute-start | bytes 589832 | tf_op jit(solution)/shard_map/ppermute | solution.py:119
  38.7 15.2 %copy-start = (f32[21,128,128]{2,1,0:T(8,128)}, f32[21,128,128]{2,1,0:T(8,128)S(1)}, u32[]{:S(2)}) copy-start(f32[21,128,128]{2,1,0:T(8,128)S(1)} %constant_dynamic-update-slice_fusion.lg.rg) | copy-start | bytes 4128772
  38.7 15.2 %collective-permute-start.4 = (f32[21,128,128]{2,1,0:T(8,128)S(1)}, f32[21,128,128]{2,1,0:T(8,128)S(1)}, u32[]{:S(2)}, u32[]{:S(2)}) collective-permute-start(f32[21,128,128]{2,1,0:T(8,128)S(1)} %constant_dynamic-update-slice_fusion.lg.rg), channel_id=1, source_target_pairs={{0,1},{1,0},{2,3},{3,2},{4,5},{5,4},{6,7},{7,6},{8,9},{9,8},{10,11... | collective-permute-start | bytes 4128776 | tf_op jit(solution)/shard_map/ppermute | solution.py:19
  53.9 1.1 copy-start.1
  61.7 3.9 %collective-permute-start.5 = (f32[7,128,128]{2,1,0:T(8,128)}, f32[7,128,128]{2,1,0:T(8,128)S(1)}, u32[]{:S(2)}, u32[]{:S(2)}) collective-permute-start(f32[7,128,128]{2,1,0:T(8,128)} %shard_map.28.rx), channel_id=1, source_target_pairs={{0,1},{1,0},{2,3},{3,2},{4,5},{5,4},{6,7},{7,6},{8,9},{9,8},{10,11... | collective-permute-start | bytes 1376264 | tf_op jit(solution)/shard_map/ppermute | solution.py:19
  65.6 1.3 %copy-start.4 = (f32[7,128,128]{2,1,0:T(8,128)}, f32[7,128,128]{2,1,0:T(8,128)S(1)}, u32[]{:S(2)}) copy-start(f32[7,128,128]{2,1,0:T(8,128)S(1)} %collective-permute-done.5.rp) | copy-start | bytes 1376260
  67.1 22.0 %collective-permute-start.6 = (f32[11,128,128]{2,1,0:T(8,128)S(1)}, f32[11,128,128]{2,1,0:T(8,128)S(1)}, u32[]{:S(2)}, u32[]{:S(2)}) collective-permute-start(f32[11,128,128]{2,1,0:T(8,128)S(1)} %maximum_select_fusion.1), channel_id=1, source_target_pairs={{0,1023},{1,2},{2,1},{3,4},{4,3},{5,6},{6,5},{7,8},{8,7},{9,10},{1... | collective-permute-start | bytes 2162696 | tf_op jit(solution)/shard_map/ppermute | solution.py:119
  69.2 20.0 %collective-permute-start.7 = (f32[7,128,128]{2,1,0:T(8,128)S(1)}, f32[7,128,128]{2,1,0:T(8,128)S(1)}, u32[]{:S(2)}, u32[]{:S(2)}) collective-permute-start(f32[7,128,128]{2,1,0:T(8,128)S(1)} %maximum_select_fusion.3), channel_id=1, source_target_pairs={{0,1021},{1,4},{2,1023},{3,6},{4,1},{5,8},{6,3},{7,10},{8,5},{9,12... | collective-permute-start | bytes 1376264 | tf_op jit(solution)/shard_map/ppermute | solution.py:119
  71.2 18.0 %collective-permute-start.8 = (f32[3,128,128]{2,1,0:T(8,128)S(1)}, f32[3,128,128]{2,1,0:T(8,128)S(1)}, u32[]{:S(2)}, u32[]{:S(2)}) collective-permute-start(f32[3,128,128]{2,1,0:T(8,128)S(1)} %maximum_select_fusion.5), channel_id=1, source_target_pairs={{0,1019},{1,6},{2,1021},{3,8},{4,1023},{5,10},{6,1},{7,12},{8,3},{... | collective-permute-start | bytes 589832 | tf_op jit(solution)/shard_map/ppermute | solution.py:119
  89.3 23.2 %copy-start.3 = (f32[21,128,128]{2,1,0:T(8,128)}, f32[21,128,128]{2,1,0:T(8,128)S(1)}, u32[]{:S(2)}) copy-start(f32[21,128,128]{2,1,0:T(8,128)S(1)} %constant_dynamic-update-slice_fusion.3.rg) | copy-start | bytes 4128772
  89.3 23.2 %collective-permute-start.9 = (f32[21,128,128]{2,1,0:T(8,128)S(1)}, f32[21,128,128]{2,1,0:T(8,128)S(1)}, u32[]{:S(2)}, u32[]{:S(2)}) collective-permute-start(f32[21,128,128]{2,1,0:T(8,128)S(1)} %constant_dynamic-update-slice_fusion.3.rg), channel_id=1, source_target_pairs={{0,1},{1,0},{2,3},{3,2},{4,5},{5,4},{6,7},{7,6},{8,9},{9,8},{10,11... | collective-permute-start | bytes 4128776 | tf_op jit(solution)/shard_map/ppermute | solution.py:19
  112.4 1.1 copy-start.5

commit v7 on v6

--- a/solution.py
+++ b/solution.py
@@ -50,17 +50,9 @@
     return hi, lo
 
 
-def product(a_hi, a_lo, b, b_dim):
-    b_hi, b_lo = split(b)
-    dims = (((1,), (b_dim,)), ((), ()))
+def band_kernel(parity, flags, lx, lp, lg, lo, rx, rp, rg, ro, out, left_all, right_all, *, final):
+    b = out.shape[-1]
 
-    def dot(x, y):
-        return lax.dot_general(x, y, dims, preferred_element_type=jnp.float32)
-
-    return dot(a_hi, b_hi) + (dot(a_hi, b_lo) + dot(a_lo, b_hi))
-
-
-def band_kernel(parity, flags, lx, lp, lg, lo, rx, rp, rg, ro, out, left_hi, left_lo, *, final):
     def compute(k):
         left = chip_refs(k, lx, lp, lg, lo)
         right = chip_refs(k, rx, rp, rg, ro)
@@ -70,17 +62,27 @@
             else:
                 a = block_source(k, inner, -inner, *left).T
             a_hi, a_lo = split(a)
-            left_hi[inner + REACH] = a_hi
-            left_lo[inner + REACH] = a_lo
+            i = 3 * (inner + REACH)
+            left_all[:, i * b:(i + 1) * b] = a_hi
+            left_all[:, (i + 1) * b:(i + 2) * b] = a_hi
+            left_all[:, (i + 2) * b:(i + 3) * b] = a_lo
         for target in range(WIDTH):
-            total = None
-            for inner in range(target - REACH, REACH + 1):
+            rows = right_all.at[target % 2]
+            for j, inner in enumerate(range(target - REACH, REACH + 1)):
                 if target >= inner:
-                    b, b_dim = block_source(k, inner, target - inner, *right), 0
+                    m = block_source(k, inner, target - inner, *right)
                 else:
-                    b, b_dim = block_source(k, target, inner - target, *right), 1
-                term = product(left_hi[inner + REACH], left_lo[inner + REACH], b, b_dim)
-                total = term if total is None else total + term
+                    m = block_source(k, target, inner - target, *right).T
+                m_hi, m_lo = split(m)
+                rows[3 * j * b:(3 * j + 1) * b, :] = m_hi
+                rows[(3 * j + 1) * b:(3 * j + 2) * b, :] = m_lo
+                rows[(3 * j + 2) * b:(3 * j + 3) * b, :] = m_hi
+            depth = 3 * (2 * REACH + 1 - target) * b
+            total = jnp.dot(
+                left_all[:, 3 * target * b:],
+                rows[:depth, :],
+                preferred_element_type=jnp.float32,
+            )
             total = flags[target] * total
             if final:
                 total = 3.0 * rx[target] - 2.0 * total
@@ -95,12 +97,16 @@
     smem = pl.BlockSpec(memory_space=pltpu.SMEM)
     local = left[0]
     b = local.shape[-1]
+    depth = 3 * (2 * REACH + 1) * b
     return pl.pallas_call(
         functools.partial(band_kernel, final=final),
         out_shape=jax.ShapeDtypeStruct(local.shape, jnp.float32),
         in_specs=[smem, smem] + [vmem] * 8,
         out_specs=vmem,
-        scratch_shapes=[pltpu.VMEM((2 * REACH + 1, b, b), jnp.bfloat16)] * 2,
+        scratch_shapes=[
+            pltpu.VMEM((b, depth), jnp.bfloat16),
+            pltpu.VMEM((2, depth, b), jnp.bfloat16),
+        ],
         interpret=INTERPRET,
     )(parity, flags, *left, *right)
 

time: 121 us -> 120 us (level)
  no operation moved by 1% of the time
where the time goes in v7:
time: 120 us; the launch traced here: 119 us
  starting transfers between devices  57.5 us (48%)
  waiting for transfers between devices  42.5 us (35%)
  Pallas kernels  12.3 us (10%)
  other arithmetic  3.58 us (3%)
  local copies, waits for them, and re-layouts  2.81 us (2%)
    ppermute x4, starting transfers between devices, swap_in_chip(): return lax.ppermute(x, AXES, [(i, i ^ 1) for i in range(n)])  37.7 us
    ppermute x6, waiting for transfers between devices, exchange_rows(): received.append(lax.ppermute(buf, AXES, route))  34.5 us
    ppermute x6, starting transfers between devices, exchange_rows(): received.append(lax.ppermute(buf, AXES, route))  19.8 us
    pallas_call x2, Pallas kernels, band_product(): pl.pallas_call(functools.partial(band_kernel, final=final), out_shape=jax...  12.3 us
    ppermute x4, waiting for transfers between devices, swap_in_chip(): return lax.ppermute(x, AXES, [(i, i ^ 1) for i in range(n)])  7.96 us
    select_n x2, other arithmetic, exchange_rows(): r1 = jnp.where(is_odd, x, partner)  2.52 us
  transfers between devices with their start and end apart: 10, of which 8 were waited for; matrix products, arithmetic and copies ran while one was open for 1% of the time, Pallas kernels for 0%

profile of v7, /device:TPU:65, one launch (start us, length us, event | category | flops | bytes accessed | tf_op | source)
XLA Modules:
  0.0 119.1 jit_solution(141991518212468679)
XLA Ops:
  0.0 2.6 %collective-permute-start = (f32[7,128,128]{2,1,0:T(8,128)}, f32[7,128,128]{2,1,0:T(8,128)S(1)}, u32[]{:S(2)}, u32[]{:S(2)}) collective-permute-start(f32[7,128,128]{2,1,0:T(8,128)} %bitcast.6), channel_id=1, source_target_pairs={{0,1},{1,0},{2,3},{3,2},{4,5},{5,4},{6,7},{7,6},{8,9},{9,8},{10,11... | collective-permute-start | bytes 1376264 | tf_op jit(solution)/shard_map/ppermute | solution.py:19
  2.6 1.6 %collective-permute-done.lp.rp = f32[7,128,128]{2,1,0:T(8,128)S(1)} collective-permute-done((f32[7,128,128]{2,1,0:T(8,128)}, f32[7,128,128]{2,1,0:T(8,128)S(1)}, u32[]{:S(2)}, u32[]{:S(2)}) %collective-permute-start) | collective-permute-done | bytes 458784 | tf_op jit(solution)/shard_map/ppermute | solution.py:19
  4.2 1.3 %broadcast_select_fusion.3 = (f32[7,128,128]{2,1,0:T(8,128)S(1)}, f32[7,128,128]{2,1,0:T(8,128)S(1)}) fusion(f32[7,128,128]{2,1,0:T(8,128)S(1)} %collective-permute-done.lp.rp, pred[]{:T(512)S(6)} %eq.27, f32[1,7,128,128]{3,2,1,0:T(8,128)} %param.2), kind=kLoop, calls=%fused_computation.7 | loop fusion | flops 229376 | bytes 1835009 | tf_op jit(solution)/shard_map/jit(_where)/select_n | solution.py:117
  5.7 3.8 %collective-permute-start.1 = (f32[11,128,128]{2,1,0:T(8,128)S(1)}, f32[11,128,128]{2,1,0:T(8,128)S(1)}, u32[]{:S(2)}, u32[]{:S(2)}) collective-permute-start(f32[11,128,128]{2,1,0:T(8,128)S(1)} %maximum_select_fusion), channel_id=1, source_target_pairs={{0,1023},{1,2},{2,1},{3,4},{4,3},{5,6},{6,5},{7,8},{8,7},{9,10},{1... | collective-permute-start | bytes 2162696 | tf_op jit(solution)/shard_map/ppermute | solution.py:125
  9.7 4.5 %collective-permute-start.2 = (f32[7,128,128]{2,1,0:T(8,128)S(1)}, f32[7,128,128]{2,1,0:T(8,128)S(1)}, u32[]{:S(2)}, u32[]{:S(2)}) collective-permute-start(f32[7,128,128]{2,1,0:T(8,128)S(1)} %maximum_select_fusion.2), channel_id=1, source_target_pairs={{0,1021},{1,4},{2,1023},{3,6},{4,1},{5,8},{6,3},{7,10},{8,5},{9,12... | collective-permute-start | bytes 1376264 | tf_op jit(solution)/shard_map/ppermute | solution.py:125
  14.3 5.8 %collective-permute-start.3 = (f32[3,128,128]{2,1,0:T(8,128)S(1)}, f32[3,128,128]{2,1,0:T(8,128)S(1)}, u32[]{:S(2)}, u32[]{:S(2)}) collective-permute-start(f32[3,128,128]{2,1,0:T(8,128)S(1)} %maximum_select_fusion.4), channel_id=1, source_target_pairs={{0,1019},{1,6},{2,1021},{3,8},{4,1023},{5,10},{6,1},{7,12},{8,3},{... | collective-permute-start | bytes 589832 | tf_op jit(solution)/shard_map/ppermute | solution.py:125
  20.0 4.7 %collective-permute-done.1 = f32[11,128,128]{2,1,0:T(8,128)S(1)} collective-permute-done((f32[11,128,128]{2,1,0:T(8,128)S(1)}, f32[11,128,128]{2,1,0:T(8,128)S(1)}, u32[]{:S(2)}, u32[]{:S(2)}) %collective-permute-start.1) | collective-permute-done | bytes 720928 | tf_op jit(solution)/shard_map/ppermute | solution.py:125
  24.8 6.5 %collective-permute-done.2 = f32[7,128,128]{2,1,0:T(8,128)S(1)} collective-permute-done((f32[7,128,128]{2,1,0:T(8,128)S(1)}, f32[7,128,128]{2,1,0:T(8,128)S(1)}, u32[]{:S(2)}, u32[]{:S(2)}) %collective-permute-start.2) | collective-permute-done | bytes 458784 | tf_op jit(solution)/shard_map/ppermute | solution.py:125
  31.4 7.3 %collective-permute-done.3 = f32[3,128,128]{2,1,0:T(8,128)S(1)} collective-permute-done((f32[3,128,128]{2,1,0:T(8,128)S(1)}, f32[3,128,128]{2,1,0:T(8,128)S(1)}, u32[]{:S(2)}, u32[]{:S(2)}) %collective-permute-start.3) | collective-permute-done | bytes 196640 | tf_op jit(solution)/shard_map/ppermute | solution.py:125
  38.7 12.4 %collective-permute-start.4 = (f32[21,128,128]{2,1,0:T(8,128)S(1)}, f32[21,128,128]{2,1,0:T(8,128)S(1)}, u32[]{:S(2)}, u32[]{:S(2)}) collective-permute-start(f32[21,128,128]{2,1,0:T(8,128)S(1)} %constant_dynamic-update-slice_fusion.lg.rg), channel_id=1, source_target_pairs={{0,1},{1,0},{2,3},{3,2},{4,5},{5,4},{6,7},{7,6},{8,9},{9,8},{10,11... | collective-permute-start | bytes 4128776 | tf_op jit(solution)/shard_map/ppermute | solution.py:19
  51.9 2.0 %collective-permute-done.4.lo.ro = f32[21,128,128]{2,1,0:T(8,128)S(1)} collective-permute-done((f32[21,128,128]{2,1,0:T(8,128)S(1)}, f32[21,128,128]{2,1,0:T(8,128)S(1)}, u32[]{:S(2)}, u32[]{:S(2)}) %collective-permute-start.4) | collective-permute-done | bytes 1376288 | tf_op jit(solution)/shard_map/ppermute | solution.py:19
  53.9 1.1 copy-done.1
  55.0 6.2 %shard_map.28.rx = f32[7,128,128]{2,1,0:T(8,128)} custom-call(s32[1]{0:T(128)} %bitcast.parity, f32[7]{0:T(128)} %convert_element_type.3.flags, f32[7,128,128]{2,1,0:T(8,128)} %bitcast.7, f32[7,128,128]{2,1,0:T(8,128)} %copy-done.2, f32[21,128,128]{2,1,0:T(8,128)} %copy-done, f32[21,128,128]{2,1,0:T(8,128)} %copy-done.1, f32[7,128,128]{2,1,0:T(8,128)} %bitcast.8, ...), custom_call_target="tpu_custom_call" | custom-call | tf_op jit(solution)/shard_map/pallas_call | solution.py:101
  61.1 2.3 %collective-permute-start.5 = (f32[7,128,128]{2,1,0:T(8,128)}, f32[7,128,128]{2,1,0:T(8,128)S(1)}, u32[]{:S(2)}, u32[]{:S(2)}) collective-permute-start(f32[7,128,128]{2,1,0:T(8,128)} %shard_map.28.rx), channel_id=1, source_target_pairs={{0,1},{1,0},{2,3},{3,2},{4,5},{5,4},{6,7},{7,6},{8,9},{9,8},{10,11... | collective-permute-start | bytes 1376264 | tf_op jit(solution)/shard_map/ppermute | solution.py:19
  63.4 1.6 %collective-permute-done.5.rp = f32[7,128,128]{2,1,0:T(8,128)S(1)} collective-permute-done((f32[7,128,128]{2,1,0:T(8,128)}, f32[7,128,128]{2,1,0:T(8,128)S(1)}, u32[]{:S(2)}, u32[]{:S(2)}) %collective-permute-start.5) | collective-permute-done | bytes 458784 | tf_op jit(solution)/shard_map/ppermute | solution.py:19
  65.0 1.3 %broadcast_select_fusion.1 = (f32[7,128,128]{2,1,0:T(8,128)S(1)}, f32[7,128,128]{2,1,0:T(8,128)S(1)}) fusion(f32[7,128,128]{2,1,0:T(8,128)} %shard_map.28.rx, f32[7,128,128]{2,1,0:T(8,128)S(1)} %collective-permute-done.5.rp, pred[]{:T(512)S(6)} %eq.27), kind=kLoop, calls=%fused_computation.5 | loop fusion | flops 229376 | bytes 1835009 | tf_op jit(solution)/shard_map/jit(_where)/select_n | solution.py:117
  66.5 1.9 %collective-permute-start.6 = (f32[11,128,128]{2,1,0:T(8,128)S(1)}, f32[11,128,128]{2,1,0:T(8,128)S(1)}, u32[]{:S(2)}, u32[]{:S(2)}) collective-permute-start(f32[11,128,128]{2,1,0:T(8,128)S(1)} %maximum_select_fusion.1), channel_id=1, source_target_pairs={{0,1023},{1,2},{2,1},{3,4},{4,3},{5,6},{6,5},{7,8},{8,7},{9,10},{1... | collective-permute-start | bytes 2162696 | tf_op jit(solution)/shard_map/ppermute | solution.py:125
  68.6 1.9 %collective-permute-start.7 = (f32[7,128,128]{2,1,0:T(8,128)S(1)}, f32[7,128,128]{2,1,0:T(8,128)S(1)}, u32[]{:S(2)}, u32[]{:S(2)}) collective-permute-start(f32[7,128,128]{2,1,0:T(8,128)S(1)} %maximum_select_fusion.3), channel_id=1, source_target_pairs={{0,1021},{1,4},{2,1023},{3,6},{4,1},{5,8},{6,3},{7,10},{8,5},{9,12... | collective-permute-start | bytes 1376264 | tf_op jit(solution)/shard_map/ppermute | solution.py:125
  70.6 1.9 %collective-permute-start.8 = (f32[3,128,128]{2,1,0:T(8,128)S(1)}, f32[3,128,128]{2,1,0:T(8,128)S(1)}, u32[]{:S(2)}, u32[]{:S(2)}) collective-permute-start(f32[3,128,128]{2,1,0:T(8,128)S(1)} %maximum_select_fusion.5), channel_id=1, source_target_pairs={{0,1019},{1,6},{2,1021},{3,8},{4,1023},{5,10},{6,1},{7,12},{8,3},{... | collective-permute-start | bytes 589832 | tf_op jit(solution)/shard_map/ppermute | solution.py:125
  72.6 16.0 %collective-permute-done.6 = f32[11,128,128]{2,1,0:T(8,128)S(1)} collective-permute-done((f32[11,128,128]{2,1,0:T(8,128)S(1)}, f32[11,128,128]{2,1,0:T(8,128)S(1)}, u32[]{:S(2)}, u32[]{:S(2)}) %collective-permute-start.6) | collective-permute-done | bytes 720928 | tf_op jit(solution)/shard_map/ppermute | solution.py:125
  88.7 20.4 %collective-permute-start.9 = (f32[21,128,128]{2,1,0:T(8,128)S(1)}, f32[21,128,128]{2,1,0:T(8,128)S(1)}, u32[]{:S(2)}, u32[]{:S(2)}) collective-permute-start(f32[21,128,128]{2,1,0:T(8,128)S(1)} %constant_dynamic-update-slice_fusion.3.rg), channel_id=1, source_target_pairs={{0,1},{1,0},{2,3},{3,2},{4,5},{5,4},{6,7},{7,6},{8,9},{9,8},{10,11... | collective-permute-start | bytes 4128776 | tf_op jit(solution)/shard_map/ppermute | solution.py:19
  109.1 2.7 %collective-permute-done.9.ro = f32[21,128,128]{2,1,0:T(8,128)S(1)} collective-permute-done((f32[21,128,128]{2,1,0:T(8,128)S(1)}, f32[21,128,128]{2,1,0:T(8,128)S(1)}, u32[]{:S(2)}, u32[]{:S(2)}) %collective-permute-start.9) | collective-permute-done | bytes 1376288 | tf_op jit(solution)/shard_map/ppermute | solution.py:19
  111.9 1.1 copy-done.5
  113.0 6.1 %shard_map.29 = f32[7,128,128]{2,1,0:T(8,128)} custom-call(s32[1]{0:T(128)} %bitcast.parity, f32[7]{0:T(128)} %convert_element_type.3.flags, f32[7,128,128]{2,1,0:T(8,128)} %bitcast.9, f32[7,128,128]{2,1,0:T(8,128)} %copy-done.2, f32[21,128,128]{2,1,0:T(8,128)} %copy-done, f32[21,128,128]{2,1,0:T(8,128)} %copy-done.1, f32[7,128,128]{2,1,0:T(8,128)} %shard_map.28.rx, ...), custom_call_target="tpu_custom_call" | custom-call | tf_op jit(solution)/shard_map/pallas_call | solution.py:101
  (53 shorter events, 1.7 us)
Async XLA Ops:
  0.0 4.2 %collective-permute-start = (f32[7,128,128]{2,1,0:T(8,128)}, f32[7,128,128]{2,1,0:T(8,128)S(1)}, u32[]{:S(2)}, u32[]{:S(2)}) collective-permute-start(f32[7,128,128]{2,1,0:T(8,128)} %bitcast.6), channel_id=1, source_target_pairs={{0,1},{1,0},{2,3},{3,2},{4,5},{5,4},{6,7},{7,6},{8,9},{9,8},{10,11... | collective-permute-start | bytes 1376264 | tf_op jit(solution)/shard_map/ppermute | solution.py:19
  4.2 1.3 %copy-start.2 = (f32[7,128,128]{2,1,0:T(8,128)}, f32[7,128,128]{2,1,0:T(8,128)S(1)}, u32[]{:S(2)}) copy-start(f32[7,128,128]{2,1,0:T(8,128)S(1)} %collective-permute-done.lp.rp) | copy-start | bytes 1376260
  5.7 19.0 %collective-permute-start.1 = (f32[11,128,128]{2,1,0:T(8,128)S(1)}, f32[11,128,128]{2,1,0:T(8,128)S(1)}, u32[]{:S(2)}, u32[]{:S(2)}) collective-permute-start(f32[11,128,128]{2,1,0:T(8,128)S(1)} %maximum_select_fusion), channel_id=1, source_target_pairs={{0,1023},{1,2},{2,1},{3,4},{4,3},{5,6},{6,5},{7,8},{8,7},{9,10},{1... | collective-permute-start | bytes 2162696 | tf_op jit(solution)/shard_map/ppermute | solution.py:125
  9.7 21.7 %collective-permute-start.2 = (f32[7,128,128]{2,1,0:T(8,128)S(1)}, f32[7,128,128]{2,1,0:T(8,128)S(1)}, u32[]{:S(2)}, u32[]{:S(2)}) collective-permute-start(f32[7,128,128]{2,1,0:T(8,128)S(1)} %maximum_select_fusion.2), channel_id=1, source_target_pairs={{0,1021},{1,4},{2,1023},{3,6},{4,1},{5,8},{6,3},{7,10},{8,5},{9,12... | collective-permute-start | bytes 1376264 | tf_op jit(solution)/shard_map/ppermute | solution.py:125
  14.3 36.9 %copy-start.6 = (s32[1,12]{1,0:T(1,128)S(1)}, s32[1,12]{1,0:T(1,128)}, u32[]{:S(2)}) copy-start(s32[1,12]{1,0:T(1,128)} %param.3) | copy-start | bytes 148
  14.3 24.4 %collective-permute-start.3 = (f32[3,128,128]{2,1,0:T(8,128)S(1)}, f32[3,128,128]{2,1,0:T(8,128)S(1)}, u32[]{:S(2)}, u32[]{:S(2)}) collective-permute-start(f32[3,128,128]{2,1,0:T(8,128)S(1)} %maximum_select_fusion.4), channel_id=1, source_target_pairs={{0,1019},{1,6},{2,1021},{3,8},{4,1023},{5,10},{6,1},{7,12},{8,3},{... | collective-permute-start | bytes 589832 | tf_op jit(solution)/shard_map/ppermute | solution.py:125
  38.7 15.2 %copy-start = (f32[21,128,128]{2,1,0:T(8,128)}, f32[21,128,128]{2,1,0:T(8,128)S(1)}, u32[]{:S(2)}) copy-start(f32[21,128,128]{2,1,0:T(8,128)S(1)} %constant_dynamic-update-slice_fusion.lg.rg) | copy-start | bytes 4128772
  38.7 15.2 %collective-permute-start.4 = (f32[21,128,128]{2,1,0:T(8,128)S(1)}, f32[21,128,128]{2,1,0:T(8,128)S(1)}, u32[]{:S(2)}, u32[]{:S(2)}) collective-permute-start(f32[21,128,128]{2,1,0:T(8,128)S(1)} %constant_dynamic-update-slice_fusion.lg.rg), channel_id=1, source_target_pairs={{0,1},{1,0},{2,3},{3,2},{4,5},{5,4},{6,7},{7,6},{8,9},{9,8},{10,11... | collective-permute-start | bytes 4128776 | tf_op jit(solution)/shard_map/ppermute | solution.py:19
  53.9 1.1 copy-start.1
  61.1 3.9 %collective-permute-start.5 = (f32[7,128,128]{2,1,0:T(8,128)}, f32[7,128,128]{2,1,0:T(8,128)S(1)}, u32[]{:S(2)}, u32[]{:S(2)}) collective-permute-start(f32[7,128,128]{2,1,0:T(8,128)} %shard_map.28.rx), channel_id=1, source_target_pairs={{0,1},{1,0},{2,3},{3,2},{4,5},{5,4},{6,7},{7,6},{8,9},{9,8},{10,11... | collective-permute-start | bytes 1376264 | tf_op jit(solution)/shard_map/ppermute | solution.py:19
  65.0 1.3 %copy-start.4 = (f32[7,128,128]{2,1,0:T(8,128)}, f32[7,128,128]{2,1,0:T(8,128)S(1)}, u32[]{:S(2)}) copy-start(f32[7,128,128]{2,1,0:T(8,128)S(1)} %collective-permute-done.5.rp) | copy-start | bytes 1376260
  66.5 22.0 %collective-permute-start.6 = (f32[11,128,128]{2,1,0:T(8,128)S(1)}, f32[11,128,128]{2,1,0:T(8,128)S(1)}, u32[]{:S(2)}, u32[]{:S(2)}) collective-permute-start(f32[11,128,128]{2,1,0:T(8,128)S(1)} %maximum_select_fusion.1), channel_id=1, source_target_pairs={{0,1023},{1,2},{2,1},{3,4},{4,3},{5,6},{6,5},{7,8},{8,7},{9,10},{1... | collective-permute-start | bytes 2162696 | tf_op jit(solution)/shard_map/ppermute | solution.py:125
  68.6 20.0 %collective-permute-start.7 = (f32[7,128,128]{2,1,0:T(8,128)S(1)}, f32[7,128,128]{2,1,0:T(8,128)S(1)}, u32[]{:S(2)}, u32[]{:S(2)}) collective-permute-start(f32[7,128,128]{2,1,0:T(8,128)S(1)} %maximum_select_fusion.3), channel_id=1, source_target_pairs={{0,1021},{1,4},{2,1023},{3,6},{4,1},{5,8},{6,3},{7,10},{8,5},{9,12... | collective-permute-start | bytes 1376264 | tf_op jit(solution)/shard_map/ppermute | solution.py:125
  70.6 18.0 %collective-permute-start.8 = (f32[3,128,128]{2,1,0:T(8,128)S(1)}, f32[3,128,128]{2,1,0:T(8,128)S(1)}, u32[]{:S(2)}, u32[]{:S(2)}) collective-permute-start(f32[3,128,128]{2,1,0:T(8,128)S(1)} %maximum_select_fusion.5), channel_id=1, source_target_pairs={{0,1019},{1,6},{2,1021},{3,8},{4,1023},{5,10},{6,1},{7,12},{8,3},{... | collective-permute-start | bytes 589832 | tf_op jit(solution)/shard_map/ppermute | solution.py:125
  88.7 23.2 %copy-start.3 = (f32[21,128,128]{2,1,0:T(8,128)}, f32[21,128,128]{2,1,0:T(8,128)S(1)}, u32[]{:S(2)}) copy-start(f32[21,128,128]{2,1,0:T(8,128)S(1)} %constant_dynamic-update-slice_fusion.3.rg) | copy-start | bytes 4128772
  88.7 23.2 %collective-permute-start.9 = (f32[21,128,128]{2,1,0:T(8,128)S(1)}, f32[21,128,128]{2,1,0:T(8,128)S(1)}, u32[]{:S(2)}, u32[]{:S(2)}) collective-permute-start(f32[21,128,128]{2,1,0:T(8,128)S(1)} %constant_dynamic-update-slice_fusion.3.rg), channel_id=1, source_target_pairs={{0,1},{1,0},{2,3},{3,2},{4,5},{5,4},{6,7},{7,6},{8,9},{9,8},{10,11... | collective-permute-start | bytes 4128776 | tf_op jit(solution)/shard_map/ppermute | solution.py:19
  111.9 1.1 copy-start.5

commit v8 on v6

--- a/solution.py
+++ b/solution.py
@@ -44,65 +44,104 @@
     return partner, own, other, got
 
 
+def block_level(k, o):
+    q = k + o
+    if q in (0, 1):
+        return 0
+    from_lower_chip = q < 0
+    return 1 + int(from_lower_chip == (k == 1))
+
+
+def term_blocks(k, inner, target):
+    left = (0, inner, False) if inner >= 0 else (inner, -inner, True)
+    if target >= inner:
+        right = (inner, target - inner, 0)
+    else:
+        right = (target, inner - target, 1)
+    level = max(block_level(k, left[0]), block_level(k, right[0]))
+    return left, right, level
+
+
 def split(x):
     hi = x.astype(jnp.bfloat16)
     lo = (x - hi.astype(jnp.float32)).astype(jnp.bfloat16)
     return hi, lo
 
 
-def product(a_hi, a_lo, b, b_dim):
-    b_hi, b_lo = split(b)
-    dims = (((1,), (b_dim,)), ((), ()))
+def product(a_hi, a_lo, m, m_dim):
+    m_hi, m_lo = split(m)
+    dims = (((1,), (m_dim,)), ((), ()))
 
     def dot(x, y):
         return lax.dot_general(x, y, dims, preferred_element_type=jnp.float32)
 
-    return dot(a_hi, b_hi) + (dot(a_hi, b_lo) + dot(a_lo, b_hi))
+    return dot(a_hi, m_hi) + (dot(a_hi, m_lo) + dot(a_lo, m_hi))
 
 
-def band_kernel(parity, flags, lx, lp, lg, lo, rx, rp, rg, ro, out, left_hi, left_lo, *, final):
+def band_kernel(*refs, level, final):
+    count = 2 + level
+    parity, flags = refs[0], refs[1]
+    left_in = list(refs[2:2 + count]) + [None] * (4 - count)
+    right_in = list(refs[2 + count:2 + 2 * count]) + [None] * (4 - count)
+    rest = refs[2 + 2 * count:]
+    partial = rest[0] if level > 0 else None
+    out, left_hi, left_lo = rest[-3:]
+
     def compute(k):
-        left = chip_refs(k, lx, lp, lg, lo)
-        right = chip_refs(k, rx, rp, rg, ro)
-        for inner in range(-REACH, REACH + 1):
-            if inner >= 0:
-                a = block_source(k, 0, inner, *left)
-            else:
-                a = block_source(k, inner, -inner, *left).T
-            a_hi, a_lo = split(a)
+        left = chip_refs(k, *left_in)
+        right = chip_refs(k, *right_in)
+        terms = {
+            t: [i for i in range(t - REACH, REACH + 1) if term_blocks(k, i, t)[2] == level]
+            for t in range(WIDTH)
+        }
+        used = sorted({i for t in terms for i in terms[t]})
+        for inner in used:
+            (o, w, transposed), _, _ = term_blocks(k, inner, 0 if inner < 0 else inner)
+            a = block_source(k, o, w, *left)
+            a_hi, a_lo = split(a.T if transposed else a)
             left_hi[inner + REACH] = a_hi
             left_lo[inner + REACH] = a_lo
         for target in range(WIDTH):
-            total = None
-            for inner in range(target - REACH, REACH + 1):
-                if target >= inner:
-                    b, b_dim = block_source(k, inner, target - inner, *right), 0
-                else:
-                    b, b_dim = block_source(k, target, inner - target, *right), 1
-                term = product(left_hi[inner + REACH], left_lo[inner + REACH], b, b_dim)
+            total = None if partial is None else partial[target]
+            for inner in terms[target]:
+                _, (o, w, m_dim), _ = term_blocks(k, inner, target)
+                m = block_source(k, o, w, *right)
+                term = product(left_hi[inner + REACH], left_lo[inner + REACH], m, m_dim)
                 total = term if total is None else total + term
-            total = flags[target] * total
-            if final:
-                total = 3.0 * rx[target] - 2.0 * total
+            if total is None:
+                total = jnp.zeros(out.shape[1:], jnp.float32)
+            if level == 2:
+                total = flags[target] * total
+                if final:
+                    total = 3.0 * right_in[0][target] - 2.0 * total
             out[target] = total
 
     for k in (0, 1):
         pl.when(parity[0] == k)(lambda k=k: compute(k))
 
 
-def band_product(parity, flags, left, right, final):
+def band_level(level, parity, flags, left, right, partial, final):
     vmem = pl.BlockSpec(memory_space=pltpu.VMEM)
     smem = pl.BlockSpec(memory_space=pltpu.SMEM)
     local = left[0]
     b = local.shape[-1]
+    count = 2 + level
+    arrays = list(left[:count]) + list(right[:count]) + ([partial] if level > 0 else [])
     return pl.pallas_call(
-        functools.partial(band_kernel, final=final),
+        functools.partial(band_kernel, level=level, final=final),
         out_shape=jax.ShapeDtypeStruct(local.shape, jnp.float32),
-        in_specs=[smem, smem] + [vmem] * 8,
+        in_specs=[smem, smem] + [vmem] * len(arrays),
         out_specs=vmem,
         scratch_shapes=[pltpu.VMEM((2 * REACH + 1, b, b), jnp.bfloat16)] * 2,
         interpret=INTERPRET,
-    )(parity, flags, *left, *right)
+    )(parity, flags, *arrays)
+
+
+def band_product(parity, flags, left, right, final):
+    partial = None
+    for level in range(3):
+        partial = band_level(level, parity, flags, left, right, partial, final)
+    return partial
 
 
 def exchange_rows(x, is_odd, n):

time: 121 us -> 128 us (1.058)
  Pallas kernels: 13.4 us -> 25.5 us
  waiting for transfers between devices: 42.5 us -> 38.2 us
    pallas_call x2 -> x6, Pallas kernels: 13.4 us -> 25.5 us  [band_level(): pl.pallas_call(functools.partial(band_kernel, level=level, final=final),...]
    ppermute x4, waiting for transfers between devices: 7.98 us -> 3.61 us  [swap_in_chip(): return lax.ppermute(x, AXES, [(i, i ^ 1) for i in range(n)])]
  transfers between devices with their start and end apart: 10 -> 10, of which waited for: 8 -> 6; matrix products, arithmetic and copies ran while one was open for 1% -> 1% of each run, Pallas kernels for 0% -> 13%
where the time goes in v8:
time: 128 us; the launch traced here: 127 us
  starting transfers between devices  56.9 us (44%)
  waiting for transfers between devices  38.2 us (30%)
  Pallas kernels  25.5 us (20%)
  other arithmetic  3.57 us (3%)
  local copies, waits for them, and re-layouts  2.81 us (2%)
    ppermute x4, starting transfers between devices, swap_in_chip(): return lax.ppermute(x, AXES, [(i, i ^ 1) for i in range(n)])  37.1 us
    ppermute x6, waiting for transfers between devices, exchange_rows(): received.append(lax.ppermute(buf, AXES, route))  34.5 us
    pallas_call x6, Pallas kernels, band_level(): pl.pallas_call(functools.partial(band_kernel, level=level, final=final),...  25.5 us
    ppermute x6, starting transfers between devices, exchange_rows(): received.append(lax.ppermute(buf, AXES, route))  19.8 us
    ppermute x4, waiting for transfers between devices, swap_in_chip(): return lax.ppermute(x, AXES, [(i, i ^ 1) for i in range(n)])  3.61 us
  transfers between devices with their start and end apart: 10, of which 6 were waited for; matrix products, arithmetic and copies ran while one was open for 1% of the time, Pallas kernels for 13%

profile of v8, /device:TPU:65, one launch (start us, length us, event | category | flops | bytes accessed | tf_op | source)
XLA Modules:
  0.0 127.4 jit_solution(17668004425478142653)
XLA Ops:
  0.0 2.6 %collective-permute-start = (f32[7,128,128]{2,1,0:T(8,128)}, f32[7,128,128]{2,1,0:T(8,128)S(1)}, u32[]{:S(2)}, u32[]{:S(2)}) collective-permute-start(f32[7,128,128]{2,1,0:T(8,128)} %bitcast.6), channel_id=1, source_target_pairs={{0,1},{1,0},{2,3},{3,2},{4,5},{5,4},{6,7},{7,6},{8,9},{9,8},{10,11... | collective-permute-start | bytes 1376264 | tf_op jit(solution)/shard_map/ppermute | solution.py:19
  2.6 1.6 %collective-permute-done.refs_3_.refs_5_.refs_6_.refs_7_ = f32[7,128,128]{2,1,0:T(8,128)S(1)} collective-permute-done((f32[7,128,128]{2,1,0:T(8,128)}, f32[7,128,128]{2,1,0:T(8,128)S(1)}, u32[]{:S(2)}, u32[]{:S(2)}) %collective-permute-start) | collective-permute-done | bytes 458784 | tf_op jit(solution)/shard_map/ppermute | solution.py:19
  4.2 1.3 broadcast_select_fusion.3
  5.7 3.8 %collective-permute-start.1 = (f32[11,128,128]{2,1,0:T(8,128)S(1)}, f32[11,128,128]{2,1,0:T(8,128)S(1)}, u32[]{:S(2)}, u32[]{:S(2)}) collective-permute-start(f32[11,128,128]{2,1,0:T(8,128)S(1)} %maximum_select_fusion), channel_id=1, source_target_pairs={{0,1023},{1,2},{2,1},{3,4},{4,3},{5,6},{6,5},{7,8},{8,7},{9,10},{1... | collective-permute-start | bytes 2162696 | tf_op jit(solution)/shard_map/ppermute | solution.py:158
  9.7 4.5 %collective-permute-start.2 = (f32[7,128,128]{2,1,0:T(8,128)S(1)}, f32[7,128,128]{2,1,0:T(8,128)S(1)}, u32[]{:S(2)}, u32[]{:S(2)}) collective-permute-start(f32[7,128,128]{2,1,0:T(8,128)S(1)} %maximum_select_fusion.2), channel_id=1, source_target_pairs={{0,1021},{1,4},{2,1023},{3,6},{4,1},{5,8},{6,3},{7,10},{8,5},{9,12... | collective-permute-start | bytes 1376264 | tf_op jit(solution)/shard_map/ppermute | solution.py:158
  14.3 5.8 %collective-permute-start.3 = (f32[3,128,128]{2,1,0:T(8,128)S(1)}, f32[3,128,128]{2,1,0:T(8,128)S(1)}, u32[]{:S(2)}, u32[]{:S(2)}) collective-permute-start(f32[3,128,128]{2,1,0:T(8,128)S(1)} %maximum_select_fusion.4), channel_id=1, source_target_pairs={{0,1019},{1,6},{2,1021},{3,8},{4,1023},{5,10},{6,1},{7,12},{8,3},{... | collective-permute-start | bytes 589832 | tf_op jit(solution)/shard_map/ppermute | solution.py:158
  20.0 4.7 %collective-permute-done.1 = f32[11,128,128]{2,1,0:T(8,128)S(1)} collective-permute-done((f32[11,128,128]{2,1,0:T(8,128)S(1)}, f32[11,128,128]{2,1,0:T(8,128)S(1)}, u32[]{:S(2)}, u32[]{:S(2)}) %collective-permute-start.1) | collective-permute-done | bytes 720928 | tf_op jit(solution)/shard_map/ppermute | solution.py:158
  24.8 6.5 %collective-permute-done.2 = f32[7,128,128]{2,1,0:T(8,128)S(1)} collective-permute-done((f32[7,128,128]{2,1,0:T(8,128)S(1)}, f32[7,128,128]{2,1,0:T(8,128)S(1)}, u32[]{:S(2)}, u32[]{:S(2)}) %collective-permute-start.2) | collective-permute-done | bytes 458784 | tf_op jit(solution)/shard_map/ppermute | solution.py:158
  31.4 7.3 %collective-permute-done.3 = f32[3,128,128]{2,1,0:T(8,128)S(1)} collective-permute-done((f32[3,128,128]{2,1,0:T(8,128)S(1)}, f32[3,128,128]{2,1,0:T(8,128)S(1)}, u32[]{:S(2)}, u32[]{:S(2)}) %collective-permute-start.3) | collective-permute-done | bytes 196640 | tf_op jit(solution)/shard_map/ppermute | solution.py:158
  38.7 12.4 %collective-permute-start.4 = (f32[21,128,128]{2,1,0:T(8,128)S(1)}, f32[21,128,128]{2,1,0:T(8,128)S(1)}, u32[]{:S(2)}, u32[]{:S(2)}) collective-permute-start(f32[21,128,128]{2,1,0:T(8,128)S(1)} %constant_dynamic-update-slice_fusion.refs_4_.refs_7_.refs_8_), channel_id=1, source_target_pairs={{0,1},{1,0},{2,3},{3,2},{4,5},{5,4},{6,7},{7,6},{8,9},{9,8},{10,11... | collective-permute-start | bytes 4128776 | tf_op jit(solution)/shard_map/ppermute | solution.py:19
  51.9 3.3 %shard_map.28.refs_8_ = f32[7,128,128]{2,1,0:T(8,128)} custom-call(s32[1]{0:T(128)} %bitcast.refs_0_, f32[7]{0:T(128)} %convert_element_type.3.refs_1_, f32[7,128,128]{2,1,0:T(8,128)} %bitcast.7, f32[7,128,128]{2,1,0:T(8,128)} %copy-done.1, f32[7,128,128]{2,1,0:T(8,128)} %bitcast.8, f32[7,128,128]{2,1,0:T(8,128)} %copy-done.1), custom_call_target="tpu_custom_call" | custom-call | tf_op jit(solution)/shard_map/pallas_call | solution.py:130
  55.1 4.9 %shard_map.29.refs_10_ = f32[7,128,128]{2,1,0:T(8,128)} custom-call(s32[1]{0:T(128)} %bitcast.refs_0_, f32[7]{0:T(128)} %convert_element_type.3.refs_1_, f32[7,128,128]{2,1,0:T(8,128)} %bitcast.9, f32[7,128,128]{2,1,0:T(8,128)} %copy-done.1, f32[21,128,128]{2,1,0:T(8,128)} %copy-done, f32[7,128,128]{2,1,0:T(8,128)} %bitcast.10, f32[7,128,128]{2,1,0:T(8,128)} %copy-done.1, ...), custom_call_target="tpu_custom_call" | custom-call | tf_op jit(solution)/shard_map/pallas_call | solution.py:130
  61.1 4.8 %shard_map.30.refs_4_.refs_5_.refs_6_ = f32[7,128,128]{2,1,0:T(8,128)} custom-call(s32[1]{0:T(128)} %bitcast.refs_0_, f32[7]{0:T(128)} %convert_element_type.3.refs_1_, f32[7,128,128]{2,1,0:T(8,128)} %bitcast.11, f32[7,128,128]{2,1,0:T(8,128)} %copy-done.1, f32[21,128,128]{2,1,0:T(8,128)} %copy-done, f32[21,128,128]{2,1,0:T(8,128)} %copy-done.2, ...), custom_call_target="tpu_custom_call" | custom-call | tf_op jit(solution)/shard_map/pallas_call | solution.py:130
  65.9 1.9 %collective-permute-start.5 = (f32[7,128,128]{2,1,0:T(8,128)}, f32[7,128,128]{2,1,0:T(8,128)S(1)}, u32[]{:S(2)}, u32[]{:S(2)}) collective-permute-start(f32[7,128,128]{2,1,0:T(8,128)} %shard_map.30.refs_4_.refs_5_.refs_6_), channel_id=1, source_target_pairs={{0,1},{1,0},{2,3},{3,2},{4,5},{5,4},{6,7},{7,6},{8,9},{9,8},{10,11... | collective-permute-start | bytes 1376264 | tf_op jit(solution)/shard_map/ppermute | solution.py:19
  67.9 2.0 %collective-permute-done.5.refs_5_.refs_6_.refs_7_ = f32[7,128,128]{2,1,0:T(8,128)S(1)} collective-permute-done((f32[7,128,128]{2,1,0:T(8,128)}, f32[7,128,128]{2,1,0:T(8,128)S(1)}, u32[]{:S(2)}, u32[]{:S(2)}) %collective-permute-start.5) | collective-permute-done | bytes 458784 | tf_op jit(solution)/shard_map/ppermute | solution.py:19
  69.8 1.3 broadcast_select_fusion.1
  71.3 1.9 %collective-permute-start.6 = (f32[11,128,128]{2,1,0:T(8,128)S(1)}, f32[11,128,128]{2,1,0:T(8,128)S(1)}, u32[]{:S(2)}, u32[]{:S(2)}) collective-permute-start(f32[11,128,128]{2,1,0:T(8,128)S(1)} %maximum_select_fusion.1), channel_id=1, source_target_pairs={{0,1023},{1,2},{2,1},{3,4},{4,3},{5,6},{6,5},{7,8},{8,7},{9,10},{1... | collective-permute-start | bytes 2162696 | tf_op jit(solution)/shard_map/ppermute | solution.py:158
  73.4 1.9 %collective-permute-start.7 = (f32[7,128,128]{2,1,0:T(8,128)S(1)}, f32[7,128,128]{2,1,0:T(8,128)S(1)}, u32[]{:S(2)}, u32[]{:S(2)}) collective-permute-start(f32[7,128,128]{2,1,0:T(8,128)S(1)} %maximum_select_fusion.3), channel_id=1, source_target_pairs={{0,1021},{1,4},{2,1023},{3,6},{4,1},{5,8},{6,3},{7,10},{8,5},{9,12... | collective-permute-start | bytes 1376264 | tf_op jit(solution)/shard_map/ppermute | solution.py:158
  75.5 1.9 %collective-permute-start.8 = (f32[3,128,128]{2,1,0:T(8,128)S(1)}, f32[3,128,128]{2,1,0:T(8,128)S(1)}, u32[]{:S(2)}, u32[]{:S(2)}) collective-permute-start(f32[3,128,128]{2,1,0:T(8,128)S(1)} %maximum_select_fusion.5), channel_id=1, source_target_pairs={{0,1019},{1,6},{2,1021},{3,8},{4,1023},{5,10},{6,1},{7,12},{8,3},{... | collective-permute-start | bytes 589832 | tf_op jit(solution)/shard_map/ppermute | solution.py:158
  77.4 16.0 %collective-permute-done.6 = f32[11,128,128]{2,1,0:T(8,128)S(1)} collective-permute-done((f32[11,128,128]{2,1,0:T(8,128)S(1)}, f32[11,128,128]{2,1,0:T(8,128)S(1)}, u32[]{:S(2)}, u32[]{:S(2)}) %collective-permute-start.6) | collective-permute-done | bytes 720928 | tf_op jit(solution)/shard_map/ppermute | solution.py:158
  93.5 20.2 %collective-permute-start.9 = (f32[21,128,128]{2,1,0:T(8,128)S(1)}, f32[21,128,128]{2,1,0:T(8,128)S(1)}, u32[]{:S(2)}, u32[]{:S(2)}) collective-permute-start(f32[21,128,128]{2,1,0:T(8,128)S(1)} %constant_dynamic-update-slice_fusion.3.refs_7_.refs_8_), channel_id=1, source_target_pairs={{0,1},{1,0},{2,3},{3,2},{4,5},{5,4},{6,7},{7,6},{8,9},{9,8},{10,11... | collective-permute-start | bytes 4128776 | tf_op jit(solution)/shard_map/ppermute | solution.py:19
  113.7 3.2 %shard_map.31.refs_8_ = f32[7,128,128]{2,1,0:T(8,128)} custom-call(s32[1]{0:T(128)} %bitcast.refs_0_, f32[7]{0:T(128)} %convert_element_type.3.refs_1_, f32[7,128,128]{2,1,0:T(8,128)} %bitcast.13, f32[7,128,128]{2,1,0:T(8,128)} %copy-done.1, f32[7,128,128]{2,1,0:T(8,128)} %shard_map.30.refs_4_.refs_5_.refs_6_, f32[7,128,128]{2,1,0:T(8,128)} %copy-done.4), custom_call_target="tpu_custom_call" | custom-call | tf_op jit(solution)/shard_map/pallas_call | solution.py:130
  116.9 4.8 %shard_map.32.refs_10_ = f32[7,128,128]{2,1,0:T(8,128)} custom-call(s32[1]{0:T(128)} %bitcast.refs_0_, f32[7]{0:T(128)} %convert_element_type.3.refs_1_, f32[7,128,128]{2,1,0:T(8,128)} %bitcast.14, f32[7,128,128]{2,1,0:T(8,128)} %copy-done.1, f32[21,128,128]{2,1,0:T(8,128)} %copy-done, f32[7,128,128]{2,1,0:T(8,128)} %shard_map.30.refs_4_.refs_5_.refs_6_, ...), custom_call_target="tpu_custom_call" | custom-call | tf_op jit(solution)/shard_map/pallas_call | solution.py:130
  122.8 4.6 %shard_map.33 = f32[7,128,128]{2,1,0:T(8,128)} custom-call(s32[1]{0:T(128)} %bitcast.refs_0_, f32[7]{0:T(128)} %convert_element_type.3.refs_1_, f32[7,128,128]{2,1,0:T(8,128)} %bitcast.15, f32[7,128,128]{2,1,0:T(8,128)} %copy-done.1, f32[21,128,128]{2,1,0:T(8,128)} %copy-done, f32[21,128,128]{2,1,0:T(8,128)} %copy-done.2, ...), custom_call_target="tpu_custom_call" | custom-call | tf_op jit(solution)/shard_map/pallas_call | solution.py:130
  (57 shorter events, 3.9 us)
Async XLA Ops:
  0.0 4.2 %collective-permute-start = (f32[7,128,128]{2,1,0:T(8,128)}, f32[7,128,128]{2,1,0:T(8,128)S(1)}, u32[]{:S(2)}, u32[]{:S(2)}) collective-permute-start(f32[7,128,128]{2,1,0:T(8,128)} %bitcast.6), channel_id=1, source_target_pairs={{0,1},{1,0},{2,3},{3,2},{4,5},{5,4},{6,7},{7,6},{8,9},{9,8},{10,11... | collective-permute-start | bytes 1376264 | tf_op jit(solution)/shard_map/ppermute | solution.py:19
  4.2 1.3 %copy-start.1 = (f32[7,128,128]{2,1,0:T(8,128)}, f32[7,128,128]{2,1,0:T(8,128)S(1)}, u32[]{:S(2)}) copy-start(f32[7,128,128]{2,1,0:T(8,128)S(1)} %collective-permute-done.refs_3_.refs_5_.refs_6_.refs_7_) | copy-start | bytes 1376260
  5.7 19.0 %collective-permute-start.1 = (f32[11,128,128]{2,1,0:T(8,128)S(1)}, f32[11,128,128]{2,1,0:T(8,128)S(1)}, u32[]{:S(2)}, u32[]{:S(2)}) collective-permute-start(f32[11,128,128]{2,1,0:T(8,128)S(1)} %maximum_select_fusion), channel_id=1, source_target_pairs={{0,1023},{1,2},{2,1},{3,4},{4,3},{5,6},{6,5},{7,8},{8,7},{9,10},{1... | collective-permute-start | bytes 2162696 | tf_op jit(solution)/shard_map/ppermute | solution.py:158
  9.7 21.7 %collective-permute-start.2 = (f32[7,128,128]{2,1,0:T(8,128)S(1)}, f32[7,128,128]{2,1,0:T(8,128)S(1)}, u32[]{:S(2)}, u32[]{:S(2)}) collective-permute-start(f32[7,128,128]{2,1,0:T(8,128)S(1)} %maximum_select_fusion.2), channel_id=1, source_target_pairs={{0,1021},{1,4},{2,1023},{3,6},{4,1},{5,8},{6,3},{7,10},{8,5},{9,12... | collective-permute-start | bytes 1376264 | tf_op jit(solution)/shard_map/ppermute | solution.py:158
  14.3 36.9 %copy-start.6 = (s32[1,12]{1,0:T(1,128)S(1)}, s32[1,12]{1,0:T(1,128)}, u32[]{:S(2)}) copy-start(s32[1,12]{1,0:T(1,128)} %param.3) | copy-start | bytes 148
  14.3 24.4 %collective-permute-start.3 = (f32[3,128,128]{2,1,0:T(8,128)S(1)}, f32[3,128,128]{2,1,0:T(8,128)S(1)}, u32[]{:S(2)}, u32[]{:S(2)}) collective-permute-start(f32[3,128,128]{2,1,0:T(8,128)S(1)} %maximum_select_fusion.4), channel_id=1, source_target_pairs={{0,1019},{1,6},{2,1021},{3,8},{4,1023},{5,10},{6,1},{7,12},{8,3},{... | collective-permute-start | bytes 589832 | tf_op jit(solution)/shard_map/ppermute | solution.py:158
  38.7 16.4 %copy-start = (f32[21,128,128]{2,1,0:T(8,128)}, f32[21,128,128]{2,1,0:T(8,128)S(1)}, u32[]{:S(2)}) copy-start(f32[21,128,128]{2,1,0:T(8,128)S(1)} %constant_dynamic-update-slice_fusion.refs_4_.refs_7_.refs_8_) | copy-start | bytes 4128772
  38.7 21.3 %collective-permute-start.4 = (f32[21,128,128]{2,1,0:T(8,128)S(1)}, f32[21,128,128]{2,1,0:T(8,128)S(1)}, u32[]{:S(2)}, u32[]{:S(2)}) collective-permute-start(f32[21,128,128]{2,1,0:T(8,128)S(1)} %constant_dynamic-update-slice_fusion.refs_4_.refs_7_.refs_8_), channel_id=1, source_target_pairs={{0,1},{1,0},{2,3},{3,2},{4,5},{5,4},{6,7},{7,6},{8,9},{9,8},{10,11... | collective-permute-start | bytes 4128776 | tf_op jit(solution)/shard_map/ppermute | solution.py:19
  60.0 1.1 copy-start.2
  65.9 3.9 %collective-permute-start.5 = (f32[7,128,128]{2,1,0:T(8,128)}, f32[7,128,128]{2,1,0:T(8,128)S(1)}, u32[]{:S(2)}, u32[]{:S(2)}) collective-permute-start(f32[7,128,128]{2,1,0:T(8,128)} %shard_map.30.refs_4_.refs_5_.refs_6_), channel_id=1, source_target_pairs={{0,1},{1,0},{2,3},{3,2},{4,5},{5,4},{6,7},{7,6},{8,9},{9,8},{10,11... | collective-permute-start | bytes 1376264 | tf_op jit(solution)/shard_map/ppermute | solution.py:19
  69.8 1.3 %copy-start.4 = (f32[7,128,128]{2,1,0:T(8,128)}, f32[7,128,128]{2,1,0:T(8,128)S(1)}, u32[]{:S(2)}) copy-start(f32[7,128,128]{2,1,0:T(8,128)S(1)} %collective-permute-done.5.refs_5_.refs_6_.refs_7_) | copy-start | bytes 1376260
  71.3 22.0 %collective-permute-start.6 = (f32[11,128,128]{2,1,0:T(8,128)S(1)}, f32[11,128,128]{2,1,0:T(8,128)S(1)}, u32[]{:S(2)}, u32[]{:S(2)}) collective-permute-start(f32[11,128,128]{2,1,0:T(8,128)S(1)} %maximum_select_fusion.1), channel_id=1, source_target_pairs={{0,1023},{1,2},{2,1},{3,4},{4,3},{5,6},{6,5},{7,8},{8,7},{9,10},{1... | collective-permute-start | bytes 2162696 | tf_op jit(solution)/shard_map/ppermute | solution.py:158
  73.4 20.0 %collective-permute-start.7 = (f32[7,128,128]{2,1,0:T(8,128)S(1)}, f32[7,128,128]{2,1,0:T(8,128)S(1)}, u32[]{:S(2)}, u32[]{:S(2)}) collective-permute-start(f32[7,128,128]{2,1,0:T(8,128)S(1)} %maximum_select_fusion.3), channel_id=1, source_target_pairs={{0,1021},{1,4},{2,1023},{3,6},{4,1},{5,8},{6,3},{7,10},{8,5},{9,12... | collective-permute-start | bytes 1376264 | tf_op jit(solution)/shard_map/ppermute | solution.py:158
  75.5 18.0 %collective-permute-start.8 = (f32[3,128,128]{2,1,0:T(8,128)S(1)}, f32[3,128,128]{2,1,0:T(8,128)S(1)}, u32[]{:S(2)}, u32[]{:S(2)}) collective-permute-start(f32[3,128,128]{2,1,0:T(8,128)S(1)} %maximum_select_fusion.5), channel_id=1, source_target_pairs={{0,1019},{1,6},{2,1021},{3,8},{4,1023},{5,10},{6,1},{7,12},{8,3},{... | collective-permute-start | bytes 589832 | tf_op jit(solution)/shard_map/ppermute | solution.py:158
  93.5 23.4 %copy-start.3 = (f32[21,128,128]{2,1,0:T(8,128)}, f32[21,128,128]{2,1,0:T(8,128)S(1)}, u32[]{:S(2)}) copy-start(f32[21,128,128]{2,1,0:T(8,128)S(1)} %constant_dynamic-update-slice_fusion.3.refs_7_.refs_8_) | copy-start | bytes 4128772
  93.5 28.1 %collective-permute-start.9 = (f32[21,128,128]{2,1,0:T(8,128)S(1)}, f32[21,128,128]{2,1,0:T(8,128)S(1)}, u32[]{:S(2)}, u32[]{:S(2)}) collective-permute-start(f32[21,128,128]{2,1,0:T(8,128)S(1)} %constant_dynamic-update-slice_fusion.3.refs_7_.refs_8_), channel_id=1, source_target_pairs={{0,1},{1,0},{2,3},{3,2},{4,5},{5,4},{6,7},{7,6},{8,9},{9,8},{10,11... | collective-permute-start | bytes 4128776 | tf_op jit(solution)/shard_map/ppermute | solution.py:19
  121.7 1.1 copy-start.5

commit v9 on v7

--- a/solution.py
+++ b/solution.py
@@ -50,22 +50,31 @@
     return hi, lo
 
 
-def band_kernel(parity, flags, lx, lp, lg, lo, rx, rp, rg, ro, out, left_all, right_all, *, final):
+def band_kernel(*refs, final):
+    parity, flags = refs[0], refs[1]
+    if final:
+        left_in, right_in = None, refs[3:7]
+        out, right_all = refs[7], refs[8]
+        left_all = refs[2]
+    else:
+        left_in = right_in = refs[2:6]
+        out, left_all, right_all = refs[6], refs[7], refs[8]
     b = out.shape[-1]
 
     def compute(k):
-        left = chip_refs(k, lx, lp, lg, lo)
-        right = chip_refs(k, rx, rp, rg, ro)
-        for inner in range(-REACH, REACH + 1):
-            if inner >= 0:
-                a = block_source(k, 0, inner, *left)
-            else:
-                a = block_source(k, inner, -inner, *left).T
-            a_hi, a_lo = split(a)
-            i = 3 * (inner + REACH)
-            left_all[:, i * b:(i + 1) * b] = a_hi
-            left_all[:, (i + 1) * b:(i + 2) * b] = a_hi
-            left_all[:, (i + 2) * b:(i + 3) * b] = a_lo
+        right = chip_refs(k, *right_in)
+        if not final:
+            left = chip_refs(k, *left_in)
+            for inner in range(-REACH, REACH + 1):
+                if inner >= 0:
+                    a = block_source(k, 0, inner, *left)
+                else:
+                    a = block_source(k, inner, -inner, *left).T
+                a_hi, a_lo = split(a)
+                i = 3 * (inner + REACH)
+                left_all[:, i * b:(i + 1) * b] = a_hi
+                left_all[:, (i + 1) * b:(i + 2) * b] = a_hi
+                left_all[:, (i + 2) * b:(i + 3) * b] = a_lo
         for target in range(WIDTH):
             rows = right_all.at[target % 2]
             for j, inner in enumerate(range(target - REACH, REACH + 1)):
@@ -85,30 +94,29 @@
             )
             total = flags[target] * total
             if final:
-                total = 3.0 * rx[target] - 2.0 * total
+                total = 3.0 * right_in[0][target] - 2.0 * total
             out[target] = total
 
     for k in (0, 1):
         pl.when(parity[0] == k)(lambda k=k: compute(k))
 
 
-def band_product(parity, flags, left, right, final):
+def band_call(parity, flags, arrays, final):
     vmem = pl.BlockSpec(memory_space=pltpu.VMEM)
     smem = pl.BlockSpec(memory_space=pltpu.SMEM)
-    local = left[0]
+    local = arrays[-4]
     b = local.shape[-1]
     depth = 3 * (2 * REACH + 1) * b
+    square_shape = jax.ShapeDtypeStruct(local.shape, jnp.float32)
+    left_shape = jax.ShapeDtypeStruct((b, depth), jnp.bfloat16)
     return pl.pallas_call(
         functools.partial(band_kernel, final=final),
-        out_shape=jax.ShapeDtypeStruct(local.shape, jnp.float32),
-        in_specs=[smem, smem] + [vmem] * 8,
-        out_specs=vmem,
-        scratch_shapes=[
-            pltpu.VMEM((b, depth), jnp.bfloat16),
-            pltpu.VMEM((2, depth, b), jnp.bfloat16),
-        ],
+        out_shape=square_shape if final else (square_shape, left_shape),
+        in_specs=[smem, smem] + [vmem] * len(arrays),
+        out_specs=vmem if final else (vmem, vmem),
+        scratch_shapes=[pltpu.VMEM((2, depth, b), jnp.bfloat16)],
         interpret=INTERPRET,
-    )(parity, flags, *left, *right)
+    )(parity, flags, *arrays)
 
 
 def exchange_rows(x, is_odd, n):
@@ -137,9 +145,9 @@
     columns = (position + jnp.arange(WIDTH, dtype=jnp.int32)) % n
     flags = jnp.any(pattern[0][None, :] == columns[:, None], axis=1).astype(jnp.float32)
     chip_p = exchange_rows(local_band, is_odd, n)
-    square = band_product(parity, flags, chip_p, chip_p, final=False)
+    square, left_all = band_call(parity, flags, chip_p, final=False)
     chip_s = exchange_rows(square, is_odd, n)
-    purified = band_product(parity, flags, chip_p, chip_s, final=True)
+    purified = band_call(parity, flags, (left_all,) + chip_s, final=True)
     return purified[None]
 
 

time: 120 us -> 118 us (0.983)
  Pallas kernels: 12.3 us -> 10.8 us
    pallas_call x2, Pallas kernels: 12.3 us -> 10.8 us  [band_call(): pl.pallas_call(functools.partial(band_kernel, final=final), out_shape=squ...]
where the time goes in v9:
time: 118 us
  starting transfers between devices  57.5 us (49%)
  waiting for transfers between devices  42.5 us (36%)
  Pallas kernels  10.8 us (9%)
  other arithmetic  3.61 us (3%)
  local copies, waits for them, and re-layouts  2.77 us (2%)
    ppermute x4, starting transfers between devices, swap_in_chip(): return lax.ppermute(x, AXES, [(i, i ^ 1) for i in range(n)])  37.7 us
    ppermute x6, waiting for transfers between devices, exchange_rows(): received.append(lax.ppermute(buf, AXES, route))  34.5 us
    ppermute x6, starting transfers between devices, exchange_rows(): received.append(lax.ppermute(buf, AXES, route))  19.8 us
    pallas_call x2, Pallas kernels, band_call(): pl.pallas_call(functools.partial(band_kernel, final=final), out_shape=squ...  10.8 us
    ppermute x4, waiting for transfers between devices, swap_in_chip(): return lax.ppermute(x, AXES, [(i, i ^ 1) for i in range(n)])  7.92 us
    select_n x2, other arithmetic, exchange_rows(): r1 = jnp.where(is_odd, x, partner)  2.52 us
  transfers between devices with their start and end apart: 10, of which 8 were waited for; matrix products, arithmetic and copies ran while one was open for 1% of the time, Pallas kernels for 0%

profile of v9, /device:TPU:65, one launch (start us, length us, event | category | flops | bytes accessed | tf_op | source)
XLA Modules:
  0.0 117.6 jit_solution(522221872264491231)
XLA Ops:
  0.0 2.6 %collective-permute-start = (f32[7,128,128]{2,1,0:T(8,128)}, f32[7,128,128]{2,1,0:T(8,128)S(1)}, u32[]{:S(2)}, u32[]{:S(2)}) collective-permute-start(f32[7,128,128]{2,1,0:T(8,128)} %bitcast.6), channel_id=1, source_target_pairs={{0,1},{1,0},{2,3},{3,2},{4,5},{5,4},{6,7},{7,6},{8,9},{9,8},{10,11... | collective-permute-start | bytes 1376264 | tf_op jit(solution)/shard_map/ppermute | solution.py:19
  2.6 1.6 %collective-permute-done.refs_3_ = f32[7,128,128]{2,1,0:T(8,128)S(1)} collective-permute-done((f32[7,128,128]{2,1,0:T(8,128)}, f32[7,128,128]{2,1,0:T(8,128)S(1)}, u32[]{:S(2)}, u32[]{:S(2)}) %collective-permute-start) | collective-permute-done | bytes 458784 | tf_op jit(solution)/shard_map/ppermute | solution.py:19
  4.2 1.3 %broadcast_select_fusion.3 = (f32[7,128,128]{2,1,0:T(8,128)S(1)}, f32[7,128,128]{2,1,0:T(8,128)S(1)}) fusion(f32[7,128,128]{2,1,0:T(8,128)S(1)} %collective-permute-done.refs_3_, pred[]{:T(512)S(6)} %eq.27, f32[1,7,128,128]{3,2,1,0:T(8,128)} %param.2), kind=kLoop, calls=%fused_computation.7 | loop fusion | flops 229376 | bytes 1835009 | tf_op jit(solution)/shard_map/jit(_where)/select_n | solution.py:125
  5.7 3.8 %collective-permute-start.1 = (f32[11,128,128]{2,1,0:T(8,128)S(1)}, f32[11,128,128]{2,1,0:T(8,128)S(1)}, u32[]{:S(2)}, u32[]{:S(2)}) collective-permute-start(f32[11,128,128]{2,1,0:T(8,128)S(1)} %maximum_select_fusion), channel_id=1, source_target_pairs={{0,1023},{1,2},{2,1},{3,4},{4,3},{5,6},{6,5},{7,8},{8,7},{9,10},{1... | collective-permute-start | bytes 2162696 | tf_op jit(solution)/shard_map/ppermute | solution.py:133
  9.7 4.5 %collective-permute-start.2 = (f32[7,128,128]{2,1,0:T(8,128)S(1)}, f32[7,128,128]{2,1,0:T(8,128)S(1)}, u32[]{:S(2)}, u32[]{:S(2)}) collective-permute-start(f32[7,128,128]{2,1,0:T(8,128)S(1)} %maximum_select_fusion.2), channel_id=1, source_target_pairs={{0,1021},{1,4},{2,1023},{3,6},{4,1},{5,8},{6,3},{7,10},{8,5},{9,12... | collective-permute-start | bytes 1376264 | tf_op jit(solution)/shard_map/ppermute | solution.py:133
  14.3 5.8 %collective-permute-start.3 = (f32[3,128,128]{2,1,0:T(8,128)S(1)}, f32[3,128,128]{2,1,0:T(8,128)S(1)}, u32[]{:S(2)}, u32[]{:S(2)}) collective-permute-start(f32[3,128,128]{2,1,0:T(8,128)S(1)} %maximum_select_fusion.4), channel_id=1, source_target_pairs={{0,1019},{1,6},{2,1021},{3,8},{4,1023},{5,10},{6,1},{7,12},{8,3},{... | collective-permute-start | bytes 589832 | tf_op jit(solution)/shard_map/ppermute | solution.py:133
  20.0 4.7 %collective-permute-done.1 = f32[11,128,128]{2,1,0:T(8,128)S(1)} collective-permute-done((f32[11,128,128]{2,1,0:T(8,128)S(1)}, f32[11,128,128]{2,1,0:T(8,128)S(1)}, u32[]{:S(2)}, u32[]{:S(2)}) %collective-permute-start.1) | collective-permute-done | bytes 720928 | tf_op jit(solution)/shard_map/ppermute | solution.py:133
  24.8 6.5 %collective-permute-done.2 = f32[7,128,128]{2,1,0:T(8,128)S(1)} collective-permute-done((f32[7,128,128]{2,1,0:T(8,128)S(1)}, f32[7,128,128]{2,1,0:T(8,128)S(1)}, u32[]{:S(2)}, u32[]{:S(2)}) %collective-permute-start.2) | collective-permute-done | bytes 458784 | tf_op jit(solution)/shard_map/ppermute | solution.py:133
  31.4 7.3 %collective-permute-done.3 = f32[3,128,128]{2,1,0:T(8,128)S(1)} collective-permute-done((f32[3,128,128]{2,1,0:T(8,128)S(1)}, f32[3,128,128]{2,1,0:T(8,128)S(1)}, u32[]{:S(2)}, u32[]{:S(2)}) %collective-permute-start.3) | collective-permute-done | bytes 196640 | tf_op jit(solution)/shard_map/ppermute | solution.py:133
  38.7 12.4 %collective-permute-start.4 = (f32[21,128,128]{2,1,0:T(8,128)S(1)}, f32[21,128,128]{2,1,0:T(8,128)S(1)}, u32[]{:S(2)}, u32[]{:S(2)}) collective-permute-start(f32[21,128,128]{2,1,0:T(8,128)S(1)} %constant_dynamic-update-slice_fusion.refs_4_), channel_id=1, source_target_pairs={{0,1},{1,0},{2,3},{3,2},{4,5},{5,4},{6,7},{7,6},{8,9},{9,8},{10,11... | collective-permute-start | bytes 4128776 | tf_op jit(solution)/shard_map/ppermute | solution.py:19
  51.9 1.9 %collective-permute-done.4.refs_5_ = f32[21,128,128]{2,1,0:T(8,128)S(1)} collective-permute-done((f32[21,128,128]{2,1,0:T(8,128)S(1)}, f32[21,128,128]{2,1,0:T(8,128)S(1)}, u32[]{:S(2)}, u32[]{:S(2)}) %collective-permute-start.4) | collective-permute-done | bytes 1376288 | tf_op jit(solution)/shard_map/ppermute | solution.py:19
  53.9 1.1 copy-done.4
  54.9 5.4 %shard_map.28 = (f32[7,128,128]{2,1,0:T(8,128)}, bf16[128,4992]{1,0:T(8,128)(2,1)}) custom-call(s32[1]{0:T(128)} %bitcast.refs_0_, f32[7]{0:T(128)} %convert_element_type.3.refs_1_, f32[7,128,128]{2,1,0:T(8,128)} %bitcast.7, f32[7,128,128]{2,1,0:T(8,128)} %copy-done.3, f32[21,128,128]{2,1,0:T(8,128)} %copy-done, f32[21,128,128]{2,1,0:T(8,128)} %copy-done.4), custom_call_target="tpu_custom_call" | custom-call | tf_op jit(solution)/shard_map/pallas_call | solution.py:112
  60.4 2.3 %collective-permute-start.5 = (f32[7,128,128]{2,1,0:T(8,128)}, f32[7,128,128]{2,1,0:T(8,128)S(1)}, u32[]{:S(2)}, u32[]{:S(2)}) collective-permute-start(f32[7,128,128]{2,1,0:T(8,128)} %get-tuple-element.8.refs_3_), channel_id=1, source_target_pairs={{0,1},{1,0},{2,3},{3,2},{4,5},{5,4},{6,7},{7,6},{8,9},{9,8},{10,11... | collective-permute-start | bytes 1376264 | tf_op jit(solution)/shard_map/ppermute | solution.py:19
  62.7 1.6 %collective-permute-done.5.refs_4_ = f32[7,128,128]{2,1,0:T(8,128)S(1)} collective-permute-done((f32[7,128,128]{2,1,0:T(8,128)}, f32[7,128,128]{2,1,0:T(8,128)S(1)}, u32[]{:S(2)}, u32[]{:S(2)}) %collective-permute-start.5) | collective-permute-done | bytes 458784 | tf_op jit(solution)/shard_map/ppermute | solution.py:19
  64.3 1.3 %broadcast_select_fusion.1 = (f32[7,128,128]{2,1,0:T(8,128)S(1)}, f32[7,128,128]{2,1,0:T(8,128)S(1)}) fusion(f32[7,128,128]{2,1,0:T(8,128)} %get-tuple-element.8.refs_3_, f32[7,128,128]{2,1,0:T(8,128)S(1)} %collective-permute-done.5.refs_4_, pred[]{:T(512)S(6)} %eq.27), kind=kLoop, calls=%fused_computation.5 | loop fusion | flops 229376 | bytes 1835009 | tf_op jit(solution)/shard_map/jit(_where)/select_n | solution.py:125
  65.8 1.9 %collective-permute-start.6 = (f32[11,128,128]{2,1,0:T(8,128)S(1)}, f32[11,128,128]{2,1,0:T(8,128)S(1)}, u32[]{:S(2)}, u32[]{:S(2)}) collective-permute-start(f32[11,128,128]{2,1,0:T(8,128)S(1)} %maximum_select_fusion.1), channel_id=1, source_target_pairs={{0,1023},{1,2},{2,1},{3,4},{4,3},{5,6},{6,5},{7,8},{8,7},{9,10},{1... | collective-permute-start | bytes 2162696 | tf_op jit(solution)/shard_map/ppermute | solution.py:133
  67.9 1.9 %collective-permute-start.7 = (f32[7,128,128]{2,1,0:T(8,128)S(1)}, f32[7,128,128]{2,1,0:T(8,128)S(1)}, u32[]{:S(2)}, u32[]{:S(2)}) collective-permute-start(f32[7,128,128]{2,1,0:T(8,128)S(1)} %maximum_select_fusion.3), channel_id=1, source_target_pairs={{0,1021},{1,4},{2,1023},{3,6},{4,1},{5,8},{6,3},{7,10},{8,5},{9,12... | collective-permute-start | bytes 1376264 | tf_op jit(solution)/shard_map/ppermute | solution.py:133
  69.9 1.9 %collective-permute-start.8 = (f32[3,128,128]{2,1,0:T(8,128)S(1)}, f32[3,128,128]{2,1,0:T(8,128)S(1)}, u32[]{:S(2)}, u32[]{:S(2)}) collective-permute-start(f32[3,128,128]{2,1,0:T(8,128)S(1)} %maximum_select_fusion.5), channel_id=1, source_target_pairs={{0,1019},{1,6},{2,1021},{3,8},{4,1023},{5,10},{6,1},{7,12},{8,3},{... | collective-permute-start | bytes 589832 | tf_op jit(solution)/shard_map/ppermute | solution.py:133
  71.8 16.0 %collective-permute-done.6 = f32[11,128,128]{2,1,0:T(8,128)S(1)} collective-permute-done((f32[11,128,128]{2,1,0:T(8,128)S(1)}, f32[11,128,128]{2,1,0:T(8,128)S(1)}, u32[]{:S(2)}, u32[]{:S(2)}) %collective-permute-start.6) | collective-permute-done | bytes 720928 | tf_op jit(solution)/shard_map/ppermute | solution.py:133
  88.0 20.4 %collective-permute-start.9 = (f32[21,128,128]{2,1,0:T(8,128)S(1)}, f32[21,128,128]{2,1,0:T(8,128)S(1)}, u32[]{:S(2)}, u32[]{:S(2)}) collective-permute-start(f32[21,128,128]{2,1,0:T(8,128)S(1)} %constant_dynamic-update-slice_fusion.3.refs_5_), channel_id=1, source_target_pairs={{0,1},{1,0},{2,3},{3,2},{4,5},{5,4},{6,7},{7,6},{8,9},{9,8},{10,11... | collective-permute-start | bytes 4128776 | tf_op jit(solution)/shard_map/ppermute | solution.py:19
  108.4 2.7 %collective-permute-done.9.refs_6_ = f32[21,128,128]{2,1,0:T(8,128)S(1)} collective-permute-done((f32[21,128,128]{2,1,0:T(8,128)S(1)}, f32[21,128,128]{2,1,0:T(8,128)S(1)}, u32[]{:S(2)}, u32[]{:S(2)}) %collective-permute-start.9) | collective-permute-done | bytes 1376288 | tf_op jit(solution)/shard_map/ppermute | solution.py:19
  111.1 1.1 copy-done.5
  112.2 5.4 %shard_map.29 = f32[7,128,128]{2,1,0:T(8,128)} custom-call(s32[1]{0:T(128)} %bitcast.refs_0_, f32[7]{0:T(128)} %convert_element_type.3.refs_1_, bf16[128,4992]{1,0:T(8,128)(2,1)} %get-tuple-element.7.refs_2_, f32[7,128,128]{2,1,0:T(8,128)} %get-tuple-element.8.refs_3_, f32[7,128,128]{2,1,0:T(8,128)} %copy-done.2, f32[21,128,128]{2,1,0:T(8,128)} %copy-done.1, ...), custom_call_target="tpu_custom_call" | custom-call | tf_op jit(solution)/shard_map/pallas_call | solution.py:112
  (53 shorter events, 1.7 us)
Async XLA Ops:
  0.0 4.2 %collective-permute-start = (f32[7,128,128]{2,1,0:T(8,128)}, f32[7,128,128]{2,1,0:T(8,128)S(1)}, u32[]{:S(2)}, u32[]{:S(2)}) collective-permute-start(f32[7,128,128]{2,1,0:T(8,128)} %bitcast.6), channel_id=1, source_target_pairs={{0,1},{1,0},{2,3},{3,2},{4,5},{5,4},{6,7},{7,6},{8,9},{9,8},{10,11... | collective-permute-start | bytes 1376264 | tf_op jit(solution)/shard_map/ppermute | solution.py:19
  4.2 1.3 %copy-start.3 = (f32[7,128,128]{2,1,0:T(8,128)}, f32[7,128,128]{2,1,0:T(8,128)S(1)}, u32[]{:S(2)}) copy-start(f32[7,128,128]{2,1,0:T(8,128)S(1)} %collective-permute-done.refs_3_) | copy-start | bytes 1376260
  5.7 19.0 %collective-permute-start.1 = (f32[11,128,128]{2,1,0:T(8,128)S(1)}, f32[11,128,128]{2,1,0:T(8,128)S(1)}, u32[]{:S(2)}, u32[]{:S(2)}) collective-permute-start(f32[11,128,128]{2,1,0:T(8,128)S(1)} %maximum_select_fusion), channel_id=1, source_target_pairs={{0,1023},{1,2},{2,1},{3,4},{4,3},{5,6},{6,5},{7,8},{8,7},{9,10},{1... | collective-permute-start | bytes 2162696 | tf_op jit(solution)/shard_map/ppermute | solution.py:133
  9.7 21.7 %collective-permute-start.2 = (f32[7,128,128]{2,1,0:T(8,128)S(1)}, f32[7,128,128]{2,1,0:T(8,128)S(1)}, u32[]{:S(2)}, u32[]{:S(2)}) collective-permute-start(f32[7,128,128]{2,1,0:T(8,128)S(1)} %maximum_select_fusion.2), channel_id=1, source_target_pairs={{0,1021},{1,4},{2,1023},{3,6},{4,1},{5,8},{6,3},{7,10},{8,5},{9,12... | collective-permute-start | bytes 1376264 | tf_op jit(solution)/shard_map/ppermute | solution.py:133
  14.3 36.9 %copy-start.6 = (s32[1,12]{1,0:T(1,128)S(1)}, s32[1,12]{1,0:T(1,128)}, u32[]{:S(2)}) copy-start(s32[1,12]{1,0:T(1,128)} %param.3) | copy-start | bytes 148
  14.3 24.4 %collective-permute-start.3 = (f32[3,128,128]{2,1,0:T(8,128)S(1)}, f32[3,128,128]{2,1,0:T(8,128)S(1)}, u32[]{:S(2)}, u32[]{:S(2)}) collective-permute-start(f32[3,128,128]{2,1,0:T(8,128)S(1)} %maximum_select_fusion.4), channel_id=1, source_target_pairs={{0,1019},{1,6},{2,1021},{3,8},{4,1023},{5,10},{6,1},{7,12},{8,3},{... | collective-permute-start | bytes 589832 | tf_op jit(solution)/shard_map/ppermute | solution.py:133
  38.7 15.2 %copy-start = (f32[21,128,128]{2,1,0:T(8,128)}, f32[21,128,128]{2,1,0:T(8,128)S(1)}, u32[]{:S(2)}) copy-start(f32[21,128,128]{2,1,0:T(8,128)S(1)} %constant_dynamic-update-slice_fusion.refs_4_) | copy-start | bytes 4128772
  38.7 15.2 %collective-permute-start.4 = (f32[21,128,128]{2,1,0:T(8,128)S(1)}, f32[21,128,128]{2,1,0:T(8,128)S(1)}, u32[]{:S(2)}, u32[]{:S(2)}) collective-permute-start(f32[21,128,128]{2,1,0:T(8,128)S(1)} %constant_dynamic-update-slice_fusion.refs_4_), channel_id=1, source_target_pairs={{0,1},{1,0},{2,3},{3,2},{4,5},{5,4},{6,7},{7,6},{8,9},{9,8},{10,11... | collective-permute-start | bytes 4128776 | tf_op jit(solution)/shard_map/ppermute | solution.py:19
  53.9 1.1 copy-start.4
  60.4 3.9 %collective-permute-start.5 = (f32[7,128,128]{2,1,0:T(8,128)}, f32[7,128,128]{2,1,0:T(8,128)S(1)}, u32[]{:S(2)}, u32[]{:S(2)}) collective-permute-start(f32[7,128,128]{2,1,0:T(8,128)} %get-tuple-element.8.refs_3_), channel_id=1, source_target_pairs={{0,1},{1,0},{2,3},{3,2},{4,5},{5,4},{6,7},{7,6},{8,9},{9,8},{10,11... | collective-permute-start | bytes 1376264 | tf_op jit(solution)/shard_map/ppermute | solution.py:19
  64.3 1.3 %copy-start.2 = (f32[7,128,128]{2,1,0:T(8,128)}, f32[7,128,128]{2,1,0:T(8,128)S(1)}, u32[]{:S(2)}) copy-start(f32[7,128,128]{2,1,0:T(8,128)S(1)} %collective-permute-done.5.refs_4_) | copy-start | bytes 1376260
  65.8 22.0 %collective-permute-start.6 = (f32[11,128,128]{2,1,0:T(8,128)S(1)}, f32[11,128,128]{2,1,0:T(8,128)S(1)}, u32[]{:S(2)}, u32[]{:S(2)}) collective-permute-start(f32[11,128,128]{2,1,0:T(8,128)S(1)} %maximum_select_fusion.1), channel_id=1, source_target_pairs={{0,1023},{1,2},{2,1},{3,4},{4,3},{5,6},{6,5},{7,8},{8,7},{9,10},{1... | collective-permute-start | bytes 2162696 | tf_op jit(solution)/shard_map/ppermute | solution.py:133
  67.9 20.0 %collective-permute-start.7 = (f32[7,128,128]{2,1,0:T(8,128)S(1)}, f32[7,128,128]{2,1,0:T(8,128)S(1)}, u32[]{:S(2)}, u32[]{:S(2)}) collective-permute-start(f32[7,128,128]{2,1,0:T(8,128)S(1)} %maximum_select_fusion.3), channel_id=1, source_target_pairs={{0,1021},{1,4},{2,1023},{3,6},{4,1},{5,8},{6,3},{7,10},{8,5},{9,12... | collective-permute-start | bytes 1376264 | tf_op jit(solution)/shard_map/ppermute | solution.py:133
  69.9 18.0 %collective-permute-start.8 = (f32[3,128,128]{2,1,0:T(8,128)S(1)}, f32[3,128,128]{2,1,0:T(8,128)S(1)}, u32[]{:S(2)}, u32[]{:S(2)}) collective-permute-start(f32[3,128,128]{2,1,0:T(8,128)S(1)} %maximum_select_fusion.5), channel_id=1, source_target_pairs={{0,1019},{1,6},{2,1021},{3,8},{4,1023},{5,10},{6,1},{7,12},{8,3},{... | collective-permute-start | bytes 589832 | tf_op jit(solution)/shard_map/ppermute | solution.py:133
  88.0 23.2 %copy-start.1 = (f32[21,128,128]{2,1,0:T(8,128)}, f32[21,128,128]{2,1,0:T(8,128)S(1)}, u32[]{:S(2)}) copy-start(f32[21,128,128]{2,1,0:T(8,128)S(1)} %constant_dynamic-update-slice_fusion.3.refs_5_) | copy-start | bytes 4128772
  88.0 23.2 %collective-permute-start.9 = (f32[21,128,128]{2,1,0:T(8,128)S(1)}, f32[21,128,128]{2,1,0:T(8,128)S(1)}, u32[]{:S(2)}, u32[]{:S(2)}) collective-permute-start(f32[21,128,128]{2,1,0:T(8,128)S(1)} %constant_dynamic-update-slice_fusion.3.refs_5_), channel_id=1, source_target_pairs={{0,1},{1,0},{2,3},{3,2},{4,5},{5,4},{6,7},{7,6},{8,9},{9,8},{10,11... | collective-permute-start | bytes 4128776 | tf_op jit(solution)/shard_map/ppermute | solution.py:19
  111.1 1.1 copy-start.5

commit v10 on v9

--- a/solution.py
+++ b/solution.py
@@ -50,21 +50,45 @@
     return hi, lo
 
 
-def band_kernel(*refs, final):
+class Fetched:
+    def __init__(self, copy, buffer):
+        self.copy, self.buffer, self.ready = copy, buffer, False
+
+    def wait(self):
+        if not self.ready:
+            self.copy.wait()
+            self.ready = True
+
+    def __getitem__(self, index):
+        self.wait()
+        return self.buffer[index]
+
+    def slab(self):
+        self.wait()
+        return self.buffer
+
+
+def band_kernel(*refs, final, count):
     parity, flags = refs[0], refs[1]
-    if final:
-        left_in, right_in = None, refs[3:7]
-        out, right_all = refs[7], refs[8]
-        left_all = refs[2]
-    else:
-        left_in = right_in = refs[2:6]
-        out, left_all, right_all = refs[6], refs[7], refs[8]
+    inputs = refs[2:2 + count]
+    outs = refs[2 + count:2 + count + (1 if final else 2)]
+    scratch = refs[2 + count + len(outs):]
+    right_all, buffers, sems = scratch[0], scratch[1:1 + count], scratch[1 + count]
+    out = outs[0]
     b = out.shape[-1]
+    copies = [pltpu.make_async_copy(inputs[i], buffers[i], sems.at[i]) for i in range(count)]
+    for copy in copies:
+        copy.start()
 
     def compute(k):
-        right = chip_refs(k, *right_in)
-        if not final:
-            left = chip_refs(k, *left_in)
+        fetched = [Fetched(copies[i], buffers[i]) for i in range(count)]
+        if final:
+            left_all = fetched[0]
+            right_in = fetched[1:]
+        else:
+            left_all = outs[1]
+            right_in = fetched
+            left = chip_refs(k, *fetched)
             for inner in range(-REACH, REACH + 1):
                 if inner >= 0:
                     a = block_source(k, 0, inner, *left)
@@ -75,6 +99,7 @@
                 left_all[:, i * b:(i + 1) * b] = a_hi
                 left_all[:, (i + 1) * b:(i + 2) * b] = a_hi
                 left_all[:, (i + 2) * b:(i + 3) * b] = a_lo
+        right = chip_refs(k, *right_in)
         for target in range(WIDTH):
             rows = right_all.at[target % 2]
             for j, inner in enumerate(range(target - REACH, REACH + 1)):
@@ -87,8 +112,9 @@
                 rows[(3 * j + 1) * b:(3 * j + 2) * b, :] = m_lo
                 rows[(3 * j + 2) * b:(3 * j + 3) * b, :] = m_hi
             depth = 3 * (2 * REACH + 1 - target) * b
+            lhs = left_all.slab() if final else left_all
             total = jnp.dot(
-                left_all[:, 3 * target * b:],
+                lhs[:, 3 * target * b:],
                 rows[:depth, :],
                 preferred_element_type=jnp.float32,
             )
@@ -96,6 +122,8 @@
             if final:
                 total = 3.0 * right_in[0][target] - 2.0 * total
             out[target] = total
+        for f in fetched:
+            f.wait()
 
     for k in (0, 1):
         pl.when(parity[0] == k)(lambda k=k: compute(k))
@@ -104,17 +132,21 @@
 def band_call(parity, flags, arrays, final):
     vmem = pl.BlockSpec(memory_space=pltpu.VMEM)
     smem = pl.BlockSpec(memory_space=pltpu.SMEM)
+    anywhere = pl.BlockSpec(memory_space=pl.ANY)
     local = arrays[-4]
     b = local.shape[-1]
     depth = 3 * (2 * REACH + 1) * b
     square_shape = jax.ShapeDtypeStruct(local.shape, jnp.float32)
     left_shape = jax.ShapeDtypeStruct((b, depth), jnp.bfloat16)
+    count = len(arrays)
     return pl.pallas_call(
-        functools.partial(band_kernel, final=final),
+        functools.partial(band_kernel, final=final, count=count),
         out_shape=square_shape if final else (square_shape, left_shape),
-        in_specs=[smem, smem] + [vmem] * len(arrays),
+        in_specs=[smem, smem] + [anywhere] * count,
         out_specs=vmem if final else (vmem, vmem),
-        scratch_shapes=[pltpu.VMEM((2, depth, b), jnp.bfloat16)],
+        scratch_shapes=[pltpu.VMEM((2, depth, b), jnp.bfloat16)]
+        + [pltpu.VMEM(a.shape, a.dtype) for a in arrays]
+        + [pltpu.SemaphoreType.DMA((count,))],
         interpret=INTERPRET,
     )(parity, flags, *arrays)
 

time: 118 us -> 120 us (1.017)
  Pallas kernels: 10.8 us -> 13 us
    pallas_call x2, Pallas kernels: 10.8 us -> 13 us  [band_call(): pl.pallas_call(functools.partial(band_kernel, final=final, count=count),...]
where the time goes in v10:
time: 120 us
  starting transfers between devices  56.9 us (47%)
  waiting for transfers between devices  42.8 us (36%)
  Pallas kernels  13 us (11%)
  other arithmetic  3.61 us (3%)
  local copies, waits for them, and re-layouts  2.77 us (2%)
    ppermute x4, starting transfers between devices, swap_in_chip(): return lax.ppermute(x, AXES, [(i, i ^ 1) for i in range(n)])  37.1 us
    ppermute x6, waiting for transfers between devices, exchange_rows(): received.append(lax.ppermute(buf, AXES, route))  34.5 us
    ppermute x6, starting transfers between devices, exchange_rows(): received.append(lax.ppermute(buf, AXES, route))  19.8 us
    pallas_call x2, Pallas kernels, band_call(): pl.pallas_call(functools.partial(band_kernel, final=final, count=count),...  13 us
    ppermute x4, waiting for transfers between devices, swap_in_chip(): return lax.ppermute(x, AXES, [(i, i ^ 1) for i in range(n)])  8.22 us
    select_n x2, other arithmetic, exchange_rows(): r1 = jnp.where(is_odd, x, partner)  2.52 us
  transfers between devices with their start and end apart: 10, of which 8 were waited for; matrix products, arithmetic and copies ran while one was open for 1% of the time, Pallas kernels for 0%

profile of v10, /device:TPU:65, one launch (start us, length us, event | category | flops | bytes accessed | tf_op | source)
XLA Modules:
  0.0 119.5 jit_solution(15272063743425263994)
XLA Ops:
  0.0 2.6 %collective-permute-start = (f32[7,128,128]{2,1,0:T(8,128)}, f32[7,128,128]{2,1,0:T(8,128)S(1)}, u32[]{:S(2)}, u32[]{:S(2)}) collective-permute-start(f32[7,128,128]{2,1,0:T(8,128)} %bitcast.6), channel_id=1, source_target_pairs={{0,1},{1,0},{2,3},{3,2},{4,5},{5,4},{6,7},{7,6},{8,9},{9,8},{10,11... | collective-permute-start | bytes 1376264 | tf_op jit(solution)/shard_map/ppermute | solution.py:19
  2.6 1.6 %collective-permute-done.refs_3_ = f32[7,128,128]{2,1,0:T(8,128)S(1)} collective-permute-done((f32[7,128,128]{2,1,0:T(8,128)}, f32[7,128,128]{2,1,0:T(8,128)S(1)}, u32[]{:S(2)}, u32[]{:S(2)}) %collective-permute-start) | collective-permute-done | bytes 458784 | tf_op jit(solution)/shard_map/ppermute | solution.py:19
  4.2 1.3 %broadcast_select_fusion.3 = (f32[7,128,128]{2,1,0:T(8,128)S(1)}, f32[7,128,128]{2,1,0:T(8,128)S(1)}) fusion(f32[7,128,128]{2,1,0:T(8,128)S(1)} %collective-permute-done.refs_3_, pred[]{:T(512)S(6)} %eq.27, f32[1,7,128,128]{3,2,1,0:T(8,128)} %param.2), kind=kLoop, calls=%fused_computation.7 | loop fusion | flops 229376 | bytes 1835009 | tf_op jit(solution)/shard_map/jit(_where)/select_n | solution.py:157
  5.7 3.8 %collective-permute-start.1 = (f32[11,128,128]{2,1,0:T(8,128)S(1)}, f32[11,128,128]{2,1,0:T(8,128)S(1)}, u32[]{:S(2)}, u32[]{:S(2)}) collective-permute-start(f32[11,128,128]{2,1,0:T(8,128)S(1)} %maximum_select_fusion), channel_id=1, source_target_pairs={{0,1023},{1,2},{2,1},{3,4},{4,3},{5,6},{6,5},{7,8},{8,7},{9,10},{1... | collective-permute-start | bytes 2162696 | tf_op jit(solution)/shard_map/ppermute | solution.py:165
  9.7 4.5 %collective-permute-start.2 = (f32[7,128,128]{2,1,0:T(8,128)S(1)}, f32[7,128,128]{2,1,0:T(8,128)S(1)}, u32[]{:S(2)}, u32[]{:S(2)}) collective-permute-start(f32[7,128,128]{2,1,0:T(8,128)S(1)} %maximum_select_fusion.2), channel_id=1, source_target_pairs={{0,1021},{1,4},{2,1023},{3,6},{4,1},{5,8},{6,3},{7,10},{8,5},{9,12... | collective-permute-start | bytes 1376264 | tf_op jit(solution)/shard_map/ppermute | solution.py:165
  14.3 5.8 %collective-permute-start.3 = (f32[3,128,128]{2,1,0:T(8,128)S(1)}, f32[3,128,128]{2,1,0:T(8,128)S(1)}, u32[]{:S(2)}, u32[]{:S(2)}) collective-permute-start(f32[3,128,128]{2,1,0:T(8,128)S(1)} %maximum_select_fusion.4), channel_id=1, source_target_pairs={{0,1019},{1,6},{2,1021},{3,8},{4,1023},{5,10},{6,1},{7,12},{8,3},{... | collective-permute-start | bytes 589832 | tf_op jit(solution)/shard_map/ppermute | solution.py:165
  20.0 4.7 %collective-permute-done.1 = f32[11,128,128]{2,1,0:T(8,128)S(1)} collective-permute-done((f32[11,128,128]{2,1,0:T(8,128)S(1)}, f32[11,128,128]{2,1,0:T(8,128)S(1)}, u32[]{:S(2)}, u32[]{:S(2)}) %collective-permute-start.1) | collective-permute-done | bytes 720928 | tf_op jit(solution)/shard_map/ppermute | solution.py:165
  24.8 6.5 %collective-permute-done.2 = f32[7,128,128]{2,1,0:T(8,128)S(1)} collective-permute-done((f32[7,128,128]{2,1,0:T(8,128)S(1)}, f32[7,128,128]{2,1,0:T(8,128)S(1)}, u32[]{:S(2)}, u32[]{:S(2)}) %collective-permute-start.2) | collective-permute-done | bytes 458784 | tf_op jit(solution)/shard_map/ppermute | solution.py:165
  31.4 7.3 %collective-permute-done.3 = f32[3,128,128]{2,1,0:T(8,128)S(1)} collective-permute-done((f32[3,128,128]{2,1,0:T(8,128)S(1)}, f32[3,128,128]{2,1,0:T(8,128)S(1)}, u32[]{:S(2)}, u32[]{:S(2)}) %collective-permute-start.3) | collective-permute-done | bytes 196640 | tf_op jit(solution)/shard_map/ppermute | solution.py:165
  38.7 12.4 %collective-permute-start.4 = (f32[21,128,128]{2,1,0:T(8,128)S(1)}, f32[21,128,128]{2,1,0:T(8,128)S(1)}, u32[]{:S(2)}, u32[]{:S(2)}) collective-permute-start(f32[21,128,128]{2,1,0:T(8,128)S(1)} %constant_dynamic-update-slice_fusion.refs_4_), channel_id=1, source_target_pairs={{0,1},{1,0},{2,3},{3,2},{4,5},{5,4},{6,7},{7,6},{8,9},{9,8},{10,11... | collective-permute-start | bytes 4128776 | tf_op jit(solution)/shard_map/ppermute | solution.py:19
  51.9 1.9 %collective-permute-done.4.refs_5_ = f32[21,128,128]{2,1,0:T(8,128)S(1)} collective-permute-done((f32[21,128,128]{2,1,0:T(8,128)S(1)}, f32[21,128,128]{2,1,0:T(8,128)S(1)}, u32[]{:S(2)}, u32[]{:S(2)}) %collective-permute-start.4) | collective-permute-done | bytes 1376288 | tf_op jit(solution)/shard_map/ppermute | solution.py:19
  53.9 1.1 copy-done.4
  54.9 6.6 %shard_map.28 = (f32[7,128,128]{2,1,0:T(8,128)}, bf16[128,4992]{1,0:T(8,128)(2,1)}) custom-call(s32[1]{0:T(128)} %bitcast.refs_0_, f32[7]{0:T(128)} %convert_element_type.3.refs_1_, f32[7,128,128]{2,1,0:T(8,128)} %bitcast.7, f32[7,128,128]{2,1,0:T(8,128)} %copy-done.3, f32[21,128,128]{2,1,0:T(8,128)} %copy-done, f32[21,128,128]{2,1,0:T(8,128)} %copy-done.4), custom_call_target="tpu_custom_call" | custom-call | tf_op jit(solution)/shard_map/pallas_call | solution.py:142
  61.5 2.0 %collective-permute-start.5 = (f32[7,128,128]{2,1,0:T(8,128)}, f32[7,128,128]{2,1,0:T(8,128)S(1)}, u32[]{:S(2)}, u32[]{:S(2)}) collective-permute-start(f32[7,128,128]{2,1,0:T(8,128)} %get-tuple-element.8.refs_3_), channel_id=1, source_target_pairs={{0,1},{1,0},{2,3},{3,2},{4,5},{5,4},{6,7},{7,6},{8,9},{9,8},{10,11... | collective-permute-start | bytes 1376264 | tf_op jit(solution)/shard_map/ppermute | solution.py:19
  63.5 1.9 %collective-permute-done.5.refs_4_ = f32[7,128,128]{2,1,0:T(8,128)S(1)} collective-permute-done((f32[7,128,128]{2,1,0:T(8,128)}, f32[7,128,128]{2,1,0:T(8,128)S(1)}, u32[]{:S(2)}, u32[]{:S(2)}) %collective-permute-start.5) | collective-permute-done | bytes 458784 | tf_op jit(solution)/shard_map/ppermute | solution.py:19
  65.5 1.3 %broadcast_select_fusion.1 = (f32[7,128,128]{2,1,0:T(8,128)S(1)}, f32[7,128,128]{2,1,0:T(8,128)S(1)}) fusion(f32[7,128,128]{2,1,0:T(8,128)} %get-tuple-element.8.refs_3_, f32[7,128,128]{2,1,0:T(8,128)S(1)} %collective-permute-done.5.refs_4_, pred[]{:T(512)S(6)} %eq.27), kind=kLoop, calls=%fused_computation.5 | loop fusion | flops 229376 | bytes 1835009 | tf_op jit(solution)/shard_map/jit(_where)/select_n | solution.py:157
  67.0 1.9 %collective-permute-start.6 = (f32[11,128,128]{2,1,0:T(8,128)S(1)}, f32[11,128,128]{2,1,0:T(8,128)S(1)}, u32[]{:S(2)}, u32[]{:S(2)}) collective-permute-start(f32[11,128,128]{2,1,0:T(8,128)S(1)} %maximum_select_fusion.1), channel_id=1, source_target_pairs={{0,1023},{1,2},{2,1},{3,4},{4,3},{5,6},{6,5},{7,8},{8,7},{9,10},{1... | collective-permute-start | bytes 2162696 | tf_op jit(solution)/shard_map/ppermute | solution.py:165
  69.0 1.9 %collective-permute-start.7 = (f32[7,128,128]{2,1,0:T(8,128)S(1)}, f32[7,128,128]{2,1,0:T(8,128)S(1)}, u32[]{:S(2)}, u32[]{:S(2)}) collective-permute-start(f32[7,128,128]{2,1,0:T(8,128)S(1)} %maximum_select_fusion.3), channel_id=1, source_target_pairs={{0,1021},{1,4},{2,1023},{3,6},{4,1},{5,8},{6,3},{7,10},{8,5},{9,12... | collective-permute-start | bytes 1376264 | tf_op jit(solution)/shard_map/ppermute | solution.py:165
  71.1 1.9 %collective-permute-start.8 = (f32[3,128,128]{2,1,0:T(8,128)S(1)}, f32[3,128,128]{2,1,0:T(8,128)S(1)}, u32[]{:S(2)}, u32[]{:S(2)}) collective-permute-start(f32[3,128,128]{2,1,0:T(8,128)S(1)} %maximum_select_fusion.5), channel_id=1, source_target_pairs={{0,1019},{1,6},{2,1021},{3,8},{4,1023},{5,10},{6,1},{7,12},{8,3},{... | collective-permute-start | bytes 589832 | tf_op jit(solution)/shard_map/ppermute | solution.py:165
  73.0 16.0 %collective-permute-done.6 = f32[11,128,128]{2,1,0:T(8,128)S(1)} collective-permute-done((f32[11,128,128]{2,1,0:T(8,128)S(1)}, f32[11,128,128]{2,1,0:T(8,128)S(1)}, u32[]{:S(2)}, u32[]{:S(2)}) %collective-permute-start.6) | collective-permute-done | bytes 720928 | tf_op jit(solution)/shard_map/ppermute | solution.py:165
  89.1 20.2 %collective-permute-start.9 = (f32[21,128,128]{2,1,0:T(8,128)S(1)}, f32[21,128,128]{2,1,0:T(8,128)S(1)}, u32[]{:S(2)}, u32[]{:S(2)}) collective-permute-start(f32[21,128,128]{2,1,0:T(8,128)S(1)} %constant_dynamic-update-slice_fusion.3.refs_5_), channel_id=1, source_target_pairs={{0,1},{1,0},{2,3},{3,2},{4,5},{5,4},{6,7},{7,6},{8,9},{9,8},{10,11... | collective-permute-start | bytes 4128776 | tf_op jit(solution)/shard_map/ppermute | solution.py:19
  109.3 2.7 %collective-permute-done.9.refs_6_ = f32[21,128,128]{2,1,0:T(8,128)S(1)} collective-permute-done((f32[21,128,128]{2,1,0:T(8,128)S(1)}, f32[21,128,128]{2,1,0:T(8,128)S(1)}, u32[]{:S(2)}, u32[]{:S(2)}) %collective-permute-start.9) | collective-permute-done | bytes 1376288 | tf_op jit(solution)/shard_map/ppermute | solution.py:19
  112.1 1.1 copy-done.5
  113.1 6.4 %shard_map.29 = f32[7,128,128]{2,1,0:T(8,128)} custom-call(s32[1]{0:T(128)} %bitcast.refs_0_, f32[7]{0:T(128)} %convert_element_type.3.refs_1_, bf16[128,4992]{1,0:T(8,128)(2,1)} %get-tuple-element.7.refs_2_, f32[7,128,128]{2,1,0:T(8,128)} %get-tuple-element.8.refs_3_, f32[7,128,128]{2,1,0:T(8,128)} %copy-done.2, f32[21,128,128]{2,1,0:T(8,128)} %copy-done.1, ...), custom_call_target="tpu_custom_call" | custom-call | tf_op jit(solution)/shard_map/pallas_call | solution.py:142
  (53 shorter events, 1.7 us)
Async XLA Ops:
  0.0 4.2 %collective-permute-start = (f32[7,128,128]{2,1,0:T(8,128)}, f32[7,128,128]{2,1,0:T(8,128)S(1)}, u32[]{:S(2)}, u32[]{:S(2)}) collective-permute-start(f32[7,128,128]{2,1,0:T(8,128)} %bitcast.6), channel_id=1, source_target_pairs={{0,1},{1,0},{2,3},{3,2},{4,5},{5,4},{6,7},{7,6},{8,9},{9,8},{10,11... | collective-permute-start | bytes 1376264 | tf_op jit(solution)/shard_map/ppermute | solution.py:19
  4.2 1.3 %copy-start.3 = (f32[7,128,128]{2,1,0:T(8,128)}, f32[7,128,128]{2,1,0:T(8,128)S(1)}, u32[]{:S(2)}) copy-start(f32[7,128,128]{2,1,0:T(8,128)S(1)} %collective-permute-done.refs_3_) | copy-start | bytes 1376260
  5.7 19.0 %collective-permute-start.1 = (f32[11,128,128]{2,1,0:T(8,128)S(1)}, f32[11,128,128]{2,1,0:T(8,128)S(1)}, u32[]{:S(2)}, u32[]{:S(2)}) collective-permute-start(f32[11,128,128]{2,1,0:T(8,128)S(1)} %maximum_select_fusion), channel_id=1, source_target_pairs={{0,1023},{1,2},{2,1},{3,4},{4,3},{5,6},{6,5},{7,8},{8,7},{9,10},{1... | collective-permute-start | bytes 2162696 | tf_op jit(solution)/shard_map/ppermute | solution.py:165
  9.7 21.7 %collective-permute-start.2 = (f32[7,128,128]{2,1,0:T(8,128)S(1)}, f32[7,128,128]{2,1,0:T(8,128)S(1)}, u32[]{:S(2)}, u32[]{:S(2)}) collective-permute-start(f32[7,128,128]{2,1,0:T(8,128)S(1)} %maximum_select_fusion.2), channel_id=1, source_target_pairs={{0,1021},{1,4},{2,1023},{3,6},{4,1},{5,8},{6,3},{7,10},{8,5},{9,12... | collective-permute-start | bytes 1376264 | tf_op jit(solution)/shard_map/ppermute | solution.py:165
  14.3 36.9 %copy-start.6 = (s32[1,12]{1,0:T(1,128)S(1)}, s32[1,12]{1,0:T(1,128)}, u32[]{:S(2)}) copy-start(s32[1,12]{1,0:T(1,128)} %param.3) | copy-start | bytes 148
  14.3 24.4 %collective-permute-start.3 = (f32[3,128,128]{2,1,0:T(8,128)S(1)}, f32[3,128,128]{2,1,0:T(8,128)S(1)}, u32[]{:S(2)}, u32[]{:S(2)}) collective-permute-start(f32[3,128,128]{2,1,0:T(8,128)S(1)} %maximum_select_fusion.4), channel_id=1, source_target_pairs={{0,1019},{1,6},{2,1021},{3,8},{4,1023},{5,10},{6,1},{7,12},{8,3},{... | collective-permute-start | bytes 589832 | tf_op jit(solution)/shard_map/ppermute | solution.py:165
  38.7 15.2 %copy-start = (f32[21,128,128]{2,1,0:T(8,128)}, f32[21,128,128]{2,1,0:T(8,128)S(1)}, u32[]{:S(2)}) copy-start(f32[21,128,128]{2,1,0:T(8,128)S(1)} %constant_dynamic-update-slice_fusion.refs_4_) | copy-start | bytes 4128772
  38.7 15.2 %collective-permute-start.4 = (f32[21,128,128]{2,1,0:T(8,128)S(1)}, f32[21,128,128]{2,1,0:T(8,128)S(1)}, u32[]{:S(2)}, u32[]{:S(2)}) collective-permute-start(f32[21,128,128]{2,1,0:T(8,128)S(1)} %constant_dynamic-update-slice_fusion.refs_4_), channel_id=1, source_target_pairs={{0,1},{1,0},{2,3},{3,2},{4,5},{5,4},{6,7},{7,6},{8,9},{9,8},{10,11... | collective-permute-start | bytes 4128776 | tf_op jit(solution)/shard_map/ppermute | solution.py:19
  53.9 1.1 copy-start.4
  61.5 3.9 %collective-permute-start.5 = (f32[7,128,128]{2,1,0:T(8,128)}, f32[7,128,128]{2,1,0:T(8,128)S(1)}, u32[]{:S(2)}, u32[]{:S(2)}) collective-permute-start(f32[7,128,128]{2,1,0:T(8,128)} %get-tuple-element.8.refs_3_), channel_id=1, source_target_pairs={{0,1},{1,0},{2,3},{3,2},{4,5},{5,4},{6,7},{7,6},{8,9},{9,8},{10,11... | collective-permute-start | bytes 1376264 | tf_op jit(solution)/shard_map/ppermute | solution.py:19
  65.5 1.3 %copy-start.2 = (f32[7,128,128]{2,1,0:T(8,128)}, f32[7,128,128]{2,1,0:T(8,128)S(1)}, u32[]{:S(2)}) copy-start(f32[7,128,128]{2,1,0:T(8,128)S(1)} %collective-permute-done.5.refs_4_) | copy-start | bytes 1376260
  67.0 22.0 %collective-permute-start.6 = (f32[11,128,128]{2,1,0:T(8,128)S(1)}, f32[11,128,128]{2,1,0:T(8,128)S(1)}, u32[]{:S(2)}, u32[]{:S(2)}) collective-permute-start(f32[11,128,128]{2,1,0:T(8,128)S(1)} %maximum_select_fusion.1), channel_id=1, source_target_pairs={{0,1023},{1,2},{2,1},{3,4},{4,3},{5,6},{6,5},{7,8},{8,7},{9,10},{1... | collective-permute-start | bytes 2162696 | tf_op jit(solution)/shard_map/ppermute | solution.py:165
  69.0 20.0 %collective-permute-start.7 = (f32[7,128,128]{2,1,0:T(8,128)S(1)}, f32[7,128,128]{2,1,0:T(8,128)S(1)}, u32[]{:S(2)}, u32[]{:S(2)}) collective-permute-start(f32[7,128,128]{2,1,0:T(8,128)S(1)} %maximum_select_fusion.3), channel_id=1, source_target_pairs={{0,1021},{1,4},{2,1023},{3,6},{4,1},{5,8},{6,3},{7,10},{8,5},{9,12... | collective-permute-start | bytes 1376264 | tf_op jit(solution)/shard_map/ppermute | solution.py:165
  71.1 18.0 %collective-permute-start.8 = (f32[3,128,128]{2,1,0:T(8,128)S(1)}, f32[3,128,128]{2,1,0:T(8,128)S(1)}, u32[]{:S(2)}, u32[]{:S(2)}) collective-permute-start(f32[3,128,128]{2,1,0:T(8,128)S(1)} %maximum_select_fusion.5), channel_id=1, source_target_pairs={{0,1019},{1,6},{2,1021},{3,8},{4,1023},{5,10},{6,1},{7,12},{8,3},{... | collective-permute-start | bytes 589832 | tf_op jit(solution)/shard_map/ppermute | solution.py:165
  89.1 22.9 %copy-start.1 = (f32[21,128,128]{2,1,0:T(8,128)}, f32[21,128,128]{2,1,0:T(8,128)S(1)}, u32[]{:S(2)}) copy-start(f32[21,128,128]{2,1,0:T(8,128)S(1)} %constant_dynamic-update-slice_fusion.3.refs_5_) | copy-start | bytes 4128772
  89.1 22.9 %collective-permute-start.9 = (f32[21,128,128]{2,1,0:T(8,128)S(1)}, f32[21,128,128]{2,1,0:T(8,128)S(1)}, u32[]{:S(2)}, u32[]{:S(2)}) collective-permute-start(f32[21,128,128]{2,1,0:T(8,128)S(1)} %constant_dynamic-update-slice_fusion.3.refs_5_), channel_id=1, source_target_pairs={{0,1},{1,0},{2,3},{3,2},{4,5},{5,4},{6,7},{7,6},{8,9},{9,8},{10,11... | collective-permute-start | bytes 4128776 | tf_op jit(solution)/shard_map/ppermute | solution.py:19
  112.1 1.1 copy-start.5

commit v11 on v9

--- a/solution.py
+++ b/solution.py
@@ -38,7 +38,27 @@
     return upper[base + (8 - 2 * d) + w]
 
 
+KEPT = {
+    0: ((1, 6), (7, 11), (12, 15), (16, 18), (19, 20)),
+    1: ((0, 5), (6, 10), (11, 14), (15, 17), (18, 19)),
+}
+
+
+class Trimmed:
+    def __init__(self, ref, sender):
+        self.ref, self.where = ref, {}
+        slot = 0
+        for start, stop in KEPT[sender]:
+            for full in range(start, stop):
+                self.where[full] = slot
+                slot += 1
+
+    def __getitem__(self, full):
+        return self.ref[self.where[full]]
+
+
 def chip_refs(k, own, partner, got, other):
+    other = Trimmed(other, 1 - k)
     if k == 0:
         return own, partner, got, other
     return partner, own, other, got
@@ -132,7 +152,11 @@
         route = [(i, (i + step) % n) if i % 2 else (i, (i - step) % n) for i in range(n)]
         received.append(lax.ppermute(buf, AXES, route))
     got = jnp.concatenate(received, axis=0)
-    other = swap_in_chip(got, n)
+
+    def kept(sender):
+        return jnp.concatenate([got[a:b] for a, b in KEPT[sender]], axis=0)
+
+    other = swap_in_chip(jnp.where(is_odd, kept(1), kept(0)), n)
     return (x, partner, got, other)
 
 

time: 118 us -> 117 us (level)
  waiting for transfers between devices: 42.5 us -> 38.9 us
  other arithmetic: 3.61 us -> 6.19 us
    ppermute x4, waiting for transfers between devices: 7.92 us -> 4.42 us  [swap_in_chip(): return lax.ppermute(x, AXES, [(i, i ^ 1) for i in range(n)])]
    concatenate x0 -> x2, other arithmetic: none -> 2.38 us  [exchange_rows(): got = jnp.concatenate(received, axis=0)]
  transfers between devices with their start and end apart: 10 -> 10, of which waited for: 8 -> 8; matrix products, arithmetic and copies ran while one was open for 1% -> 3% of each run, Pallas kernels for 0% -> 0%
where the time goes in v11:
time: 117 us; the launch traced here: 116 us
  starting transfers between devices  57.4 us (49%)
  waiting for transfers between devices  38.9 us (33%)
  Pallas kernels  10.5 us (9%)
  other arithmetic  6.19 us (5%)
  local copies, waits for them, and re-layouts  2.61 us (2%)
    ppermute x4, starting transfers between devices, swap_in_chip(): return lax.ppermute(x, AXES, [(i, i ^ 1) for i in range(n)])  37.6 us
    ppermute x6, waiting for transfers between devices, exchange_rows(): received.append(lax.ppermute(buf, AXES, route))  34.5 us
    ppermute x6, starting transfers between devices, exchange_rows(): received.append(lax.ppermute(buf, AXES, route))  19.8 us
    pallas_call x2, Pallas kernels, band_call(): pl.pallas_call(functools.partial(band_kernel, final=final), out_shape=squ...  10.5 us
    ppermute x4, waiting for transfers between devices, swap_in_chip(): return lax.ppermute(x, AXES, [(i, i ^ 1) for i in range(n)])  4.42 us
    select_n x2, other arithmetic, exchange_rows(): r1 = jnp.where(is_odd, x, partner)  2.52 us
    concatenate x2, other arithmetic, exchange_rows(): got = jnp.concatenate(received, axis=0)  2.38 us
  transfers between devices with their start and end apart: 10, of which 8 were waited for; matrix products, arithmetic and copies ran while one was open for 3% of the time, Pallas kernels for 0%

profile of v11, /device:TPU:65, one launch (start us, length us, event | category | flops | bytes accessed | tf_op | source)
XLA Modules:
  0.0 116.2 jit_solution(14993657660999902869)
XLA Ops:
  0.0 2.6 %collective-permute-start = (f32[7,128,128]{2,1,0:T(8,128)}, f32[7,128,128]{2,1,0:T(8,128)S(1)}, u32[]{:S(2)}, u32[]{:S(2)}) collective-permute-start(f32[7,128,128]{2,1,0:T(8,128)} %bitcast.6), channel_id=1, source_target_pairs={{0,1},{1,0},{2,3},{3,2},{4,5},{5,4},{6,7},{7,6},{8,9},{9,8},{10,11... | collective-permute-start | bytes 1376264 | tf_op jit(solution)/shard_map/ppermute | solution.py:19
  2.6 1.6 %collective-permute-done.refs_3_ = f32[7,128,128]{2,1,0:T(8,128)S(1)} collective-permute-done((f32[7,128,128]{2,1,0:T(8,128)}, f32[7,128,128]{2,1,0:T(8,128)S(1)}, u32[]{:S(2)}, u32[]{:S(2)}) %collective-permute-start) | collective-permute-done | bytes 458784 | tf_op jit(solution)/shard_map/ppermute | solution.py:19
  4.2 1.3 %broadcast_select_fusion.5 = (f32[7,128,128]{2,1,0:T(8,128)S(1)}, f32[7,128,128]{2,1,0:T(8,128)S(1)}) fusion(f32[7,128,128]{2,1,0:T(8,128)S(1)} %collective-permute-done.refs_3_, pred[]{:T(512)S(6)} %eq.27, f32[1,7,128,128]{3,2,1,0:T(8,128)} %param.2), kind=kLoop, calls=%fused_computation.19 | loop fusion | flops 229376 | bytes 1835009 | tf_op jit(solution)/shard_map/jit(_where)/select_n | solution.py:145
  5.7 3.8 %collective-permute-start.1 = (f32[11,128,128]{2,1,0:T(8,128)S(1)}, f32[11,128,128]{2,1,0:T(8,128)S(1)}, u32[]{:S(2)}, u32[]{:S(2)}) collective-permute-start(f32[11,128,128]{2,1,0:T(8,128)S(1)} %maximum_select_fusion), channel_id=1, source_target_pairs={{0,1023},{1,2},{2,1},{3,4},{4,3},{5,6},{6,5},{7,8},{8,7},{9,10},{1... | collective-permute-start | bytes 2162696 | tf_op jit(solution)/shard_map/ppermute | solution.py:153
  9.8 4.5 %collective-permute-start.2 = (f32[7,128,128]{2,1,0:T(8,128)S(1)}, f32[7,128,128]{2,1,0:T(8,128)S(1)}, u32[]{:S(2)}, u32[]{:S(2)}) collective-permute-start(f32[7,128,128]{2,1,0:T(8,128)S(1)} %maximum_select_fusion.2), channel_id=1, source_target_pairs={{0,1021},{1,4},{2,1023},{3,6},{4,1},{5,8},{6,3},{7,10},{8,5},{9,12... | collective-permute-start | bytes 1376264 | tf_op jit(solution)/shard_map/ppermute | solution.py:153
  14.3 5.8 %collective-permute-start.3 = (f32[3,128,128]{2,1,0:T(8,128)S(1)}, f32[3,128,128]{2,1,0:T(8,128)S(1)}, u32[]{:S(2)}, u32[]{:S(2)}) collective-permute-start(f32[3,128,128]{2,1,0:T(8,128)S(1)} %maximum_select_fusion.4), channel_id=1, source_target_pairs={{0,1019},{1,6},{2,1021},{3,8},{4,1023},{5,10},{6,1},{7,12},{8,3},{... | collective-permute-start | bytes 589832 | tf_op jit(solution)/shard_map/ppermute | solution.py:153
  20.0 4.7 %collective-permute-done.1 = f32[11,128,128]{2,1,0:T(8,128)S(1)} collective-permute-done((f32[11,128,128]{2,1,0:T(8,128)S(1)}, f32[11,128,128]{2,1,0:T(8,128)S(1)}, u32[]{:S(2)}, u32[]{:S(2)}) %collective-permute-start.1) | collective-permute-done | bytes 720928 | tf_op jit(solution)/shard_map/ppermute | solution.py:153
  24.9 6.5 %collective-permute-done.2 = f32[7,128,128]{2,1,0:T(8,128)S(1)} collective-permute-done((f32[7,128,128]{2,1,0:T(8,128)S(1)}, f32[7,128,128]{2,1,0:T(8,128)S(1)}, u32[]{:S(2)}, u32[]{:S(2)}) %collective-permute-start.2) | collective-permute-done | bytes 458784 | tf_op jit(solution)/shard_map/ppermute | solution.py:153
  31.4 7.3 %collective-permute-done.3 = f32[3,128,128]{2,1,0:T(8,128)S(1)} collective-permute-done((f32[3,128,128]{2,1,0:T(8,128)S(1)}, f32[3,128,128]{2,1,0:T(8,128)S(1)}, u32[]{:S(2)}, u32[]{:S(2)}) %collective-permute-start.3) | collective-permute-done | bytes 196640 | tf_op jit(solution)/shard_map/ppermute | solution.py:153
  38.8 12.4 %collective-permute-start.4 = (f32[15,128,128]{2,1,0:T(8,128)S(1)}, f32[15,128,128]{2,1,0:T(8,128)S(1)}, u32[]{:S(2)}, u32[]{:S(2)}) collective-permute-start(f32[15,128,128]{2,1,0:T(8,128)S(1)} %broadcast_select_fusion.1), channel_id=1, source_target_pairs={{0,1},{1,0},{2,3},{3,2},{4,5},{5,4},{6,7},{7,6},{8,9},{9,8},{10,11... | collective-permute-start | bytes 2949128 | tf_op jit(solution)/shard_map/ppermute | solution.py:19
  52.0 1.2 %pad_maximum_fusion.refs_4_ = f32[21,128,128]{2,1,0:T(8,128)} fusion(f32[3,128,128]{2,1,0:T(8,128)S(1)} %collective-permute-done.3, f32[7,128,128]{2,1,0:T(8,128)S(1)} %collective-permute-done.2, f32[11,128,128]{2,1,0:T(8,128)S(1)} %collective-permute-done.1), kind=kLoop, calls=%fused_computation | loop fusion | flops 688128 | bytes 2752512 | tf_op jit(solution)/shard_map/concatenate | solution.py:154
  54.3 5.3 %shard_map.28 = (f32[7,128,128]{2,1,0:T(8,128)}, bf16[128,4992]{1,0:T(8,128)(2,1)}) custom-call(s32[1]{0:T(128)} %bitcast.refs_0_, f32[7]{0:T(128)} %convert_element_type.3.refs_1_, f32[7,128,128]{2,1,0:T(8,128)} %bitcast.7, f32[7,128,128]{2,1,0:T(8,128)} %copy-done, f32[21,128,128]{2,1,0:T(8,128)} %pad_maximum_fusion.refs_4_, f32[15,128,128]{2,1,0:T(8,128)} %copy-done.2), custom_call_target="tpu_custom_call" | custom-call | tf_op jit(solution)/shard_map/pallas_call | solution.py:132
  59.6 2.3 %collective-permute-start.5 = (f32[7,128,128]{2,1,0:T(8,128)}, f32[7,128,128]{2,1,0:T(8,128)S(1)}, u32[]{:S(2)}, u32[]{:S(2)}) collective-permute-start(f32[7,128,128]{2,1,0:T(8,128)} %get-tuple-element.8.refs_3_), channel_id=1, source_target_pairs={{0,1},{1,0},{2,3},{3,2},{4,5},{5,4},{6,7},{7,6},{8,9},{9,8},{10,11... | collective-permute-start | bytes 1376264 | tf_op jit(solution)/shard_map/ppermute | solution.py:19
  61.9 1.6 %collective-permute-done.5.refs_4_ = f32[7,128,128]{2,1,0:T(8,128)S(1)} collective-permute-done((f32[7,128,128]{2,1,0:T(8,128)}, f32[7,128,128]{2,1,0:T(8,128)S(1)}, u32[]{:S(2)}, u32[]{:S(2)}) %collective-permute-start.5) | collective-permute-done | bytes 458784 | tf_op jit(solution)/shard_map/ppermute | solution.py:19
  63.5 1.3 %broadcast_select_fusion.3 = (f32[7,128,128]{2,1,0:T(8,128)S(1)}, f32[7,128,128]{2,1,0:T(8,128)S(1)}) fusion(f32[7,128,128]{2,1,0:T(8,128)} %get-tuple-element.8.refs_3_, f32[7,128,128]{2,1,0:T(8,128)S(1)} %collective-permute-done.5.refs_4_, pred[]{:T(512)S(6)} %eq.27), kind=kLoop, calls=%fused_computation.17 | loop fusion | flops 229376 | bytes 1835009 | tf_op jit(solution)/shard_map/jit(_where)/select_n | solution.py:145
  65.0 1.9 %collective-permute-start.6 = (f32[11,128,128]{2,1,0:T(8,128)S(1)}, f32[11,128,128]{2,1,0:T(8,128)S(1)}, u32[]{:S(2)}, u32[]{:S(2)}) collective-permute-start(f32[11,128,128]{2,1,0:T(8,128)S(1)} %maximum_select_fusion.1), channel_id=1, source_target_pairs={{0,1023},{1,2},{2,1},{3,4},{4,3},{5,6},{6,5},{7,8},{8,7},{9,10},{1... | collective-permute-start | bytes 2162696 | tf_op jit(solution)/shard_map/ppermute | solution.py:153
  67.2 1.9 %collective-permute-start.7 = (f32[7,128,128]{2,1,0:T(8,128)S(1)}, f32[7,128,128]{2,1,0:T(8,128)S(1)}, u32[]{:S(2)}, u32[]{:S(2)}) collective-permute-start(f32[7,128,128]{2,1,0:T(8,128)S(1)} %maximum_select_fusion.3), channel_id=1, source_target_pairs={{0,1021},{1,4},{2,1023},{3,6},{4,1},{5,8},{6,3},{7,10},{8,5},{9,12... | collective-permute-start | bytes 1376264 | tf_op jit(solution)/shard_map/ppermute | solution.py:153
  69.1 1.9 %collective-permute-start.8 = (f32[3,128,128]{2,1,0:T(8,128)S(1)}, f32[3,128,128]{2,1,0:T(8,128)S(1)}, u32[]{:S(2)}, u32[]{:S(2)}) collective-permute-start(f32[3,128,128]{2,1,0:T(8,128)S(1)} %maximum_select_fusion.5), channel_id=1, source_target_pairs={{0,1019},{1,6},{2,1021},{3,8},{4,1023},{5,10},{6,1},{7,12},{8,3},{... | collective-permute-start | bytes 589832 | tf_op jit(solution)/shard_map/ppermute | solution.py:153
  71.1 16.0 %collective-permute-done.6 = f32[11,128,128]{2,1,0:T(8,128)S(1)} collective-permute-done((f32[11,128,128]{2,1,0:T(8,128)S(1)}, f32[11,128,128]{2,1,0:T(8,128)S(1)}, u32[]{:S(2)}, u32[]{:S(2)}) %collective-permute-start.6) | collective-permute-done | bytes 720928 | tf_op jit(solution)/shard_map/ppermute | solution.py:153
  87.4 20.4 %collective-permute-start.9 = (f32[15,128,128]{2,1,0:T(8,128)S(1)}, f32[15,128,128]{2,1,0:T(8,128)S(1)}, u32[]{:S(2)}, u32[]{:S(2)}) collective-permute-start(f32[15,128,128]{2,1,0:T(8,128)S(1)} %broadcast_select_fusion), channel_id=1, source_target_pairs={{0,1},{1,0},{2,3},{3,2},{4,5},{5,4},{6,7},{7,6},{8,9},{9,8},{10,11... | collective-permute-start | bytes 2949128 | tf_op jit(solution)/shard_map/ppermute | solution.py:19
  107.8 1.2 %pad_maximum_fusion.1.refs_5_ = f32[21,128,128]{2,1,0:T(8,128)} fusion(f32[3,128,128]{2,1,0:T(8,128)S(1)} %collective-permute-done.8, f32[7,128,128]{2,1,0:T(8,128)S(1)} %collective-permute-done.7, f32[11,128,128]{2,1,0:T(8,128)S(1)} %collective-permute-done.6), kind=kLoop, calls=%fused_computation.1 | loop fusion | flops 688128 | bytes 2752512 | tf_op jit(solution)/shard_map/concatenate | solution.py:154
  109.0 1.0 collective-permute-done.9.refs_6_
  110.0 1.0 copy-done.3
  110.9 5.2 %shard_map.29 = f32[7,128,128]{2,1,0:T(8,128)} custom-call(s32[1]{0:T(128)} %bitcast.refs_0_, f32[7]{0:T(128)} %convert_element_type.3.refs_1_, bf16[128,4992]{1,0:T(8,128)(2,1)} %get-tuple-element.7.refs_2_, f32[7,128,128]{2,1,0:T(8,128)} %get-tuple-element.8.refs_3_, f32[7,128,128]{2,1,0:T(8,128)} %copy-done.1, f32[21,128,128]{2,1,0:T(8,128)} %pad_maximum_fusion.1.refs_5_, ...), custom_call_target="tpu_custom_call" | custom-call | tf_op jit(solution)/shard_map/pallas_call | solution.py:132
  (57 shorter events, 3.2 us)
Async XLA Ops:
  0.0 4.2 %collective-permute-start = (f32[7,128,128]{2,1,0:T(8,128)}, f32[7,128,128]{2,1,0:T(8,128)S(1)}, u32[]{:S(2)}, u32[]{:S(2)}) collective-permute-start(f32[7,128,128]{2,1,0:T(8,128)} %bitcast.6), channel_id=1, source_target_pairs={{0,1},{1,0},{2,3},{3,2},{4,5},{5,4},{6,7},{7,6},{8,9},{9,8},{10,11... | collective-permute-start | bytes 1376264 | tf_op jit(solution)/shard_map/ppermute | solution.py:19
  4.2 1.3 %copy-start = (f32[7,128,128]{2,1,0:T(8,128)}, f32[7,128,128]{2,1,0:T(8,128)S(1)}, u32[]{:S(2)}) copy-start(f32[7,128,128]{2,1,0:T(8,128)S(1)} %collective-permute-done.refs_3_) | copy-start | bytes 1376260
  5.7 19.0 %collective-permute-start.1 = (f32[11,128,128]{2,1,0:T(8,128)S(1)}, f32[11,128,128]{2,1,0:T(8,128)S(1)}, u32[]{:S(2)}, u32[]{:S(2)}) collective-permute-start(f32[11,128,128]{2,1,0:T(8,128)S(1)} %maximum_select_fusion), channel_id=1, source_target_pairs={{0,1023},{1,2},{2,1},{3,4},{4,3},{5,6},{6,5},{7,8},{8,7},{9,10},{1... | collective-permute-start | bytes 2162696 | tf_op jit(solution)/shard_map/ppermute | solution.py:153
  9.8 21.6 %collective-permute-start.2 = (f32[7,128,128]{2,1,0:T(8,128)S(1)}, f32[7,128,128]{2,1,0:T(8,128)S(1)}, u32[]{:S(2)}, u32[]{:S(2)}) collective-permute-start(f32[7,128,128]{2,1,0:T(8,128)S(1)} %maximum_select_fusion.2), channel_id=1, source_target_pairs={{0,1021},{1,4},{2,1023},{3,6},{4,1},{5,8},{6,3},{7,10},{8,5},{9,12... | collective-permute-start | bytes 1376264 | tf_op jit(solution)/shard_map/ppermute | solution.py:153
  14.3 24.4 %collective-permute-start.3 = (f32[3,128,128]{2,1,0:T(8,128)S(1)}, f32[3,128,128]{2,1,0:T(8,128)S(1)}, u32[]{:S(2)}, u32[]{:S(2)}) collective-permute-start(f32[3,128,128]{2,1,0:T(8,128)S(1)} %maximum_select_fusion.4), channel_id=1, source_target_pairs={{0,1019},{1,6},{2,1021},{3,8},{4,1023},{5,10},{6,1},{7,12},{8,3},{... | collective-permute-start | bytes 589832 | tf_op jit(solution)/shard_map/ppermute | solution.py:153
  38.7 12.5 %copy-start.4 = (s32[1,12]{1,0:T(1,128)S(1)}, s32[1,12]{1,0:T(1,128)}, u32[]{:S(2)}) copy-start(s32[1,12]{1,0:T(1,128)} %param.3) | copy-start | bytes 148
  38.8 14.5 %collective-permute-start.4 = (f32[15,128,128]{2,1,0:T(8,128)S(1)}, f32[15,128,128]{2,1,0:T(8,128)S(1)}, u32[]{:S(2)}, u32[]{:S(2)}) collective-permute-start(f32[15,128,128]{2,1,0:T(8,128)S(1)} %broadcast_select_fusion.1), channel_id=1, source_target_pairs={{0,1},{1,0},{2,3},{3,2},{4,5},{5,4},{6,7},{7,6},{8,9},{9,8},{10,11... | collective-permute-start | bytes 2949128 | tf_op jit(solution)/shard_map/ppermute | solution.py:19
  53.4 1.0 copy-start.2
  59.6 3.9 %collective-permute-start.5 = (f32[7,128,128]{2,1,0:T(8,128)}, f32[7,128,128]{2,1,0:T(8,128)S(1)}, u32[]{:S(2)}, u32[]{:S(2)}) collective-permute-start(f32[7,128,128]{2,1,0:T(8,128)} %get-tuple-element.8.refs_3_), channel_id=1, source_target_pairs={{0,1},{1,0},{2,3},{3,2},{4,5},{5,4},{6,7},{7,6},{8,9},{9,8},{10,11... | collective-permute-start | bytes 1376264 | tf_op jit(solution)/shard_map/ppermute | solution.py:19
  63.5 1.3 %copy-start.1 = (f32[7,128,128]{2,1,0:T(8,128)}, f32[7,128,128]{2,1,0:T(8,128)S(1)}, u32[]{:S(2)}) copy-start(f32[7,128,128]{2,1,0:T(8,128)S(1)} %collective-permute-done.5.refs_4_) | copy-start | bytes 1376260
  65.0 22.0 %collective-permute-start.6 = (f32[11,128,128]{2,1,0:T(8,128)S(1)}, f32[11,128,128]{2,1,0:T(8,128)S(1)}, u32[]{:S(2)}, u32[]{:S(2)}) collective-permute-start(f32[11,128,128]{2,1,0:T(8,128)S(1)} %maximum_select_fusion.1), channel_id=1, source_target_pairs={{0,1023},{1,2},{2,1},{3,4},{4,3},{5,6},{6,5},{7,8},{8,7},{9,10},{1... | collective-permute-start | bytes 2162696 | tf_op jit(solution)/shard_map/ppermute | solution.py:153
  67.2 20.0 %collective-permute-start.7 = (f32[7,128,128]{2,1,0:T(8,128)S(1)}, f32[7,128,128]{2,1,0:T(8,128)S(1)}, u32[]{:S(2)}, u32[]{:S(2)}) collective-permute-start(f32[7,128,128]{2,1,0:T(8,128)S(1)} %maximum_select_fusion.3), channel_id=1, source_target_pairs={{0,1021},{1,4},{2,1023},{3,6},{4,1},{5,8},{6,3},{7,10},{8,5},{9,12... | collective-permute-start | bytes 1376264 | tf_op jit(solution)/shard_map/ppermute | solution.py:153
  69.1 18.1 %collective-permute-start.8 = (f32[3,128,128]{2,1,0:T(8,128)S(1)}, f32[3,128,128]{2,1,0:T(8,128)S(1)}, u32[]{:S(2)}, u32[]{:S(2)}) collective-permute-start(f32[3,128,128]{2,1,0:T(8,128)S(1)} %maximum_select_fusion.5), channel_id=1, source_target_pairs={{0,1019},{1,6},{2,1021},{3,8},{4,1023},{5,10},{6,1},{7,12},{8,3},{... | collective-permute-start | bytes 589832 | tf_op jit(solution)/shard_map/ppermute | solution.py:153
  87.4 22.6 %collective-permute-start.9 = (f32[15,128,128]{2,1,0:T(8,128)S(1)}, f32[15,128,128]{2,1,0:T(8,128)S(1)}, u32[]{:S(2)}, u32[]{:S(2)}) collective-permute-start(f32[15,128,128]{2,1,0:T(8,128)S(1)} %broadcast_select_fusion), channel_id=1, source_target_pairs={{0,1},{1,0},{2,3},{3,2},{4,5},{5,4},{6,7},{7,6},{8,9},{9,8},{10,11... | collective-permute-start | bytes 2949128 | tf_op jit(solution)/shard_map/ppermute | solution.py:19
  110.0 1.0 copy-start.3

commit v12 on v11

--- a/solution.py
+++ b/solution.py
@@ -57,8 +57,18 @@
         return self.ref[self.where[full]]
 
 
+class Shifted:
+    def __init__(self, ref, first):
+        self.ref, self.first = ref, first
+
+    def __getitem__(self, w):
+        assert self.first <= w < self.first + WIDTH - 1
+        return self.ref[w - self.first]
+
+
 def chip_refs(k, own, partner, got, other):
     other = Trimmed(other, 1 - k)
+    partner = Shifted(partner, k)
     if k == 0:
         return own, partner, got, other
     return partner, own, other, got
@@ -140,13 +150,11 @@
 
 
 def exchange_rows(x, is_odd, n):
-    partner = swap_in_chip(x, n)
-    r0 = jnp.where(is_odd, partner, x)
-    r1 = jnp.where(is_odd, x, partner)
+    partner = swap_in_chip(jnp.where(is_odd, x[: WIDTH - 1], x[1:]), n)
     received = []
     for d in range(1, CHIPS_OUT + 1):
-        up = jnp.concatenate([r1[2 * d - 1:], r0[2 * d:]], axis=0)
-        down = jnp.concatenate([r0[: 8 - 2 * d], r1[: 7 - 2 * d]], axis=0)
+        up = jnp.concatenate([x[2 * d - 1:], partner[2 * d - 1:]], axis=0)
+        down = jnp.concatenate([x[: 8 - 2 * d], partner[: 7 - 2 * d]], axis=0)
         buf = jnp.where(is_odd, up, down)
         step = 2 * d - 1
         route = [(i, (i + step) % n) if i % 2 else (i, (i - step) % n) for i in range(n)]

time: 117 us -> 116 us (level)
    slice x0 -> x1, other arithmetic: none -> 1.31 us  [exchange_rows(): partner = swap_in_chip(jnp.where(is_odd, x[:WIDTH - 1], x[1:]), n)]
    select_n x2 -> x1, other arithmetic: 2.52 us -> 1.23 us  [exchange_rows(): partner = swap_in_chip(jnp.where(is_odd, x[:WIDTH - 1], x[1:]), n)]
where the time goes in v12:
time: 116 us; the launch traced here: 115 us
  starting transfers between devices  57.4 us (49%)
  waiting for transfers between devices  38.2 us (33%)
  Pallas kernels  10.5 us (9%)
  other arithmetic  6.25 us (5%)
  local copies, waits for them, and re-layouts  2.59 us (2%)
    ppermute x4, starting transfers between devices, swap_in_chip(): return lax.ppermute(x, AXES, [(i, i ^ 1) for i in range(n)])  37.6 us
    ppermute x6, waiting for transfers between devices, exchange_rows(): received.append(lax.ppermute(buf, AXES, route))  34.6 us
    ppermute x6, starting transfers between devices, exchange_rows(): received.append(lax.ppermute(buf, AXES, route))  19.8 us
    pallas_call x2, Pallas kernels, band_call(): pl.pallas_call(functools.partial(band_kernel, final=final), out_shape=squ...  10.5 us
    ppermute x4, waiting for transfers between devices, swap_in_chip(): return lax.ppermute(x, AXES, [(i, i ^ 1) for i in range(n)])  3.61 us
    concatenate x2, other arithmetic, exchange_rows(): got = jnp.concatenate(received, axis=0)  2.41 us
  transfers between devices with their start and end apart: 10, of which 8 were waited for; matrix products, arithmetic and copies ran while one was open for 3% of the time, Pallas kernels for 0%

profile of v12, /device:TPU:65, one launch (start us, length us, event | category | flops | bytes accessed | tf_op | source)
XLA Modules:
  0.0 115.4 jit_solution(4455922302729269448)
XLA Ops:
  0.0 1.2 %broadcast_select_fusion.3 = f32[6,128,128]{2,1,0:T(8,128)S(1)} fusion(pred[]{:T(512)S(6)} %eq.27, f32[1,7,128,128]{3,2,1,0:T(8,128)} %param.2), kind=kLoop, calls=%fused_computation.27 | loop fusion | flops 98304 | bytes 1179649 | tf_op jit(solution)/shard_map/jit(_where)/select_n | solution.py:153
  1.2 2.6 %collective-permute-start = (f32[6,128,128]{2,1,0:T(8,128)S(1)}, f32[6,128,128]{2,1,0:T(8,128)S(1)}, u32[]{:S(2)}, u32[]{:S(2)}) collective-permute-start(f32[6,128,128]{2,1,0:T(8,128)S(1)} %broadcast_select_fusion.3), channel_id=1, source_target_pairs={{0,1},{1,0},{2,3},{3,2},{4,5},{5,4},{6,7},{7,6},{8,9},{9,8},{10,11... | collective-permute-start | bytes 1179656 | tf_op jit(solution)/shard_map/ppermute | solution.py:19
  4.0 1.2 %collective-permute-done.refs_3_ = f32[6,128,128]{2,1,0:T(8,128)S(1)} collective-permute-done((f32[6,128,128]{2,1,0:T(8,128)S(1)}, f32[6,128,128]{2,1,0:T(8,128)S(1)}, u32[]{:S(2)}, u32[]{:S(2)}) %collective-permute-start) | collective-permute-done | bytes 393248 | tf_op jit(solution)/shard_map/ppermute | solution.py:19
  5.3 3.8 %collective-permute-start.1 = (f32[11,128,128]{2,1,0:T(8,128)S(1)}, f32[11,128,128]{2,1,0:T(8,128)S(1)}, u32[]{:S(2)}, u32[]{:S(2)}) collective-permute-start(f32[11,128,128]{2,1,0:T(8,128)S(1)} %maximum_select_fusion), channel_id=1, source_target_pairs={{0,1023},{1,2},{2,1},{3,4},{4,3},{5,6},{6,5},{7,8},{8,7},{9,10},{1... | collective-permute-start | bytes 2162696 | tf_op jit(solution)/shard_map/ppermute | solution.py:161
  9.2 4.5 %collective-permute-start.2 = (f32[7,128,128]{2,1,0:T(8,128)S(1)}, f32[7,128,128]{2,1,0:T(8,128)S(1)}, u32[]{:S(2)}, u32[]{:S(2)}) collective-permute-start(f32[7,128,128]{2,1,0:T(8,128)S(1)} %maximum_select_fusion.2), channel_id=1, source_target_pairs={{0,1021},{1,4},{2,1023},{3,6},{4,1},{5,8},{6,3},{7,10},{8,5},{9,12... | collective-permute-start | bytes 1376264 | tf_op jit(solution)/shard_map/ppermute | solution.py:161
  13.8 5.8 %collective-permute-start.3 = (f32[3,128,128]{2,1,0:T(8,128)S(1)}, f32[3,128,128]{2,1,0:T(8,128)S(1)}, u32[]{:S(2)}, u32[]{:S(2)}) collective-permute-start(f32[3,128,128]{2,1,0:T(8,128)S(1)} %maximum_select_fusion.4), channel_id=1, source_target_pairs={{0,1019},{1,6},{2,1021},{3,8},{4,1023},{5,10},{6,1},{7,12},{8,3},{... | collective-permute-start | bytes 589832 | tf_op jit(solution)/shard_map/ppermute | solution.py:161
  19.5 4.8 %collective-permute-done.1 = f32[11,128,128]{2,1,0:T(8,128)S(1)} collective-permute-done((f32[11,128,128]{2,1,0:T(8,128)S(1)}, f32[11,128,128]{2,1,0:T(8,128)S(1)}, u32[]{:S(2)}, u32[]{:S(2)}) %collective-permute-start.1) | collective-permute-done | bytes 720928 | tf_op jit(solution)/shard_map/ppermute | solution.py:161
  24.4 6.5 %collective-permute-done.2 = f32[7,128,128]{2,1,0:T(8,128)S(1)} collective-permute-done((f32[7,128,128]{2,1,0:T(8,128)S(1)}, f32[7,128,128]{2,1,0:T(8,128)S(1)}, u32[]{:S(2)}, u32[]{:S(2)}) %collective-permute-start.2) | collective-permute-done | bytes 458784 | tf_op jit(solution)/shard_map/ppermute | solution.py:161
  31.0 7.3 %collective-permute-done.3 = f32[3,128,128]{2,1,0:T(8,128)S(1)} collective-permute-done((f32[3,128,128]{2,1,0:T(8,128)S(1)}, f32[3,128,128]{2,1,0:T(8,128)S(1)}, u32[]{:S(2)}, u32[]{:S(2)}) %collective-permute-start.3) | collective-permute-done | bytes 196640 | tf_op jit(solution)/shard_map/ppermute | solution.py:161
  38.4 12.4 %collective-permute-start.4 = (f32[15,128,128]{2,1,0:T(8,128)S(1)}, f32[15,128,128]{2,1,0:T(8,128)S(1)}, u32[]{:S(2)}, u32[]{:S(2)}) collective-permute-start(f32[15,128,128]{2,1,0:T(8,128)S(1)} %broadcast_select_fusion.1), channel_id=1, source_target_pairs={{0,1},{1,0},{2,3},{3,2},{4,5},{5,4},{6,7},{7,6},{8,9},{9,8},{10,11... | collective-permute-start | bytes 2949128 | tf_op jit(solution)/shard_map/ppermute | solution.py:19
  51.6 1.2 %pad_maximum_fusion.refs_4_ = f32[21,128,128]{2,1,0:T(8,128)} fusion(f32[3,128,128]{2,1,0:T(8,128)S(1)} %collective-permute-done.3, f32[7,128,128]{2,1,0:T(8,128)S(1)} %collective-permute-done.2, f32[11,128,128]{2,1,0:T(8,128)S(1)} %collective-permute-done.1), kind=kLoop, calls=%fused_computation | loop fusion | flops 688128 | bytes 2752512 | tf_op jit(solution)/shard_map/concatenate | solution.py:162
  53.0 1.0 copy-done.4
  54.0 5.3 %shard_map.28 = (f32[7,128,128]{2,1,0:T(8,128)}, bf16[128,4992]{1,0:T(8,128)(2,1)}) custom-call(s32[1]{0:T(128)} %bitcast.refs_0_, f32[7]{0:T(128)} %convert_element_type.3.refs_1_, f32[7,128,128]{2,1,0:T(8,128)} %bitcast.20, f32[6,128,128]{2,1,0:T(8,128)} %copy-done.2, f32[21,128,128]{2,1,0:T(8,128)} %pad_maximum_fusion.refs_4_, f32[15,128,128]{2,1,0:T(8,128)} %copy-done.4), custom_call_target="tpu_custom_call" | custom-call | tf_op jit(solution)/shard_map/pallas_call | solution.py:142
  59.3 1.3 %fusion.1 = (f32[6,128,128]{2,1,0:T(8,128)S(1)}, f32[6,128,128]{2,1,0:T(8,128)S(1)}, f32[6,128,128]{2,1,0:T(8,128)S(1)}) fusion(f32[7,128,128]{2,1,0:T(8,128)} %get-tuple-element.8.refs_3_, pred[]{:T(512)S(6)} %eq.27), kind=kLoop, calls=%fused_computation.43 | loop fusion | flops 98304 | bytes 1966081 | tf_op jit(solution)/shard_map/slice | solution.py:153
  60.6 2.3 %collective-permute-start.5 = (f32[6,128,128]{2,1,0:T(8,128)S(1)}, f32[6,128,128]{2,1,0:T(8,128)S(1)}, u32[]{:S(2)}, u32[]{:S(2)}) collective-permute-start(f32[6,128,128]{2,1,0:T(8,128)S(1)} %get-tuple-element.22), channel_id=1, source_target_pairs={{0,1},{1,0},{2,3},{3,2},{4,5},{5,4},{6,7},{7,6},{8,9},{9,8},{10,11... | collective-permute-start | bytes 1179656 | tf_op jit(solution)/shard_map/ppermute | solution.py:19
  62.9 1.3 %collective-permute-done.5.refs_4_ = f32[6,128,128]{2,1,0:T(8,128)S(1)} collective-permute-done((f32[6,128,128]{2,1,0:T(8,128)S(1)}, f32[6,128,128]{2,1,0:T(8,128)S(1)}, u32[]{:S(2)}, u32[]{:S(2)}) %collective-permute-start.5) | collective-permute-done | bytes 393248 | tf_op jit(solution)/shard_map/ppermute | solution.py:19
  64.3 1.9 %collective-permute-start.6 = (f32[11,128,128]{2,1,0:T(8,128)S(1)}, f32[11,128,128]{2,1,0:T(8,128)S(1)}, u32[]{:S(2)}, u32[]{:S(2)}) collective-permute-start(f32[11,128,128]{2,1,0:T(8,128)S(1)} %maximum_select_fusion.1), channel_id=1, source_target_pairs={{0,1023},{1,2},{2,1},{3,4},{4,3},{5,6},{6,5},{7,8},{8,7},{9,10},{1... | collective-permute-start | bytes 2162696 | tf_op jit(solution)/shard_map/ppermute | solution.py:161
  66.4 1.9 %collective-permute-start.7 = (f32[7,128,128]{2,1,0:T(8,128)S(1)}, f32[7,128,128]{2,1,0:T(8,128)S(1)}, u32[]{:S(2)}, u32[]{:S(2)}) collective-permute-start(f32[7,128,128]{2,1,0:T(8,128)S(1)} %maximum_select_fusion.3), channel_id=1, source_target_pairs={{0,1021},{1,4},{2,1023},{3,6},{4,1},{5,8},{6,3},{7,10},{8,5},{9,12... | collective-permute-start | bytes 1376264 | tf_op jit(solution)/shard_map/ppermute | solution.py:161
  68.4 1.9 %collective-permute-start.8 = (f32[3,128,128]{2,1,0:T(8,128)S(1)}, f32[3,128,128]{2,1,0:T(8,128)S(1)}, u32[]{:S(2)}, u32[]{:S(2)}) collective-permute-start(f32[3,128,128]{2,1,0:T(8,128)S(1)} %maximum_select_fusion.5), channel_id=1, source_target_pairs={{0,1019},{1,6},{2,1021},{3,8},{4,1023},{5,10},{6,1},{7,12},{8,3},{... | collective-permute-start | bytes 589832 | tf_op jit(solution)/shard_map/ppermute | solution.py:161
  70.3 16.1 %collective-permute-done.6 = f32[11,128,128]{2,1,0:T(8,128)S(1)} collective-permute-done((f32[11,128,128]{2,1,0:T(8,128)S(1)}, f32[11,128,128]{2,1,0:T(8,128)S(1)}, u32[]{:S(2)}, u32[]{:S(2)}) %collective-permute-start.6) | collective-permute-done | bytes 720928 | tf_op jit(solution)/shard_map/ppermute | solution.py:161
  86.7 20.3 %collective-permute-start.9 = (f32[15,128,128]{2,1,0:T(8,128)S(1)}, f32[15,128,128]{2,1,0:T(8,128)S(1)}, u32[]{:S(2)}, u32[]{:S(2)}) collective-permute-start(f32[15,128,128]{2,1,0:T(8,128)S(1)} %broadcast_select_fusion), channel_id=1, source_target_pairs={{0,1},{1,0},{2,3},{3,2},{4,5},{5,4},{6,7},{7,6},{8,9},{9,8},{10,11... | collective-permute-start | bytes 2949128 | tf_op jit(solution)/shard_map/ppermute | solution.py:19
  107.0 1.2 %pad_maximum_fusion.1.refs_5_ = f32[21,128,128]{2,1,0:T(8,128)} fusion(f32[3,128,128]{2,1,0:T(8,128)S(1)} %collective-permute-done.8, f32[7,128,128]{2,1,0:T(8,128)S(1)} %collective-permute-done.7, f32[11,128,128]{2,1,0:T(8,128)S(1)} %collective-permute-done.6), kind=kLoop, calls=%fused_computation.1 | loop fusion | flops 688128 | bytes 2752512 | tf_op jit(solution)/shard_map/concatenate | solution.py:162
  108.2 1.0 collective-permute-done.9.refs_6_
  110.2 5.2 %shard_map.29 = f32[7,128,128]{2,1,0:T(8,128)} custom-call(s32[1]{0:T(128)} %bitcast.refs_0_, f32[7]{0:T(128)} %convert_element_type.3.refs_1_, bf16[128,4992]{1,0:T(8,128)(2,1)} %get-tuple-element.7.refs_2_, f32[7,128,128]{2,1,0:T(8,128)} %get-tuple-element.8.refs_3_, f32[6,128,128]{2,1,0:T(8,128)} %copy-done.3, f32[21,128,128]{2,1,0:T(8,128)} %pad_maximum_fusion.1.refs_5_, ...), custom_call_target="tpu_custom_call" | custom-call | tf_op jit(solution)/shard_map/pallas_call | solution.py:142
  (48 shorter events, 3.1 us)
Async XLA Ops:
  0.0 3.8 %copy-start = (f32[1,7,128,128]{3,2,1,0:T(8,128)S(1)}, f32[1,7,128,128]{3,2,1,0:T(8,128)}, u32[]{:S(2)}) copy-start(f32[1,7,128,128]{3,2,1,0:T(8,128)} %param.2) | copy-start | bytes 1376260
  1.2 3.9 %collective-permute-start = (f32[6,128,128]{2,1,0:T(8,128)S(1)}, f32[6,128,128]{2,1,0:T(8,128)S(1)}, u32[]{:S(2)}, u32[]{:S(2)}) collective-permute-start(f32[6,128,128]{2,1,0:T(8,128)S(1)} %broadcast_select_fusion.3), channel_id=1, source_target_pairs={{0,1},{1,0},{2,3},{3,2},{4,5},{5,4},{6,7},{7,6},{8,9},{9,8},{10,11... | collective-permute-start | bytes 1179656 | tf_op jit(solution)/shard_map/ppermute | solution.py:19
  5.2 8.6 %copy-start.2 = (f32[6,128,128]{2,1,0:T(8,128)}, f32[6,128,128]{2,1,0:T(8,128)S(1)}, u32[]{:S(2)}) copy-start(f32[6,128,128]{2,1,0:T(8,128)S(1)} %collective-permute-done.refs_3_) | copy-start | bytes 1179652
  5.3 19.0 %collective-permute-start.1 = (f32[11,128,128]{2,1,0:T(8,128)S(1)}, f32[11,128,128]{2,1,0:T(8,128)S(1)}, u32[]{:S(2)}, u32[]{:S(2)}) collective-permute-start(f32[11,128,128]{2,1,0:T(8,128)S(1)} %maximum_select_fusion), channel_id=1, source_target_pairs={{0,1023},{1,2},{2,1},{3,4},{4,3},{5,6},{6,5},{7,8},{8,7},{9,10},{1... | collective-permute-start | bytes 2162696 | tf_op jit(solution)/shard_map/ppermute | solution.py:161
  9.2 21.7 %collective-permute-start.2 = (f32[7,128,128]{2,1,0:T(8,128)S(1)}, f32[7,128,128]{2,1,0:T(8,128)S(1)}, u32[]{:S(2)}, u32[]{:S(2)}) collective-permute-start(f32[7,128,128]{2,1,0:T(8,128)S(1)} %maximum_select_fusion.2), channel_id=1, source_target_pairs={{0,1021},{1,4},{2,1023},{3,6},{4,1},{5,8},{6,3},{7,10},{8,5},{9,12... | collective-permute-start | bytes 1376264 | tf_op jit(solution)/shard_map/ppermute | solution.py:161
  13.8 24.5 %collective-permute-start.3 = (f32[3,128,128]{2,1,0:T(8,128)S(1)}, f32[3,128,128]{2,1,0:T(8,128)S(1)}, u32[]{:S(2)}, u32[]{:S(2)}) collective-permute-start(f32[3,128,128]{2,1,0:T(8,128)S(1)} %maximum_select_fusion.4), channel_id=1, source_target_pairs={{0,1019},{1,6},{2,1021},{3,8},{4,1023},{5,10},{6,1},{7,12},{8,3},{... | collective-permute-start | bytes 589832 | tf_op jit(solution)/shard_map/ppermute | solution.py:161
  38.3 12.6 %copy-start.6 = (s32[1,12]{1,0:T(1,128)S(1)}, s32[1,12]{1,0:T(1,128)}, u32[]{:S(2)}) copy-start(s32[1,12]{1,0:T(1,128)} %param.3) | copy-start | bytes 148
  38.4 14.6 %collective-permute-start.4 = (f32[15,128,128]{2,1,0:T(8,128)S(1)}, f32[15,128,128]{2,1,0:T(8,128)S(1)}, u32[]{:S(2)}, u32[]{:S(2)}) collective-permute-start(f32[15,128,128]{2,1,0:T(8,128)S(1)} %broadcast_select_fusion.1), channel_id=1, source_target_pairs={{0,1},{1,0},{2,3},{3,2},{4,5},{5,4},{6,7},{7,6},{8,9},{9,8},{10,11... | collective-permute-start | bytes 2949128 | tf_op jit(solution)/shard_map/ppermute | solution.py:19
  53.0 1.0 copy-start.4
  59.3 3.6 %copy-start.1 = (f32[7,128,128]{2,1,0:T(8,128)S(1)}, f32[7,128,128]{2,1,0:T(8,128)}, u32[]{:S(2)}) copy-start(f32[7,128,128]{2,1,0:T(8,128)} %get-tuple-element.8.refs_3_) | copy-start | bytes 1376260
  60.6 3.6 %collective-permute-start.5 = (f32[6,128,128]{2,1,0:T(8,128)S(1)}, f32[6,128,128]{2,1,0:T(8,128)S(1)}, u32[]{:S(2)}, u32[]{:S(2)}) collective-permute-start(f32[6,128,128]{2,1,0:T(8,128)S(1)} %get-tuple-element.22), channel_id=1, source_target_pairs={{0,1},{1,0},{2,3},{3,2},{4,5},{5,4},{6,7},{7,6},{8,9},{9,8},{10,11... | collective-permute-start | bytes 1179656 | tf_op jit(solution)/shard_map/ppermute | solution.py:19
  64.2 4.1 %copy-start.3 = (f32[6,128,128]{2,1,0:T(8,128)}, f32[6,128,128]{2,1,0:T(8,128)S(1)}, u32[]{:S(2)}) copy-start(f32[6,128,128]{2,1,0:T(8,128)S(1)} %collective-permute-done.5.refs_4_) | copy-start | bytes 1179652
  64.3 22.0 %collective-permute-start.6 = (f32[11,128,128]{2,1,0:T(8,128)S(1)}, f32[11,128,128]{2,1,0:T(8,128)S(1)}, u32[]{:S(2)}, u32[]{:S(2)}) collective-permute-start(f32[11,128,128]{2,1,0:T(8,128)S(1)} %maximum_select_fusion.1), channel_id=1, source_target_pairs={{0,1023},{1,2},{2,1},{3,4},{4,3},{5,6},{6,5},{7,8},{8,7},{9,10},{1... | collective-permute-start | bytes 2162696 | tf_op jit(solution)/shard_map/ppermute | solution.py:161
  66.4 20.1 %collective-permute-start.7 = (f32[7,128,128]{2,1,0:T(8,128)S(1)}, f32[7,128,128]{2,1,0:T(8,128)S(1)}, u32[]{:S(2)}, u32[]{:S(2)}) collective-permute-start(f32[7,128,128]{2,1,0:T(8,128)S(1)} %maximum_select_fusion.3), channel_id=1, source_target_pairs={{0,1021},{1,4},{2,1023},{3,6},{4,1},{5,8},{6,3},{7,10},{8,5},{9,12... | collective-permute-start | bytes 1376264 | tf_op jit(solution)/shard_map/ppermute | solution.py:161
  68.4 18.2 %collective-permute-start.8 = (f32[3,128,128]{2,1,0:T(8,128)S(1)}, f32[3,128,128]{2,1,0:T(8,128)S(1)}, u32[]{:S(2)}, u32[]{:S(2)}) collective-permute-start(f32[3,128,128]{2,1,0:T(8,128)S(1)} %maximum_select_fusion.5), channel_id=1, source_target_pairs={{0,1019},{1,6},{2,1021},{3,8},{4,1023},{5,10},{6,1},{7,12},{8,3},{... | collective-permute-start | bytes 589832 | tf_op jit(solution)/shard_map/ppermute | solution.py:161
  86.7 22.5 %collective-permute-start.9 = (f32[15,128,128]{2,1,0:T(8,128)S(1)}, f32[15,128,128]{2,1,0:T(8,128)S(1)}, u32[]{:S(2)}, u32[]{:S(2)}) collective-permute-start(f32[15,128,128]{2,1,0:T(8,128)S(1)} %broadcast_select_fusion), channel_id=1, source_target_pairs={{0,1},{1,0},{2,3},{3,2},{4,5},{5,4},{6,7},{7,6},{8,9},{9,8},{10,11... | collective-permute-start | bytes 2949128 | tf_op jit(solution)/shard_map/ppermute | solution.py:19
  109.2 1.0 copy-start.5
